TPU v7x, 256 devices: a whole 4x4x8 slice. The times are simulated.
256 devices in a mesh: dp: 32 (over y, z), fsdp: 8 (over x, core).
Axes of the slice: x: 4, y: 4, z: 8, core: 2. Of those that a mesh axis runs over, the one named last changes fastest.
Arguments:
- prefill_tokens: bfloat16 [16384, 2048], P('dp'), may hold values from -3 to 3
- decode_tokens: bfloat16 [128, 2048], P('dp'), may hold values from -3 to 3
- query_weight: bfloat16 [2048, 2048], P('dp', 'fsdp'), may hold values from -0.125 to 0.125
- key_weight: bfloat16 [2048, 2048], P('dp', 'fsdp'), may hold values from -0.125 to 0.125
- value_weight: bfloat16 [2048, 2048], P('dp', 'fsdp'), may hold values from -0.125 to 0.125
- out_weight: bfloat16 [2048, 2048], P('fsdp', 'dp'), may hold values from -0.125 to 0.125
- prior_keys: bfloat16 [32, 2048, 2048], P('dp', None, 'fsdp'), may hold values from -480 to 480
- prior_values: bfloat16 [32, 2048, 2048], P('dp', None, 'fsdp'), may hold values from -6 to 6
- prior_length: int32 [32], P('dp'), may hold values from 0 to 2048, as said below
- pool_keys: bfloat16 [1536, 128, 2048], P('dp', None, 'fsdp'), may hold values from -480 to 480
- pool_values: bfloat16 [1536, 128, 2048], P('dp', None, 'fsdp'), may hold values from -6 to 6
- page_slots: int32 [1536], replicated, may hold values from 0 to 1535, each once
- page_counts: int32 [128], replicated, may hold values from 1 to 128, 1536 in all
- last_fill: int32 [128], replicated, may hold values from 1 to 128
- decode_request: int32 [128], replicated, may hold values from 0 to 127, each once
Outputs:
- mixed_prefill: bfloat16 [16384, 2048], P('dp', 'fsdp')
- mixed_decode: bfloat16 [128, 2048], P('dp', 'fsdp')
Inputs may be any that keep to these rules, and one draw needn't show every extreme that they name: `prior_length`: one prefill request's prior fills all 2048 slots. Request r owns the logical pages first_page[r] to first_page[r] + page_counts[r] - 1; the counts sum to 1536, and some request has exactly 128 pages. A permutation: pool slot page_slots[k] holds logical page k. `decode_request`: A permutation of the decode requests.
All inputs are finite; a program needn't handle non-finite values.
Results may differ from a plain program's by a relative error of at most 0.015.
The roundings to bfloat16 on the way count: a program that leaves them out, or rounds other values in their place, can miss the bound.
Values may be sent and summed in bfloat16 or wider, within the bound.
No kernel may reach another device: no remote copies, remote signals or barrier semaphores. Data moves between devices by JAX's collectives and lax.ppermute only.
A program may use at most 128 MiB of HBM per device.

v0:
```python
import jax
import jax.numpy as jnp
from jax import lax
from jax.sharding import PartitionSpec as P

HEAD = 128
PAGE = 128


EPSILON = 1e-05
ROPE_BASE = 10000.0
NEG_FILL = -1e30


def merged(value, axis, join):
    pieces = jax.tree.map(lambda part: lax.all_gather(part, axis), value)
    head = jax.tree.map(lambda part: part[0], pieces)
    tail = jax.tree.map(lambda part: part[1:], pieces)
    total, _ = lax.scan(lambda total, share: (join(total, share), None), head, tail)
    return total


def layer_norm(rows_in):
    widened = rows_in.astype(jnp.float32)
    average = jnp.mean(widened, axis=-1, keepdims=True)
    centred = widened - average
    variance = jnp.mean(centred * centred, axis=-1, keepdims=True)
    return (centred * lax.rsqrt(variance + EPSILON)).astype(jnp.bfloat16)


def rotary(vectors, positions, head_size):
    row_count = vectors.shape[0]
    split_heads = vectors.reshape(row_count, -1, head_size)
    halfway = head_size // 2
    exponent = jnp.arange(halfway, dtype=jnp.float32) * (2.0 / head_size)
    frequency = jnp.power(jnp.float32(ROPE_BASE), -exponent)
    angles = positions.astype(jnp.float32)[:, None] * frequency[None, :]
    cosine = jnp.cos(angles)[:, None, :]
    sine_part = jnp.sin(angles)[:, None, :]
    leading = split_heads[..., :halfway]
    trailing = split_heads[..., halfway:]
    turned = jnp.concatenate(
        [leading * cosine - trailing * sine_part, trailing * cosine + leading * sine_part], axis=-1
    )
    return turned.reshape(row_count, -1)


def rescale(vectors, factor, head_size):
    shaped = vectors.reshape(vectors.shape[0], factor.shape[1], head_size)
    return (shaped * factor[:, :, None]).reshape(vectors.shape)


def combine_pair(earlier, later):
    early_top, early_total, early_mix = earlier
    late_top, late_total, late_mix = later
    joined_top = jnp.maximum(early_top, late_top)
    early_factor = jnp.exp(early_top - joined_top)
    late_factor = jnp.exp(late_top - joined_top)
    joined_total = early_total * early_factor + late_total * late_factor
    joined_mix = rescale(early_mix, early_factor, HEAD) + rescale(late_mix, late_factor, HEAD)
    return (joined_top, joined_total, joined_mix)


def per_device(
    prefill_tokens,
    decode_tokens,
    query_weight,
    key_weight,
    value_weight,
    out_weight,
    prior_keys,
    prior_values,
    prior_length,
    pool_keys,
    pool_values,
    page_slots,
    page_counts,
    last_fill,
    decode_request,
):
    group_rows = prefill_tokens.shape[0]
    decode_rows = decode_tokens.shape[0]
    local_width = query_weight.shape[1]
    head_count = local_width // HEAD
    score_scale = HEAD ** (-0.5)
    data_index = lax.axis_index("dp")
    model_index = lax.axis_index("fsdp")
    tokens = jnp.concatenate([prefill_tokens, decode_tokens], axis=0)
    normed = layer_norm(tokens)
    portions = (
        lax.all_gather(query_weight, "dp", axis=0, tiled=True),
        lax.all_gather(key_weight, "dp", axis=0, tiled=True),
        lax.all_gather(value_weight, "dp", axis=0, tiled=True),
    )
    raw_queries, raw_keys, raw_values = tuple(
        (jnp.dot(normed, portion, preferred_element_type=jnp.float32) for portion in portions)
    )
    cache_length = (page_counts - 1) * PAGE + last_fill
    first_page = jnp.cumsum(page_counts) - page_counts
    request_count = decode_request.shape[0]
    slot_numbers = jnp.arange(request_count, dtype=jnp.int32)
    slot_of_request = jnp.zeros((request_count,), jnp.int32).at[decode_request].set(slot_numbers)
    my_slots = data_index * decode_rows + jnp.arange(decode_rows, dtype=jnp.int32)
    my_requests = jnp.take(decode_request, my_slots)
    positions = jnp.concatenate(
        [
            prior_length[0] + jnp.arange(group_rows, dtype=jnp.int32),
            jnp.take(cache_length, my_requests),
        ]
    )
    queries = rotary(raw_queries, positions, HEAD).astype(jnp.bfloat16)
    keys_new = rotary(raw_keys, positions, HEAD).astype(jnp.bfloat16)
    values_new = raw_values.astype(jnp.bfloat16)
    prior_slots = prior_keys.shape[1]
    group_queries = queries[:group_rows].reshape(group_rows, head_count, HEAD)
    group_keys = keys_new[:group_rows].reshape(group_rows, head_count, HEAD)
    group_values = values_new[:group_rows].reshape(group_rows, head_count, HEAD)
    stored_keys = prior_keys[0].reshape(prior_slots, head_count, HEAD)
    stored_values = prior_values[0].reshape(prior_slots, head_count, HEAD)
    prior_scores = (
        jnp.einsum("qhd,khd->hqk", group_queries, stored_keys, preferred_element_type=jnp.float32)
        * score_scale
    )
    prior_live = jnp.arange(prior_slots, dtype=jnp.int32) < prior_length[0]
    prior_scores = jnp.where(prior_live[None, None, :], prior_scores, NEG_FILL)
    group_scores = (
        jnp.einsum("qhd,khd->hqk", group_queries, group_keys, preferred_element_type=jnp.float32)
        * score_scale
    )
    causal = jnp.arange(group_rows)[None, :] <= jnp.arange(group_rows)[:, None]
    group_scores = jnp.where(causal[None], group_scores, NEG_FILL)
    row_top = jnp.maximum(
        jnp.max(prior_scores, axis=2, keepdims=True), jnp.max(group_scores, axis=2, keepdims=True)
    )
    prior_weights = jnp.exp(prior_scores - row_top)
    group_weights = jnp.exp(group_scores - row_top)
    weight_total = jnp.sum(prior_weights, axis=2) + jnp.sum(group_weights, axis=2)
    combined = jnp.einsum(
        "hqk,khd->qhd",
        prior_weights.astype(jnp.bfloat16),
        stored_values,
        preferred_element_type=jnp.float32,
    )
    combined = combined + jnp.einsum(
        "hqk,khd->qhd",
        group_weights.astype(jnp.bfloat16),
        group_values,
        preferred_element_type=jnp.float32,
    )
    prefill_attended = (
        (combined / jnp.transpose(weight_total)[:, :, None])
        .reshape(group_rows, local_width)
        .astype(jnp.bfloat16)
    )
    own_queries = queries[group_rows:]
    slot_queries = lax.all_gather(own_queries, "dp", axis=0, tiled=True)
    pool_count = page_slots.shape[0]
    pool_local = pool_keys.shape[0]
    logical_of_slot = (
        jnp.zeros((pool_count,), jnp.int32)
        .at[page_slots]
        .set(jnp.arange(pool_count, dtype=jnp.int32))
    )
    local_logical = lax.dynamic_slice_in_dim(logical_of_slot, data_index * pool_local, pool_local)
    page_owner = (
        jnp.sum((first_page[None, :] <= local_logical[:, None]).astype(jnp.int32), axis=1) - 1
    )
    page_number = local_logical - jnp.take(first_page, page_owner)
    page_slot = jnp.take(slot_of_request, page_owner)
    page_queries = jnp.take(slot_queries, page_slot, axis=0).reshape(pool_local, head_count, HEAD)
    page_keys = pool_keys.reshape(pool_local, PAGE, head_count, HEAD)
    page_scores = (
        jnp.einsum("phd,pkhd->phk", page_queries, page_keys, preferred_element_type=jnp.float32)
        * score_scale
    )
    key_place = page_number[:, None] * PAGE + jnp.arange(PAGE, dtype=jnp.int32)[None, :]
    page_live = key_place < jnp.take(cache_length, page_owner)[:, None]
    page_scores = jnp.where(page_live[:, None, :], page_scores, NEG_FILL)
    member = page_slot[:, None] == slot_numbers[None, :]
    page_top = jnp.max(page_scores, axis=2)
    slot_top = jnp.max(jnp.where(member[:, :, None], page_top[:, None, :], NEG_FILL), axis=0)
    page_weights = jnp.exp(page_scores - jnp.take(slot_top, page_slot, axis=0)[:, :, None])
    member_weights = member.astype(jnp.float32)
    slot_total = jnp.dot(
        member_weights.T, jnp.sum(page_weights, axis=2), precision=lax.Precision.HIGHEST
    )
    page_values = pool_values.reshape(pool_local, PAGE, head_count, HEAD).astype(jnp.float32)
    page_mix = jnp.einsum(
        "phk,pkhd->phd", page_weights, page_values, precision=lax.Precision.HIGHEST
    )
    slot_mix = jnp.dot(
        member_weights.T, page_mix.reshape(pool_local, local_width), precision=lax.Precision.HIGHEST
    )
    merged_top, merged_total, merged_mix = merged(
        (slot_top, slot_total, slot_mix), "dp", combine_pair
    )
    mine_top = lax.dynamic_slice_in_dim(merged_top, data_index * decode_rows, decode_rows, 0)
    mine_total = lax.dynamic_slice_in_dim(merged_total, data_index * decode_rows, decode_rows, 0)
    mine_mix = lax.dynamic_slice_in_dim(merged_mix, data_index * decode_rows, decode_rows, 0)
    own_keys = keys_new[group_rows:].reshape(decode_rows, head_count, HEAD)
    own_score = (
        jnp.einsum(
            "rhd,rhd->rh",
            own_queries.reshape(decode_rows, head_count, HEAD),
            own_keys,
            preferred_element_type=jnp.float32,
        )
        * score_scale
    )
    final_top = jnp.maximum(mine_top, own_score)
    cache_factor = jnp.exp(mine_top - final_top)
    own_factor = jnp.exp(own_score - final_top)
    final_total = mine_total * cache_factor + own_factor
    final_mix = rescale(mine_mix, cache_factor, HEAD) + rescale(
        values_new[group_rows:].astype(jnp.float32), own_factor, HEAD
    )
    decode_attended = rescale(final_mix, 1.0 / final_total, HEAD).astype(jnp.bfloat16)
    attended = jnp.concatenate([prefill_attended, decode_attended], axis=0)
    residual = lax.dynamic_slice_in_dim(tokens, model_index * local_width, local_width, 1)
    terms = jnp.dot(
        attended,
        lax.all_gather(out_weight, "dp", axis=1, tiled=True),
        preferred_element_type=jnp.float32,
    )
    branch = lax.psum_scatter(
        terms.astype(jnp.bfloat16), "fsdp", scatter_dimension=1, tiled=True
    ).astype(jnp.float32)
    result = (residual.astype(jnp.float32) + branch).astype(jnp.bfloat16)
    return (result[:group_rows], result[group_rows:])


def solution(mesh):
    in_specs = (
        P("dp", None),
        P("dp", None),
        P("dp", "fsdp"),
        P("dp", "fsdp"),
        P("dp", "fsdp"),
        P("fsdp", "dp"),
        P("dp", None, "fsdp"),
        P("dp", None, "fsdp"),
        P("dp"),
        P("dp", None, "fsdp"),
        P("dp", None, "fsdp"),
        P(),
        P(),
        P(),
        P(),
    )
    out_specs = (P("dp", "fsdp"), P("dp", "fsdp"))
    return jax.shard_map(
        per_device, mesh=mesh, in_specs=in_specs, out_specs=out_specs, check_vma=False
    )
```

profile of v0, /device:TPU:1, one launch (start us, length us, event | category | flops | bytes accessed | tf_op | source)
XLA Modules:
  0.0 471.2 jit_solution(2688506723281561803)
XLA Ops:
  11.9 6.2 %scatter_custom_fusion.1 = s32[1536]{0:T(1024)S(1)} fusion(s32[1536]{0:T(1024)S(1)} %compare_select_fusion, s32[1536]{0:T(1024)S(1)} %iota.55, s32[]{:T(128)} %constant.45.clone.1), kind=kCustom, calls=%fused_computation.111 | custom fusion | bytes 6148 | tf_op jit(solution)/shard_map/scatter | solution.py:162
  24.2 4.7 %copy.120 = bf16[48,128,256]{1,2,0:T(8,128)(2,1)} copy(bf16[48,128,256]{2,1,0:T(8,128)(2,1)} %param.30) | data formatting | bytes 6291456 | tf_op jit(solution)/shard_map/reshape | solution.py:171
  28.9 1.7 constant_dynamic-update-slice_fusion.1
  31.8 1.9 fusion.9
  35.9 1.8 multiply_cosine_fusion
  37.9 47.8 %all-gather.10.cloned.1.call-done = bf16[2048,256]{1,0:T(8,128)(2,1)} async-done(((bf16[64,256]{1,0:T(8,128)(2,1)}), bf16[2048,256]{1,0:T(8,128)(2,1)}) %all-gather.10.cloned.1.call-update) | async-done | bytes 1048592 | tf_op jit(solution)/shard_map/all_gather | solution.py:91
  85.7 3.4 fusion.77
  89.1 2.1 reshape.284
  91.2 71.0 %all-gather.12.cloned.1.call-done = bf16[2048,256]{1,0:T(8,128)(2,1)} async-done(((bf16[64,256]{1,0:T(8,128)(2,1)}), bf16[2048,256]{1,0:T(8,128)(2,1)}) %all-gather.12.cloned.1.call-update) | async-done | bytes 1048592 | tf_op jit(solution)/shard_map/all_gather | solution.py:92
  162.2 3.4 fusion.78
  165.5 2.1 reshape.285
  167.6 2.7 fusion.74
  172.1 37.0 %all-gather.3 = bf16[32,4,256]{2,1,0:T(4,128)(2,1)S(1)} all-gather(bf16[1,4,256]{2,1,0:T(4,128)(2,1)S(1)} %bitcast.127), channel_id=1, replica_groups=mesh['dp'=32,'fsdp'=8] {'dp'}, dimensions={0}, use_global_device_ids=true | all-gather | bytes 67584 | tf_op jit(solution)/shard_map/all_gather | solution.py:156
  210.6 2.8 fusion.44
  216.8 2.5 fusion.13
  219.4 1.7 fusion.39
  222.5 2.3 copy.118
  224.8 2.2 reshape_squeeze.6
  227.0 32.3 %all-gather = f32[4096,2]{0,1:T(2,128)S(1)} all-gather(f32[128,2]{0,1:T(2,128)S(1)} %select_reduce_fusion), channel_id=2, replica_groups=mesh['dp'=32,'fsdp'=8] {'dp'}, dimensions={0}, use_global_device_ids=true | all-gather | bytes 33792 | tf_op jit(solution)/shard_map/all_gather | solution.py:16
  260.1 33.9 %all-gather.1 = f32[4096,2]{0,1:T(2,128)S(1)} all-gather(f32[128,2]{0,1:T(2,128)S(1)} %fusion.50), channel_id=3, replica_groups=mesh['dp'=32,'fsdp'=8] {'dp'}, dimensions={0}, use_global_device_ids=true | all-gather | bytes 33792 | tf_op jit(solution)/shard_map/all_gather | solution.py:16
  294.6 3.3 fusion.16
  299.6 1.9 fusion.4
  301.5 2.8 fusion.19
  304.3 2.7 convolution_convert_fusion.1
  308.4 1.8 copy.119
  310.2 2.1 fusion.17
  312.4 3.2 fusion.24
  315.6 6.4 %all-gather.18.cloned.1.call-done = f32[4096,256]{1,0:T(8,128)} async-done(((f32[128,256]{1,0:T(8,128)}), f32[4096,256]{1,0:T(8,128)}) %all-gather.18.cloned.1.call-update) | async-done | bytes 4194320 | tf_op jit(solution)/shard_map/all_gather | solution.py:16
  322.0 4.5 slice.113
  326.4 72.1 %while.14 = (s32[]{:T(128)}, f32[128,2]{0,1:T(2,128)S(1)}, f32[128,2]{0,1:T(2,128)S(1)}, f32[128,256]{1,0:T(8,128)S(1)}, f32[31,128,2]{1,2,0:T(2,128)}, /*index=...) while((s32[]{:T(128)}, f32[128,2]{0,1:T(2,128)S(1)}, f32[128,2]{0,1:T(2,128)S(1)}, ...), condition=%wide.region_14.17_spmd, body=%wide.region_13.16_spmd.sunk | while | flops 99842 | bytes 931941 | solution.py:19
  400.0 3.7 convolution_convert_fusion
  403.7 58.3 %reduce-scatter.2.cloned.1.call-done = bf16[516,256]{1,0:T(8,128)(2,1)} async-done(((bf16[516,2048]{1,0:T(8,128)(2,1)}), bf16[516,256]{1,0:T(8,128)(2,1)}) %reduce-scatter.2.cloned.1.call-update) | async-done | bytes 264208 | tf_op jit(solution)/shard_map/reduce_scatter | solution.py:225
  (316 shorter events, 101.3 us)
Async XLA Ops:
  7.2 209.7 %copy-start = (bf16[48,128,256]{2,1,0:T(8,128)(2,1)S(1)}, bf16[48,128,256]{2,1,0:T(8,128)(2,1)}, u32[]{:S(2)}) copy-start(bf16[48,128,256]{2,1,0:T(8,128)(2,1)} %param.31) | copy-start | bytes 9437188
  7.2 78.5 %all-gather.10.cloned.1.call-start = ((), (), s32[]{:S(2)}) async-start(), calls=%async_computation.1 | async-start | bytes 1081344 | tf_op jit(solution)/shard_map/all_gather | solution.py:91
  7.9 154.2 %all-gather.12.cloned.1.call-start = ((), (), s32[]{:S(2)}) async-start(), calls=%async_computation.2 | async-start | bytes 1081344 | tf_op jit(solution)/shard_map/all_gather | solution.py:92
  8.7 295.7 %all-gather.14.cloned.1.call-start = ((), (), s32[]{:S(2)}) async-start(), calls=%async_computation.3 | async-start | bytes 1081344 | tf_op jit(solution)/shard_map/all_gather | solution.py:93
  9.4 312.6 %all-gather.18.cloned.1.call-start = ((), (), s32[]{:S(2)}) async-start(), calls=%async_computation.6 | async-start | bytes 4325376 | tf_op jit(solution)/shard_map/all_gather | solution.py:16
  23.5 5.4 %copy-start.17 = (s32[48]{0:T(128)}, s32[48]{0:T(128)S(1)}, u32[]{:S(2)}) copy-start(s32[48]{0:T(128)S(1)} %get-tuple-element.103) | copy-start | bytes 580
  28.9 1.7 copy-start.15
  30.7 3.0 copy-start.1
  35.8 173.3 %copy-start.16 = (s32[1024]{0:T(1024)}, s32[1024]{0:T(1024)S(1)}, u32[]{:S(2)}) copy-start(s32[1024]{0:T(1024)S(1)} %pad_clamp_fusion) | copy-start | bytes 12292
  37.9 175.6 %copy-start.14 = (pred[48,128]{1,0:T(8,128)(4,1)}, pred[48,128]{1,0:T(8,128)(4,1)S(1)}, u32[]{:S(2)}) copy-start(pred[48,128]{1,0:T(8,128)(4,1)S(1)} %add_compare_fusion) | copy-start | bytes 18436
  167.6 2.7 copy-start.7
  167.6 2.7 copy-start.8
  170.7 0.7 copy-start.3
  170.7 1.4 copy-start.5
  170.7 1.4 copy-start.6
  219.4 40.5 %copy-start.18 = (s32[48]{0:T(128)S(1)}, s32[48]{0:T(128)}, u32[]{:S(2)}) copy-start(s32[48]{0:T(128)} %copy-done.17) | copy-start | bytes 580
  221.1 178.9 %all-gather.16.cloned.1.call-start = ((), (), s32[]{:S(2)}) async-start(), calls=%async_computation.4 | async-start | bytes 1081344 | tf_op jit(solution)/shard_map/all_gather | solution.py:222
  221.7 240.2 %reduce-scatter.2.cloned.1.call-start = ((), (), s32[]{:S(2)}) async-start(), calls=%async_computation.5 | async-start | bytes 2396160 | tf_op jit(solution)/shard_map/reduce_scatter | solution.py:225
  227.0 71.0 %copy-start.2 = (bf16[2048,2,128]{2,1,0:T(2,128)(2,1)S(1)}, bf16[2048,2,128]{2,1,0:T(2,128)(2,1)}, u32[]{:S(2)}) copy-start(bf16[2048,2,128]{2,1,0:T(2,128)(2,1)} %reshape_squeeze.6) | copy-start | bytes 3145732
  227.0 71.0 %copy-start.4 = (bf16[516,2,64]{2,0,1:T(8,128)(2,1)S(1)}, bf16[516,2,64]{2,0,1:T(8,128)(2,1)}, u32[]{:S(2)}) copy-start(bf16[516,2,64]{2,0,1:T(8,128)(2,1)} %copy-done.3) | copy-start | bytes 396292
  259.3 40.3 %copy-start.12 = (f32[4096,2]{0,1:T(2,128)}, f32[4096,2]{0,1:T(2,128)S(1)}, u32[]{:S(2)}) copy-start(f32[4096,2]{0,1:T(2,128)S(1)} %all-gather) | copy-start | bytes 98308
  294.0 5.6 %copy-start.13 = (f32[4096,2]{0,1:T(2,128)}, f32[4096,2]{0,1:T(2,128)S(1)}, u32[]{:S(2)}) copy-start(f32[4096,2]{0,1:T(2,128)S(1)} %all-gather.1) | copy-start | bytes 98308
  299.6 1.9 copy-start.10
  304.3 5.9 %copy-start.9 = (pred[512,512]{0,1:T(8,128)(4,1)S(1)}, pred[512,512]{0,1:T(8,128)(4,1)}, u32[]{:S(2)}) copy-start(pred[512,512]{0,1:T(8,128)(4,1)} %iota_compare_fusion) | copy-start | bytes 786436
  307.0 0.7 copy-start.11
  322.0 4.5 slice-start
  322.0 4.5 slice-start.1
  322.0 4.5 slice-start.2
  326.4 72.1 %copy-start.19 = (f32[4,2]{0,1:T(2,128)S(1)}, f32[4,2]{0,1:T(2,128)}, u32[]{:S(2)}) copy-start(f32[4,2]{0,1:T(2,128)} %get-tuple-element.104) | copy-start | bytes 100
Sparse Core Ops, SparseCore 0:
  10.6 75.0 all-gather.9
  88.3 73.8 all-gather.11
  164.7 73.8 all-gather.13
  241.1 80.8 all-gather.17
  324.4 71.7 all-gather.15
  403.8 58.1 reduce-scatter.1
where the time goes:
time: 475 us; the launch traced here: 471 us
  waiting for transfers between devices  186 us (39%)
  blocking collectives  103 us (22%)
  other arithmetic  72.1 us (15%)
  local copies, waits for them, and re-layouts  62.6 us (13%)
  matrix products  31.3 us (7%)
  between operations  15.1 us (3%)
    all_gather x1, waiting for transfers between devices, per_device(): lax.all_gather(key_weight, 'dp', axis=0, tiled=True)  71 us
    all_gather x2, blocking collectives, merged(): pieces = jax.tree.map(lambda part: lax.all_gather(part, axis), value)  66.2 us
    reduce_scatter x1, waiting for transfers between devices, per_device(): lax.psum_scatter(terms.astype(jnp.bfloat16), 'fsdp', scatter_dimension=1,...  58.3 us
    all_gather x1, waiting for transfers between devices, per_device(): lax.all_gather(query_weight, 'dp', axis=0, tiled=True)  47.8 us
    all_gather x1, blocking collectives, per_device(): slot_queries = lax.all_gather(own_queries, 'dp', axis=0, tiled=True)  37 us
    add x31, other arithmetic, combine_pair(): rescale(early_mix, early_factor, HEAD)  30.6 us
    add x31, other arithmetic, combine_pair(): joined_total = early_total * early_factor + late_total * late_factor  21.6 us
    mul x62, local copies, waits for them, and re-layouts, rescale(): return (shaped * factor[:, :, None]).reshape(vectors.shape)  12.2 us
  transfers between devices with their start and end apart: 6, of which 4 were waited for; matrix products, arithmetic and copies ran while one was open for 34% of the time, Pallas kernels for 0%

commit v1 on v0

--- a/solution.py
+++ b/solution.py
@@ -1,3 +1,5 @@
+import functools
+
 import jax
 import jax.numpy as jnp
 from jax import lax
@@ -10,14 +12,6 @@
 EPSILON = 1e-05
 ROPE_BASE = 10000.0
 NEG_FILL = -1e30
-
-
-def merged(value, axis, join):
-    pieces = jax.tree.map(lambda part: lax.all_gather(part, axis), value)
-    head = jax.tree.map(lambda part: part[0], pieces)
-    tail = jax.tree.map(lambda part: part[1:], pieces)
-    total, _ = lax.scan(lambda total, share: (join(total, share), None), head, tail)
-    return total
 
 
 def layer_norm(rows_in):
@@ -50,15 +44,11 @@
     return (shaped * factor[:, :, None]).reshape(vectors.shape)
 
 
-def combine_pair(earlier, later):
-    early_top, early_total, early_mix = earlier
-    late_top, late_total, late_mix = later
-    joined_top = jnp.maximum(early_top, late_top)
-    early_factor = jnp.exp(early_top - joined_top)
-    late_factor = jnp.exp(late_top - joined_top)
-    joined_total = early_total * early_factor + late_total * late_factor
-    joined_mix = rescale(early_mix, early_factor, HEAD) + rescale(late_mix, late_factor, HEAD)
-    return (joined_top, joined_total, joined_mix)
+def inverse_permutation(order):
+    count = order.shape[0]
+    numbers = jnp.arange(count, dtype=jnp.int32)
+    hit = order[None, :] == numbers[:, None]
+    return jnp.sum(jnp.where(hit, numbers[None, :], 0), axis=1)
 
 
 def per_device(
@@ -77,40 +67,54 @@
     page_counts,
     last_fill,
     decode_request,
+    *,
+    dp_size,
 ):
     group_rows = prefill_tokens.shape[0]
     decode_rows = decode_tokens.shape[0]
+    weight_rows = query_weight.shape[0]
     local_width = query_weight.shape[1]
     head_count = local_width // HEAD
     score_scale = HEAD ** (-0.5)
     data_index = lax.axis_index("dp")
     model_index = lax.axis_index("fsdp")
-    tokens = jnp.concatenate([prefill_tokens, decode_tokens], axis=0)
+
+    projection_piece = jnp.concatenate([query_weight, key_weight, value_weight], axis=1)
+    bundle_width = projection_piece.shape[1]
+    out_size = out_weight.size
+    tail = jnp.concatenate([out_weight.reshape(-1), decode_tokens.reshape(-1)])
+    bundle = jnp.concatenate([projection_piece, tail.reshape(-1, bundle_width)], axis=0)
+    gathered = lax.all_gather(bundle, "dp", axis=0, tiled=False)
+    projection_weight = gathered[:, :weight_rows].reshape(-1, bundle_width)
+    gathered_tail = gathered[:, weight_rows:].reshape(dp_size, -1)
+    out_full = jnp.transpose(
+        gathered_tail[:, :out_size].reshape(dp_size, out_weight.shape[0], out_weight.shape[1]),
+        (1, 0, 2),
+    ).reshape(out_weight.shape[0], -1)
+    all_decode = gathered_tail[:, out_size:].reshape(dp_size * decode_rows, -1)
+
+    tokens = jnp.concatenate([prefill_tokens, all_decode], axis=0)
     normed = layer_norm(tokens)
-    portions = (
-        lax.all_gather(query_weight, "dp", axis=0, tiled=True),
-        lax.all_gather(key_weight, "dp", axis=0, tiled=True),
-        lax.all_gather(value_weight, "dp", axis=0, tiled=True),
-    )
-    raw_queries, raw_keys, raw_values = tuple(
-        (jnp.dot(normed, portion, preferred_element_type=jnp.float32) for portion in portions)
-    )
+    raw = jnp.dot(normed, projection_weight, preferred_element_type=jnp.float32)
+    raw_queries = raw[:, :local_width]
+    raw_keys = raw[:, local_width : 2 * local_width]
+    raw_values = raw[:, 2 * local_width :]
+
     cache_length = (page_counts - 1) * PAGE + last_fill
     first_page = jnp.cumsum(page_counts) - page_counts
     request_count = decode_request.shape[0]
     slot_numbers = jnp.arange(request_count, dtype=jnp.int32)
-    slot_of_request = jnp.zeros((request_count,), jnp.int32).at[decode_request].set(slot_numbers)
-    my_slots = data_index * decode_rows + jnp.arange(decode_rows, dtype=jnp.int32)
-    my_requests = jnp.take(decode_request, my_slots)
+    slot_of_request = inverse_permutation(decode_request)
     positions = jnp.concatenate(
         [
             prior_length[0] + jnp.arange(group_rows, dtype=jnp.int32),
-            jnp.take(cache_length, my_requests),
+            jnp.take(cache_length, decode_request),
         ]
     )
     queries = rotary(raw_queries, positions, HEAD).astype(jnp.bfloat16)
     keys_new = rotary(raw_keys, positions, HEAD).astype(jnp.bfloat16)
     values_new = raw_values.astype(jnp.bfloat16)
+
     prior_slots = prior_keys.shape[1]
     group_queries = queries[:group_rows].reshape(group_rows, head_count, HEAD)
     group_keys = keys_new[:group_rows].reshape(group_rows, head_count, HEAD)
@@ -152,16 +156,19 @@
         .reshape(group_rows, local_width)
         .astype(jnp.bfloat16)
     )
-    own_queries = queries[group_rows:]
-    slot_queries = lax.all_gather(own_queries, "dp", axis=0, tiled=True)
+
+    slot_queries = queries[group_rows:]
+    own_start = data_index * decode_rows
+    own_queries = lax.dynamic_slice_in_dim(slot_queries, own_start, decode_rows, 0)
+    own_keys = lax.dynamic_slice_in_dim(keys_new[group_rows:], own_start, decode_rows, 0)
+    own_values = lax.dynamic_slice_in_dim(values_new[group_rows:], own_start, decode_rows, 0)
     pool_count = page_slots.shape[0]
     pool_local = pool_keys.shape[0]
-    logical_of_slot = (
-        jnp.zeros((pool_count,), jnp.int32)
-        .at[page_slots]
-        .set(jnp.arange(pool_count, dtype=jnp.int32))
-    )
-    local_logical = lax.dynamic_slice_in_dim(logical_of_slot, data_index * pool_local, pool_local)
+    local_slots = data_index * pool_local + jnp.arange(pool_local, dtype=jnp.int32)
+    slot_hit = page_slots[None, :] == local_slots[:, None]
+    local_logical = jnp.sum(
+        jnp.where(slot_hit, jnp.arange(pool_count, dtype=jnp.int32)[None, :], 0), axis=1
+    )
     page_owner = (
         jnp.sum((first_page[None, :] <= local_logical[:, None]).astype(jnp.int32), axis=1) - 1
     )
@@ -178,7 +185,8 @@
     page_scores = jnp.where(page_live[:, None, :], page_scores, NEG_FILL)
     member = page_slot[:, None] == slot_numbers[None, :]
     page_top = jnp.max(page_scores, axis=2)
-    slot_top = jnp.max(jnp.where(member[:, :, None], page_top[:, None, :], NEG_FILL), axis=0)
+    local_top = jnp.max(jnp.where(member[:, :, None], page_top[:, None, :], NEG_FILL), axis=0)
+    slot_top = lax.pmax(local_top, "dp")
     page_weights = jnp.exp(page_scores - jnp.take(slot_top, page_slot, axis=0)[:, :, None])
     member_weights = member.astype(jnp.float32)
     slot_total = jnp.dot(
@@ -191,18 +199,16 @@
     slot_mix = jnp.dot(
         member_weights.T, page_mix.reshape(pool_local, local_width), precision=lax.Precision.HIGHEST
     )
-    merged_top, merged_total, merged_mix = merged(
-        (slot_top, slot_total, slot_mix), "dp", combine_pair
-    )
-    mine_top = lax.dynamic_slice_in_dim(merged_top, data_index * decode_rows, decode_rows, 0)
-    mine_total = lax.dynamic_slice_in_dim(merged_total, data_index * decode_rows, decode_rows, 0)
-    mine_mix = lax.dynamic_slice_in_dim(merged_mix, data_index * decode_rows, decode_rows, 0)
-    own_keys = keys_new[group_rows:].reshape(decode_rows, head_count, HEAD)
+    partials = jnp.concatenate([slot_total, slot_mix], axis=1)
+    mine = lax.psum_scatter(partials, "dp", scatter_dimension=0, tiled=True)
+    mine_total = mine[:, :head_count]
+    mine_mix = mine[:, head_count:]
+    mine_top = lax.dynamic_slice_in_dim(slot_top, own_start, decode_rows, 0)
     own_score = (
         jnp.einsum(
             "rhd,rhd->rh",
             own_queries.reshape(decode_rows, head_count, HEAD),
-            own_keys,
+            own_keys.reshape(decode_rows, head_count, HEAD),
             preferred_element_type=jnp.float32,
         )
         * score_scale
@@ -212,16 +218,13 @@
     own_factor = jnp.exp(own_score - final_top)
     final_total = mine_total * cache_factor + own_factor
     final_mix = rescale(mine_mix, cache_factor, HEAD) + rescale(
-        values_new[group_rows:].astype(jnp.float32), own_factor, HEAD
+        own_values.astype(jnp.float32), own_factor, HEAD
     )
     decode_attended = rescale(final_mix, 1.0 / final_total, HEAD).astype(jnp.bfloat16)
     attended = jnp.concatenate([prefill_attended, decode_attended], axis=0)
-    residual = lax.dynamic_slice_in_dim(tokens, model_index * local_width, local_width, 1)
-    terms = jnp.dot(
-        attended,
-        lax.all_gather(out_weight, "dp", axis=1, tiled=True),
-        preferred_element_type=jnp.float32,
-    )
+    own_tokens = jnp.concatenate([prefill_tokens, decode_tokens], axis=0)
+    residual = lax.dynamic_slice_in_dim(own_tokens, model_index * local_width, local_width, 1)
+    terms = jnp.dot(attended, out_full, preferred_element_type=jnp.float32)
     branch = lax.psum_scatter(
         terms.astype(jnp.bfloat16), "fsdp", scatter_dimension=1, tiled=True
     ).astype(jnp.float32)
@@ -249,5 +252,9 @@
     )
     out_specs = (P("dp", "fsdp"), P("dp", "fsdp"))
     return jax.shard_map(
-        per_device, mesh=mesh, in_specs=in_specs, out_specs=out_specs, check_vma=False
-    )
+        functools.partial(per_device, dp_size=mesh.shape["dp"]),
+        mesh=mesh,
+        in_specs=in_specs,
+        out_specs=out_specs,
+        check_vma=False,
+    )

time: 475 us -> 478 us (level)
  waiting for transfers between devices: 186 us -> 241 us
  other arithmetic: 72.1 us -> 25 us
  blocking collectives: 103 us -> 112 us
  matrix products: 31.3 us -> 22.4 us
    unnamed x6 -> x4, waiting for transfers between devices: 2.62 us -> 145 us
    pmax x0 -> x1, blocking collectives: none -> 112 us  [per_device(): slot_top = lax.pmax(local_top, 'dp')]
    all_gather x3 -> x0, blocking collectives: 103 us -> none  [the longest x2 66.2 us: merged(): pieces = jax.tree.map(lambda part: lax.all_gather(part, axis), value)]
    all_gather x5 -> x1, waiting for transfers between devices: 125 us -> 59.6 us  [per_device(): gathered = lax.all_gather(bundle, 'dp', axis=0, tiled=False)]
    add x62 -> x1, other arithmetic: 52.2 us -> 0.01 us  [per_device(): data_index * pool_local + jnp.arange(pool_local, dtype=jnp.int32)]
    reduce_scatter x1, waiting for transfers between devices: 58.3 us -> 36.2 us  [per_device(): lax.psum_scatter(terms.astype(jnp.bfloat16), 'fsdp', scatter_dimension=1,...]
    mul x62 -> x0, local copies, waits for them, and re-layouts: 12.2 us -> none  [rescale(): return (shaped * factor[:, :, None]).reshape(vectors.shape)]
    slice x7 -> x9, local copies, waits for them, and re-layouts: 4.47 us -> 13.2 us  [the longest x1 3.97 us: per_device(): projection_weight = gathered[:, :weight_rows].reshape(-1, bundle_width)]
  transfers between devices with their start and end apart: 6 -> 3, of which waited for: 4 -> 3; matrix products, arithmetic and copies ran while one was open for 34% -> 9% of each run, Pallas kernels for 0% -> 0%
where the time goes in v1:
time: 478 us; the launch traced here: 475 us
  waiting for transfers between devices  241 us (50%)
  blocking collectives  112 us (23%)
  local copies, waits for them, and re-layouts  58.8 us (12%)
  other arithmetic  25 us (5%)
  matrix products  22.4 us (5%)
  between operations  15.5 us (3%)
    unnamed x4, waiting for transfers between devices  145 us
    pmax x1, blocking collectives, per_device(): slot_top = lax.pmax(local_top, 'dp')  112 us
    all_gather x1, waiting for transfers between devices, per_device(): gathered = lax.all_gather(bundle, 'dp', axis=0, tiled=False)  59.6 us
    reduce_scatter x1, waiting for transfers between devices, per_device(): lax.psum_scatter(terms.astype(jnp.bfloat16), 'fsdp', scatter_dimension=1,...  36.2 us
  transfers between devices with their start and end apart: 3, of which 3 were waited for; matrix products, arithmetic and copies ran while one was open for 9% of the time, Pallas kernels for 0%

profile of v1, /device:TPU:1, one launch (start us, length us, event | category | flops | bytes accessed | tf_op | source)
XLA Modules:
  0.0 474.6 jit_solution(4003070454238723475)
XLA Ops:
  9.2 1.5 pad_maximum_fusion.3
  19.2 2.2 reshape_squeeze.6
  21.4 2.3 copy.91
  23.7 4.7 copy.93
  32.3 2.1 multiply_cosine_fusion
  34.4 59.6 %all-gather.3.cloned.1.call-done = bf16[3072,768]{1,0:T(8,128)(2,1)} async-done(((bf16[96,768]{1,0:T(8,128)(2,1)}), bf16[3072,768]{1,0:T(8,128)(2,1)}) %all-gather.3.cloned.1.call-update) | async-done | bytes 4718608 | tf_op jit(solution)/shard_map/all_gather | solution.py:87
  94.0 1.5 slice.106
  95.5 4.0 slice.108
  102.3 2.2 reshape.307
  104.6 2.3 convert_reduce_fusion
  106.9 1.9 fusion.5
  108.8 5.1 %fusion.80 = (bf16[640,768]{1,0:T(8,128)(2,1)}, f32[640,768]{1,0:T(8,128)S(1)}) fusion(bf16[2048,768]{1,0:T(8,128)(2,1)} %bitcast.96, f32[640]{0:T(1024)S(1)} %add_rsqrt_fusion, f32[640]{0:T(1024)S(1)} %broadcast_multiply_fusion, bf16[128,2048]{1,0:T(8,128)(2,1)S(1)} %copy-done.6, bf16[512,2048]{1,0:T(8,128)(2,1)S(1)} %copy-done.1), kind=kOutput, calls=%fused_computation.147 | convolution fusion | flops 2022932480 | bytes 8721408 | tf_op jit(solution)/shard_map/dot_general | solution.py:98
  115.1 2.2 reshape.310
  119.2 2.3 reshape.309
  121.5 2.1 fusion.78
  127.8 1.4 gather_fusion.1
  130.0 4.0 fusion.17
  137.2 112.0 %pmax.7 = f32[128,2]{1,0:T(8,128)S(1)} all-reduce(f32[128,2]{1,0:T(8,128)} %copy.72), channel_id=1, replica_groups=mesh['dp'=32,'fsdp'=8] {'dp'}, use_global_device_ids=true, to_apply=%region_12.14 | all-reduce | flops 256 | bytes 2048 | tf_op jit(solution)/shard_map/pmax | solution.py:189
  249.2 1.3 gather_fusion.2
  250.5 1.4 broadcast_select_fusion.1
  251.9 1.4 copy.73
  254.5 2.5 fusion.10
  258.3 2.9 fusion
  261.2 1.9 fusion.1
  263.2 2.0 fusion.20
  268.2 1.5 slice.120
  269.7 1.6 copy.75
  272.3 4.1 reshape.319
  276.4 2.7 copy.77
  279.1 144.9 %all-reduce.3.cloned.1.call-done = f32[128,258]{1,0:T(8,128)} async-done(((f32[128,258]{1,0:T(8,128)}), f32[128,258]{1,0:T(8,128)}) %all-reduce.3.cloned.1.call-update) | async-done | bytes 132112
  425.9 3.6 convolution_convert_fusion
  429.5 36.2 %reduce-scatter.2.cloned.1.call-done = bf16[516,256]{1,0:T(8,128)(2,1)} async-done(((bf16[516,2048]{1,0:T(8,128)(2,1)}), bf16[516,256]{1,0:T(8,128)(2,1)}) %reduce-scatter.2.cloned.1.call-update) | async-done | bytes 264208 | tf_op jit(solution)/shard_map/reduce_scatter | solution.py:228
  (123 shorter events, 38.0 us)
Async XLA Ops:
  7.2 247.4 %copy-start = (bf16[48,128,256]{2,1,0:T(8,128)(2,1)S(1)}, bf16[48,128,256]{2,1,0:T(8,128)(2,1)}, u32[]{:S(2)}) copy-start(bf16[48,128,256]{2,1,0:T(8,128)(2,1)} %param.27) | copy-start | bytes 9437188
  7.2 86.8 %all-gather.3.cloned.1.call-start = ((), (), s32[]{:S(2)}) async-start(), calls=%async_computation.2 | async-start | bytes 4866048 | tf_op jit(solution)/shard_map/all_gather | solution.py:87
  10.7 413.3 %all-reduce.3.cloned.1.call-start = ((), (), s32[]{:S(2)}) async-start(), calls=%async_computation.3 | async-start | bytes 393216
  23.7 4.7 copy-start.22
  23.7 7.1 %copy-start.21 = (s32[128]{0:T(128)S(1)}, s32[128]{0:T(128)}, u32[]{:S(2)}) copy-start(s32[128]{0:T(128)} %param.31) | copy-start | bytes 1540
  100.3 1.2 copy-start.3
  104.6 2.4 copy-start.1
  104.6 4.2 copy-start.6
  121.5 2.1 copy-start.5
  121.5 2.9 copy-start.9
  121.5 2.9 copy-start.10
  124.7 0.7 copy-start.7
  124.7 1.4 copy-start.11
  124.7 1.4 copy-start.12
  130.0 4.8 %copy-start.2 = (bf16[48,128,256]{1,2,0:T(8,128)(2,1)S(1)}, bf16[48,128,256]{1,2,0:T(8,128)(2,1)}, u32[]{:S(2)}) copy-start(bf16[48,128,256]{1,2,0:T(8,128)(2,1)} %copy.93) | copy-start | bytes 9437188
  130.0 6.4 %copy-start.19 = (pred[48,128]{1,0:T(8,128)(4,1)S(1)}, pred[48,128]{1,0:T(8,128)(4,1)}, u32[]{:S(2)}) copy-start(pred[48,128]{1,0:T(8,128)(4,1)} %iota_compare_fusion.2) | copy-start | bytes 18436
  135.7 0.6 copy-start.16
  258.3 2.9 copy-start.20
  258.3 207.4 %reduce-scatter.2.cloned.1.call-start = ((), (), s32[]{:S(2)}) async-start(), calls=%async_computation.1 | async-start | bytes 2396160 | tf_op jit(solution)/shard_map/reduce_scatter | solution.py:228
  261.2 1.9 copy-start.14
  263.1 2.1 copy-start.8
  263.1 2.1 copy-start.13
  263.1 2.6 copy-start.17
  265.7 1.4 copy-start.4
  265.8 5.5 %copy-start.15 = (bf16[128,2,128]{0,2,1:T(8,128)(2,1)S(1)}, bf16[128,2,128]{0,2,1:T(8,128)(2,1)}, u32[]{:S(2)}) copy-start(bf16[128,2,128]{0,2,1:T(8,128)(2,1)} %copy.70) | copy-start | bytes 196612
  425.9 39.8 %copy-start.18 = (bf16[4,2048]{1,0:T(4,128)(2,1)S(1)}, bf16[4,2048]{1,0:T(4,128)(2,1)}, u32[]{:S(2)}) copy-start(bf16[4,2048]{1,0:T(4,128)(2,1)} %param.18) | copy-start | bytes 49156
Sparse Core Ops, SparseCore 0:
  10.8 83.1 all-gather.2
  258.4 165.5 all-reduce.2
  429.6 36.0 reduce-scatter.1

commit v2 on v1

--- a/solution.py
+++ b/solution.py
@@ -185,8 +185,7 @@
     page_scores = jnp.where(page_live[:, None, :], page_scores, NEG_FILL)
     member = page_slot[:, None] == slot_numbers[None, :]
     page_top = jnp.max(page_scores, axis=2)
-    local_top = jnp.max(jnp.where(member[:, :, None], page_top[:, None, :], NEG_FILL), axis=0)
-    slot_top = lax.pmax(local_top, "dp")
+    slot_top = jnp.max(jnp.where(member[:, :, None], page_top[:, None, :], NEG_FILL), axis=0)
     page_weights = jnp.exp(page_scores - jnp.take(slot_top, page_slot, axis=0)[:, :, None])
     member_weights = member.astype(jnp.float32)
     slot_total = jnp.dot(
@@ -199,11 +198,19 @@
     slot_mix = jnp.dot(
         member_weights.T, page_mix.reshape(pool_local, local_width), precision=lax.Precision.HIGHEST
     )
-    partials = jnp.concatenate([slot_total, slot_mix], axis=1)
-    mine = lax.psum_scatter(partials, "dp", scatter_dimension=0, tiled=True)
-    mine_total = mine[:, :head_count]
-    mine_mix = mine[:, head_count:]
-    mine_top = lax.dynamic_slice_in_dim(slot_top, own_start, decode_rows, 0)
+    partials = jnp.concatenate([slot_top, slot_total, slot_mix], axis=1)
+    received = lax.all_to_all(
+        partials.reshape(dp_size, decode_rows, -1), "dp", 0, 0, tiled=False
+    )
+    source_top = received[:, :, :head_count]
+    source_total = received[:, :, head_count : 2 * head_count]
+    source_mix = received[:, :, 2 * head_count :]
+    mine_top = jnp.max(source_top, axis=0)
+    source_factor = jnp.exp(source_top - mine_top[None])
+    mine_total = jnp.sum(source_total * source_factor, axis=0)
+    mine_mix = jnp.sum(
+        source_mix.reshape(dp_size, decode_rows, head_count, HEAD) * source_factor[..., None], axis=0
+    ).reshape(decode_rows, local_width)
     own_score = (
         jnp.einsum(
             "rhd,rhd->rh",
@@ -224,10 +231,12 @@
     attended = jnp.concatenate([prefill_attended, decode_attended], axis=0)
     own_tokens = jnp.concatenate([prefill_tokens, decode_tokens], axis=0)
     residual = lax.dynamic_slice_in_dim(own_tokens, model_index * local_width, local_width, 1)
-    terms = jnp.dot(attended, out_full, preferred_element_type=jnp.float32)
-    branch = lax.psum_scatter(
-        terms.astype(jnp.bfloat16), "fsdp", scatter_dimension=1, tiled=True
-    ).astype(jnp.float32)
+    terms = jnp.dot(attended, out_full, preferred_element_type=jnp.float32).astype(jnp.bfloat16)
+    model_size = terms.shape[1] // local_width
+    shares = jnp.transpose(terms.reshape(terms.shape[0], model_size, local_width), (1, 0, 2))
+    branch = jnp.sum(
+        lax.all_to_all(shares, "fsdp", 0, 0, tiled=False).astype(jnp.float32), axis=0
+    )
     result = (residual.astype(jnp.float32) + branch).astype(jnp.bfloat16)
     return (result[:group_rows], result[group_rows:])
 

time: 478 us -> 225 us (0.47)
  waiting for transfers between devices: 241 us -> 88.7 us
  blocking collectives: 112 us -> 0 us
  starting transfers between devices: 0.12 us -> 15.7 us
    unnamed x4 -> x1, waiting for transfers between devices: 145 us -> 0.02 us
    pmax x1 -> x0, blocking collectives: 112 us -> none  [per_device(): slot_top = lax.pmax(local_top, 'dp')]
    reduce_scatter x1 -> x0, waiting for transfers between devices: 36.2 us -> none  [per_device(): lax.psum_scatter(terms.astype(jnp.bfloat16), 'fsdp', scatter_dimension=1,...]
    all_to_all x0 -> x2, waiting for transfers between devices: none -> 27.8 us  [the longest x1 26.7 us: per_device(): lax.all_to_all(shares, 'fsdp', 0, 0, tiled=False).astype(jnp.float32)]
    all_to_all x0 -> x2, starting transfers between devices: none -> 15.6 us  [the longest x1 9.83 us: per_device(): lax.all_to_all(shares, 'fsdp', 0, 0, tiled=False).astype(jnp.float32)]
  transfers between devices with their start and end apart: 3 -> 3, of which waited for: 3 -> 3; matrix products, arithmetic and copies ran while one was open for 9% -> 13% of each run, Pallas kernels for 0% -> 0%
where the time goes in v2:
time: 225 us; the launch traced here: 224 us
  waiting for transfers between devices  88.7 us (39%)
  local copies, waits for them, and re-layouts  58.9 us (26%)
  other arithmetic  25.1 us (11%)
  matrix products  20.1 us (9%)
  starting transfers between devices  15.7 us (7%)
  between operations  15.1 us (7%)
    all_gather x1, waiting for transfers between devices, per_device(): gathered = lax.all_gather(bundle, 'dp', axis=0, tiled=False)  60.8 us
    all_to_all x1, waiting for transfers between devices, per_device(): lax.all_to_all(shares, 'fsdp', 0, 0, tiled=False).astype(jnp.float32)  26.7 us
    all_to_all x1, starting transfers between devices, per_device(): lax.all_to_all(shares, 'fsdp', 0, 0, tiled=False).astype(jnp.float32)  9.83 us
    all_to_all x1, starting transfers between devices, per_device(): lax.all_to_all(partials.reshape(dp_size, decode_rows, -1), 'dp', 0, 0, ti...  5.79 us
    unnamed x53, local copies, waits for them, and re-layouts  5.05 us
    reshape x1, local copies, waits for them, and re-layouts, per_device(): page_keys = pool_keys.reshape(pool_local, PAGE, head_count, HEAD)  4.66 us
  transfers between devices with their start and end apart: 3, of which 3 were waited for; matrix products, arithmetic and copies ran while one was open for 13% of the time, Pallas kernels for 0%

profile of v2, /device:TPU:1, one launch (start us, length us, event | category | flops | bytes accessed | tf_op | source)
XLA Modules:
  0.0 223.5 jit_solution(5751060634929760157)
XLA Ops:
  9.2 1.5 pad_maximum_fusion.3
  19.2 2.2 reshape_squeeze.6
  21.3 2.3 %copy.94 = bf16[1,2048,256]{1,2,0:T(8,128)(2,1)} copy(bf16[1,2048,256]{2,1,0:T(8,128)(2,1)} %param.24) | data formatting | bytes 2097152 | tf_op jit(solution)/shard_map/reshape;squeeze | solution.py:123
  23.6 4.7 %copy.96 = bf16[48,128,256]{1,2,0:T(8,128)(2,1)} copy(bf16[48,128,256]{2,1,0:T(8,128)(2,1)} %param.26) | data formatting | bytes 6291456 | tf_op jit(solution)/shard_map/reshape | solution.py:178
  31.1 2.1 multiply_cosine_fusion
  33.1 60.8 %all-gather.3.cloned.1.call-done = bf16[3072,768]{1,0:T(8,128)(2,1)} async-done(((bf16[96,768]{1,0:T(8,128)(2,1)}), bf16[3072,768]{1,0:T(8,128)(2,1)}) %all-gather.3.cloned.1.call-update) | async-done | bytes 4718608 | tf_op jit(solution)/shard_map/all_gather | solution.py:87
  93.9 1.5 slice.110
  95.5 4.0 %slice.112 = bf16[32,64,768]{2,1,0:T(8,128)(2,1)} slice(bf16[32,96,768]{2,1,0:T(8,128)(2,1)} %bitcast.102), slice={[0:32], [0:64], [0:768]} | slice | bytes 6291456 | tf_op jit(solution)/shard_map/slice | solution.py:88
  102.2 2.3 %reshape.320 = bf16[128,2048]{1,0:T(8,128)(2,1)} reshape(bf16[32,8192]{1,0:T(8,128)(2,1)} %slice.111) | data formatting | bytes 1048576 | tf_op jit(solution)/shard_map/reshape | solution.py:94
  104.4 2.3 %convert_reduce_fusion = f32[640]{0:T(1024)S(1)} fusion(bf16[128,2048]{1,0:T(8,128)(2,1)} %reshape.320, bf16[512,2048]{1,0:T(8,128)(2,1)} %param.17), kind=kLoop, calls=%fused_computation.10 | loop fusion | flops 6552960 | bytes 2624000 | tf_op jit(solution)/shard_map/reduce_sum | solution.py:19
  106.8 1.9 fusion.5
  108.7 4.2 %fusion.80 = (bf16[640,768]{1,0:T(8,128)(2,1)S(1)}, f32[640,768]{1,0:T(8,128)S(1)}) fusion(bf16[2048,768]{1,0:T(8,128)(2,1)} %bitcast.104, f32[640]{0:T(1024)S(1)} %add_rsqrt_fusion, f32[640]{0:T(1024)S(1)} %broadcast_multiply_fusion, bf16[128,2048]{1,0:T(8,128)(2,1)S(1)} %copy-done.6, bf16[512,2048]{1,0:T(8,128)(2,1)S(1)} %copy-done.2), kind=kOutput, calls=%fused_computation.153 | convolution fusion | flops 2022932480 | bytes 8721408 | tf_op jit(solution)/shard_map/dot_general | solution.py:98
  114.7 2.2 %reshape.323 = f32[640,2,128]{2,1,0:T(2,128)} reshape(f32[640,256]{1,0:T(8,128)} %get-tuple-element.12) | data formatting | bytes 1310720 | tf_op jit(solution)/shard_map/reshape | solution.py:27
  117.7 2.2 %reshape.322 = f32[640,2,128]{2,1,0:T(2,128)} reshape(f32[640,256]{1,0:T(8,128)} %get-tuple-element.13) | data formatting | bytes 1310720 | tf_op jit(solution)/shard_map/reshape | solution.py:27
  120.0 2.1 fusion.78
  124.7 1.6 copy.77
  128.0 1.4 gather_fusion.1
  131.8 4.1 %reshape.333 = bf16[32,256,64]{2,1,0:T(8,128)(2,1)} reshape(bf16[32,16384]{1,0:T(8,128)(2,1)} %slice.128) | data formatting | bytes 2097152 | tf_op jit(solution)/shard_map/reshape | solution.py:91
  135.9 2.7 %copy.79 = bf16[256,32,64]{0,2,1:T(8,128)(2,1)} copy(bf16[256,32,64]{2,0,1:T(8,128)(2,1)} %bitcast.97) | data formatting | bytes 2097152 | tf_op jit(solution)/shard_map/transpose | solution.py:90
  138.6 4.0 %fusion.17 = (f32[2,512]{1,0:T(2,128)}, f32[2,512,512]{1,2,0:T(8,128)}) fusion(pred[512,512]{0,1:T(8,128)(4,1)} %iota_compare_fusion, bf16[640,2,64]{2,0,1:T(8,128)(2,1)} %copy-done.11, bf16[640,2,64]{2,0,1:T(8,128)(2,1)} %copy-done.12, bf16[640,2,64]{2,0,1:T(8,128)(2,1)} %copy-done.7, bf16[640,2,64]{2,0,1:T(8,128)(2,1)S(1)} %get-tuple-element.16), kind=kOutput, calls=%fused_computation.33 | convolution fusion | flops 136838144 | bytes 3018752 | tf_op jit(solution)/shard_map/qhd,khd->hqk/dot_general | solution.py:131
  147.0 1.4 broadcast_select_fusion.1
  148.4 1.4 copy.74
  151.1 2.5 %fusion.10 = f32[48,2,1,128]{3,2,1,0:T(1,128)S(1)} fusion(f32[48,2,128,1]{2,0,1,3:T(8,128)S(1)} %get-tuple-element.23, bf16[48,128,256]{2,1,0:T(8,128)(2,1)S(1)} %copy-done), kind=kOutput, calls=%fused_computation.20 | convolution fusion | flops 18874368 | bytes 3244032 | tf_op jit(solution)/shard_map/phk,pkhd->phd/dot_general | solution.py:195
  154.9 5.8 %all-to-all-start = ((f32[32,4,260]{2,1,0:T(4,128)}), f32[32,4,260]{2,1,0:T(4,128)S(1)}, u32[]{:S(2)}, u32[]{:S(2)}) async-start(f32[32,4,260]{2,1,0:T(4,128)} %reshape.330), calls=%async_computation | async-start | bytes 393216 | tf_op jit(solution)/shard_map/all_to_all | solution.py:202
  160.7 2.9 %fusion = (f32[2,512]{1,0:T(2,128)S(1)}, f32[2,512,2048]{2,1,0:T(8,128)S(1)}) fusion(pred[2048]{0:T(1024)(128)(4,1)S(1)} %iota_compare_fusion.4, bf16[2048,2,128]{2,1,0:T(2,128)(2,1)} %reshape_squeeze.6, bf16[640,2,64]{2,0,1:T(8,128)(2,1)} %copy-done.7, bf16[640,2,64]{2,0,1:T(8,128)(2,1)S(1)} %get-tuple-element.16), kind=kOutput, calls=%fused_computation.8 | convolution fusion | flops 543685632 | bytes 9771008 | tf_op jit(solution)/shard_map/qhd,khd->hqk/dot_general | solution.py:125
  163.6 1.9 fusion.1
  165.5 2.0 fusion.20
  171.8 2.2 convolution_convert_fusion
  174.8 1.8 copy.145
  176.6 9.8 %all-to-all-start.1 = ((bf16[8,516,256]{2,1,0:T(8,128)(2,1)}), bf16[8,516,256]{2,1,0:T(8,128)(2,1)}, u32[]{:S(2)}, u32[]{:S(2)}) async-start(bf16[8,516,256]{2,1,0:T(8,128)(2,1)} %bitcast.95), calls=%async_computation.1 | async-start | bytes 4259840 | tf_op jit(solution)/shard_map/all_to_all | solution.py:238
  186.4 26.7 %all-to-all-done.1 = bf16[8,516,256]{2,1,0:T(8,128)(2,1)} async-done(((bf16[8,516,256]{2,1,0:T(8,128)(2,1)}), bf16[8,516,256]{2,1,0:T(8,128)(2,1)}, u32[]{:S(2)}, u32[]{:S(2)}) %all-to-all-start.1) | async-done | bytes 2113568 | tf_op jit(solution)/shard_map/all_to_all | solution.py:238
  213.1 2.1 convert_reduce_fusion.1
  (129 shorter events, 38.1 us)
Async XLA Ops:
  7.2 143.9 %copy-start = (bf16[48,128,256]{2,1,0:T(8,128)(2,1)S(1)}, bf16[48,128,256]{2,1,0:T(8,128)(2,1)}, u32[]{:S(2)}) copy-start(bf16[48,128,256]{2,1,0:T(8,128)(2,1)} %param.27) | copy-start | bytes 9437188
  7.2 86.8 %all-gather.3.cloned.1.call-start = ((), (), s32[]{:S(2)}) async-start(), calls=%async_computation.2 | async-start | bytes 4866048 | tf_op jit(solution)/shard_map/all_gather | solution.py:87
  23.6 5.9 %copy-start.22 = (s32[128]{0:T(128)S(1)}, s32[128]{0:T(128)}, u32[]{:S(2)}) copy-start(s32[128]{0:T(128)} %param.31) | copy-start | bytes 1540
  104.4 2.4 %copy-start.2 = (bf16[512,2048]{1,0:T(8,128)(2,1)S(1)}, bf16[512,2048]{1,0:T(8,128)(2,1)}, u32[]{:S(2)}) copy-start(bf16[512,2048]{1,0:T(8,128)(2,1)} %param.17) | copy-start | bytes 6291460
  104.4 4.2 %copy-start.6 = (bf16[128,2048]{1,0:T(8,128)(2,1)S(1)}, bf16[128,2048]{1,0:T(8,128)(2,1)}, u32[]{:S(2)}) copy-start(bf16[128,2048]{1,0:T(8,128)(2,1)} %reshape.320) | copy-start | bytes 1572868
  120.0 2.1 copy-start.5
  120.0 2.9 %copy-start.9 = (f32[640,64]{1,0:T(8,128)S(1)}, f32[640,64]{1,0:T(8,128)}, u32[]{:S(2)}) copy-start(f32[640,64]{1,0:T(8,128)} %get-tuple-element.24) | copy-start | bytes 491524
  120.0 2.9 %copy-start.10 = (f32[640,64]{1,0:T(8,128)S(1)}, f32[640,64]{1,0:T(8,128)}, u32[]{:S(2)}) copy-start(f32[640,64]{1,0:T(8,128)} %get-tuple-element.25) | copy-start | bytes 491524
  123.2 0.7 copy-start.7
  123.3 1.5 copy-start.11
  123.3 1.4 copy-start.12
  135.8 6.7 %copy-start.20 = (pred[48]{0:T(512)(128)(4,1)S(1)}, pred[48]{0:T(512)(128)(4,1)}, u32[]{:S(2)}) copy-start(pred[48]{0:T(512)(128)(4,1)} %get-tuple-element.8) | copy-start | bytes 148
  138.6 4.1 %copy-start.4 = (bf16[48,128,256]{1,2,0:T(8,128)(2,1)S(1)}, bf16[48,128,256]{1,2,0:T(8,128)(2,1)}, u32[]{:S(2)}) copy-start(bf16[48,128,256]{1,2,0:T(8,128)(2,1)} %copy.96) | copy-start | bytes 9437188
  138.6 5.7 %copy-start.18 = (pred[48,128]{1,0:T(8,128)(4,1)S(1)}, pred[48,128]{1,0:T(8,128)(4,1)}, u32[]{:S(2)}) copy-start(pred[48,128]{1,0:T(8,128)(4,1)} %iota_compare_fusion.2) | copy-start | bytes 18436
  143.6 0.6 copy-start.15
  154.9 15.2 %all-to-all-start = ((f32[32,4,260]{2,1,0:T(4,128)}), f32[32,4,260]{2,1,0:T(4,128)S(1)}, u32[]{:S(2)}, u32[]{:S(2)}) async-start(f32[32,4,260]{2,1,0:T(4,128)} %reshape.330), calls=%async_computation | async-start | bytes 393216 | tf_op jit(solution)/shard_map/all_to_all | solution.py:202
  160.6 2.9 %copy-start.21 = (f32[2,512]{1,0:T(2,128)S(1)}, f32[2,512]{1,0:T(2,128)}, u32[]{:S(2)}) copy-start(f32[2,512]{1,0:T(2,128)} %get-tuple-element.34) | copy-start | bytes 12292
  163.6 1.9 copy-start.14
  165.5 2.1 copy-start.8
  165.5 2.1 copy-start.13
  165.5 2.6 %copy-start.16 = (bf16[512,256]{0,1:T(8,128)(2,1)S(1)}, bf16[512,256]{0,1:T(8,128)(2,1)}, u32[]{:S(2)}) copy-start(bf16[512,256]{0,1:T(8,128)(2,1)} %copy.95) | copy-start | bytes 786436
  168.1 2.1 copy-start.19
  176.6 38.6 %copy-start.17 = (bf16[4,2048]{1,0:T(4,128)(2,1)S(1)}, bf16[4,2048]{1,0:T(4,128)(2,1)}, u32[]{:S(2)}) copy-start(bf16[4,2048]{1,0:T(4,128)(2,1)} %param.18) | copy-start | bytes 49156
  176.6 36.5 %all-to-all-start.1 = ((bf16[8,516,256]{2,1,0:T(8,128)(2,1)}), bf16[8,516,256]{2,1,0:T(8,128)(2,1)}, u32[]{:S(2)}, u32[]{:S(2)}) async-start(bf16[8,516,256]{2,1,0:T(8,128)(2,1)} %bitcast.95), calls=%async_computation.1 | async-start | bytes 4259840 | tf_op jit(solution)/shard_map/all_to_all | solution.py:238
  186.4 30.3 %copy-start.1 = (bf16[48,128,256]{2,1,0:T(8,128)(2,1)S(1)}, bf16[48,128,256]{2,1,0:T(8,128)(2,1)}, u32[]{:S(2)}) copy-start(bf16[48,128,256]{2,1,0:T(8,128)(2,1)} %param.27) | copy-start | bytes 9437188
  213.1 2.2 copy-start.3
Sparse Core Ops, SparseCore 0:
  10.8 83.0 all-gather.2

commit v3 on v2

--- a/solution.py
+++ b/solution.py
@@ -80,45 +80,39 @@
     model_index = lax.axis_index("fsdp")
 
     projection_piece = jnp.concatenate([query_weight, key_weight, value_weight], axis=1)
-    bundle_width = projection_piece.shape[1]
+    projection_weight = lax.all_gather(projection_piece, "dp", axis=0, tiled=True)
     out_size = out_weight.size
-    tail = jnp.concatenate([out_weight.reshape(-1), decode_tokens.reshape(-1)])
-    bundle = jnp.concatenate([projection_piece, tail.reshape(-1, bundle_width)], axis=0)
-    gathered = lax.all_gather(bundle, "dp", axis=0, tiled=False)
-    projection_weight = gathered[:, :weight_rows].reshape(-1, bundle_width)
-    gathered_tail = gathered[:, weight_rows:].reshape(dp_size, -1)
+    late_piece = jnp.concatenate([decode_tokens.reshape(-1), out_weight.reshape(-1)])
+    projection_weight, late_piece = lax.optimization_barrier((projection_weight, late_piece))
+    late = lax.all_gather(late_piece.reshape(-1, local_width), "dp", axis=0, tiled=False)
+    late = late.reshape(dp_size, -1)
+    decode_size = decode_tokens.size
+    all_decode = late[:, :decode_size].reshape(dp_size * decode_rows, -1)
     out_full = jnp.transpose(
-        gathered_tail[:, :out_size].reshape(dp_size, out_weight.shape[0], out_weight.shape[1]),
+        late[:, decode_size:].reshape(dp_size, out_weight.shape[0], out_weight.shape[1]),
         (1, 0, 2),
     ).reshape(out_weight.shape[0], -1)
-    all_decode = gathered_tail[:, out_size:].reshape(dp_size * decode_rows, -1)
-
-    tokens = jnp.concatenate([prefill_tokens, all_decode], axis=0)
-    normed = layer_norm(tokens)
-    raw = jnp.dot(normed, projection_weight, preferred_element_type=jnp.float32)
-    raw_queries = raw[:, :local_width]
-    raw_keys = raw[:, local_width : 2 * local_width]
-    raw_values = raw[:, 2 * local_width :]
+
+    def project(rows_in):
+        raw = jnp.dot(layer_norm(rows_in), projection_weight, preferred_element_type=jnp.float32)
+        return raw[:, :local_width], raw[:, local_width : 2 * local_width], raw[:, 2 * local_width :]
 
     cache_length = (page_counts - 1) * PAGE + last_fill
     first_page = jnp.cumsum(page_counts) - page_counts
     request_count = decode_request.shape[0]
     slot_numbers = jnp.arange(request_count, dtype=jnp.int32)
     slot_of_request = inverse_permutation(decode_request)
-    positions = jnp.concatenate(
-        [
-            prior_length[0] + jnp.arange(group_rows, dtype=jnp.int32),
-            jnp.take(cache_length, decode_request),
-        ]
-    )
-    queries = rotary(raw_queries, positions, HEAD).astype(jnp.bfloat16)
-    keys_new = rotary(raw_keys, positions, HEAD).astype(jnp.bfloat16)
-    values_new = raw_values.astype(jnp.bfloat16)
+    prefill_q, prefill_k, prefill_v = project(prefill_tokens)
+    prefill_positions = prior_length[0] + jnp.arange(group_rows, dtype=jnp.int32)
+    decode_positions = jnp.take(cache_length, decode_request)
+    group_queries = rotary(prefill_q, prefill_positions, HEAD).astype(jnp.bfloat16)
+    group_keys = rotary(prefill_k, prefill_positions, HEAD).astype(jnp.bfloat16)
+    group_values = prefill_v.astype(jnp.bfloat16)
 
     prior_slots = prior_keys.shape[1]
-    group_queries = queries[:group_rows].reshape(group_rows, head_count, HEAD)
-    group_keys = keys_new[:group_rows].reshape(group_rows, head_count, HEAD)
-    group_values = values_new[:group_rows].reshape(group_rows, head_count, HEAD)
+    group_queries = group_queries.reshape(group_rows, head_count, HEAD)
+    group_keys = group_keys.reshape(group_rows, head_count, HEAD)
+    group_values = group_values.reshape(group_rows, head_count, HEAD)
     stored_keys = prior_keys[0].reshape(prior_slots, head_count, HEAD)
     stored_values = prior_values[0].reshape(prior_slots, head_count, HEAD)
     prior_scores = (
@@ -157,11 +151,33 @@
         .astype(jnp.bfloat16)
     )
 
-    slot_queries = queries[group_rows:]
+    model_size = out_full.shape[1] // local_width
+    column_start = model_index * local_width
+
+    def send_shares(attended):
+        terms = jnp.dot(attended, out_full, preferred_element_type=jnp.float32).astype(jnp.bfloat16)
+        return jnp.transpose(terms.reshape(terms.shape[0], model_size, local_width), (1, 0, 2))
+
+    def exchange(shares):
+        return lax.all_to_all(shares, "fsdp", 0, 0, tiled=False)
+
+    def mixed(received, own_tokens):
+        branch = jnp.sum(received.astype(jnp.float32), axis=0)
+        residual = lax.dynamic_slice_in_dim(own_tokens, column_start, local_width, 1)
+        return (residual.astype(jnp.float32) + branch).astype(jnp.bfloat16)
+
+    prefill_shares, all_decode = lax.optimization_barrier(
+        (send_shares(prefill_attended), all_decode)
+    )
+    prefill_received = exchange(prefill_shares)
+    decode_q, decode_k, decode_v = project(all_decode)
+    slot_queries = rotary(decode_q, decode_positions, HEAD).astype(jnp.bfloat16)
+    slot_keys = rotary(decode_k, decode_positions, HEAD).astype(jnp.bfloat16)
+    slot_values = decode_v.astype(jnp.bfloat16)
     own_start = data_index * decode_rows
     own_queries = lax.dynamic_slice_in_dim(slot_queries, own_start, decode_rows, 0)
-    own_keys = lax.dynamic_slice_in_dim(keys_new[group_rows:], own_start, decode_rows, 0)
-    own_values = lax.dynamic_slice_in_dim(values_new[group_rows:], own_start, decode_rows, 0)
+    own_keys = lax.dynamic_slice_in_dim(slot_keys, own_start, decode_rows, 0)
+    own_values = lax.dynamic_slice_in_dim(slot_values, own_start, decode_rows, 0)
     pool_count = page_slots.shape[0]
     pool_local = pool_keys.shape[0]
     local_slots = data_index * pool_local + jnp.arange(pool_local, dtype=jnp.int32)
@@ -199,6 +215,7 @@
         member_weights.T, page_mix.reshape(pool_local, local_width), precision=lax.Precision.HIGHEST
     )
     partials = jnp.concatenate([slot_top, slot_total, slot_mix], axis=1)
+    partials, prefill_received = lax.optimization_barrier((partials, prefill_received))
     received = lax.all_to_all(
         partials.reshape(dp_size, decode_rows, -1), "dp", 0, 0, tiled=False
     )
@@ -228,17 +245,10 @@
         own_values.astype(jnp.float32), own_factor, HEAD
     )
     decode_attended = rescale(final_mix, 1.0 / final_total, HEAD).astype(jnp.bfloat16)
-    attended = jnp.concatenate([prefill_attended, decode_attended], axis=0)
-    own_tokens = jnp.concatenate([prefill_tokens, decode_tokens], axis=0)
-    residual = lax.dynamic_slice_in_dim(own_tokens, model_index * local_width, local_width, 1)
-    terms = jnp.dot(attended, out_full, preferred_element_type=jnp.float32).astype(jnp.bfloat16)
-    model_size = terms.shape[1] // local_width
-    shares = jnp.transpose(terms.reshape(terms.shape[0], model_size, local_width), (1, 0, 2))
-    branch = jnp.sum(
-        lax.all_to_all(shares, "fsdp", 0, 0, tiled=False).astype(jnp.float32), axis=0
-    )
-    result = (residual.astype(jnp.float32) + branch).astype(jnp.bfloat16)
-    return (result[:group_rows], result[group_rows:])
+    return (
+        mixed(prefill_received, prefill_tokens),
+        mixed(exchange(send_shares(decode_attended)), decode_tokens),
+    )
 
 
 def solution(mesh):

time: 225 us -> 278 us (1.24)
  waiting for transfers between devices: 88.7 us -> 146 us
  local copies, waits for them, and re-layouts: 58.9 us -> 47.2 us
  starting transfers between devices: 15.7 us -> 21.2 us
  matrix products: 20.1 us -> 23 us
    all_gather x1 -> x2, waiting for transfers between devices: 60.8 us -> 120 us  [the longest x1 61.4 us: per_device(): lax.all_gather(late_piece.reshape(-1, local_width), 'dp', axis=0, tiled=F...]
    slice x12 -> x6, local copies, waits for them, and re-layouts: 13.7 us -> 4.7 us  [the longest x2 1.64 us: project(): raw[:, 2 * local_width:]]
    all_to_all x1 -> x2, waiting for transfers between devices: 26.7 us -> 20.6 us  [exchange(): return lax.all_to_all(shares, 'fsdp', 0, 0, tiled=False)]
    all_to_all x1 -> x2, starting transfers between devices: 9.83 us -> 15.6 us  [exchange(): return lax.all_to_all(shares, 'fsdp', 0, 0, tiled=False)]
    dot_general x2 -> x4, matrix products: 6.38 us -> 11.2 us  [the longest x2 7.04 us: project(): jnp.dot(layer_norm(rows_in), projection_weight, preferred_element_type=jn...]
    all_to_all x1, waiting for transfers between devices: 1.17 us -> 5.69 us  [per_device(): lax.all_to_all(partials.reshape(dp_size, decode_rows, -1), 'dp', 0, 0, ti...]
    dot_general x1, matrix products: 3.98 us -> 0.72 us  [per_device(): jnp.einsum('qhd,khd->hqk', group_queries, group_keys, preferred_element_t...]
  transfers between devices with their start and end apart: 3 -> 5, of which waited for: 3 -> 5; matrix products, arithmetic and copies ran while one was open for 13% -> 17% of each run, Pallas kernels for 0% -> 0%
where the time goes in v3:
time: 278 us; the launch traced here: 276 us
  waiting for transfers between devices  146 us (53%)
  local copies, waits for them, and re-layouts  47.2 us (17%)
  other arithmetic  23.9 us (9%)
  matrix products  23 us (8%)
  starting transfers between devices  21.2 us (8%)
  between operations  15.2 us (5%)
    all_gather x1, waiting for transfers between devices, per_device(): lax.all_gather(late_piece.reshape(-1, local_width), 'dp', axis=0, tiled=F...  61.4 us
    all_gather x1, waiting for transfers between devices, per_device(): lax.all_gather(projection_piece, 'dp', axis=0, tiled=True)  58.1 us
    all_to_all x2, waiting for transfers between devices, exchange(): return lax.all_to_all(shares, 'fsdp', 0, 0, tiled=False)  20.6 us
    all_to_all x2, starting transfers between devices, exchange(): return lax.all_to_all(shares, 'fsdp', 0, 0, tiled=False)  15.6 us
    dot_general x2, matrix products, project(): jnp.dot(layer_norm(rows_in), projection_weight, preferred_element_type=jn...  7.04 us
    all_to_all x1, waiting for transfers between devices, per_device(): lax.all_to_all(partials.reshape(dp_size, decode_rows, -1), 'dp', 0, 0, ti...  5.69 us
    all_to_all x1, starting transfers between devices, per_device(): lax.all_to_all(partials.reshape(dp_size, decode_rows, -1), 'dp', 0, 0, ti...  5.57 us
  transfers between devices with their start and end apart: 5, of which 5 were waited for; matrix products, arithmetic and copies ran while one was open for 17% of the time, Pallas kernels for 0%

profile of v3, /device:TPU:1, one launch (start us, length us, event | category | flops | bytes accessed | tf_op | source)
XLA Modules:
  0.0 276.4 jit_solution(9007101533001358844)
XLA Ops:
  7.3 1.6 pad_maximum_fusion.2
  11.3 2.2 reshape_squeeze.6
  13.5 2.3 copy.82
  20.4 4.6 %copy.84 = bf16[48,128,256]{1,2,0:T(8,128)(2,1)} copy(bf16[48,128,256]{2,1,0:T(8,128)(2,1)} %param.26) | data formatting | bytes 6291456 | tf_op jit(solution)/shard_map/reshape | solution.py:194
  26.3 2.0 convert_reduce_fusion
  30.1 1.8 multiply_cosine_fusion
  31.9 58.1 %all-gather.3.cloned.1.call-done = bf16[2048,768]{1,0:T(8,128)(2,1)} async-done(((bf16[64,768]{1,0:T(8,128)(2,1)}), bf16[2048,768]{1,0:T(8,128)(2,1)}) %all-gather.3.cloned.1.call-update) | async-done | bytes 3145744 | tf_op jit(solution)/shard_map/all_gather | solution.py:83
  90.0 4.4 %fusion.13 = f32[512,768]{1,0:T(8,128)S(1)} fusion(bf16[2048,768]{1,0:T(8,128)(2,1)} %all-gather.3.cloned.1.call-done, bf16[512,2048]{1,0:T(8,128)(2,1)} %param.17, f32[512]{0:T(512)S(1)} %add_rsqrt_fusion, f32[512]{0:T(512)S(1)} %broadcast_multiply_fusion), kind=kOutput, calls=%fused_computation.25 | convolution fusion | flops 1614807040 | bytes 6819840 | tf_op jit(solution)/shard_map/dot_general | solution.py:97
  96.2 2.1 reshape.373
  98.3 2.1 reshape.374
  100.4 1.8 copy.83
  102.9 2.7 fusion.81
  108.9 2.1 fusion.1
  111.0 2.1 fusion.22
  114.6 61.4 %all-gather.5.cloned.1.call-done = bf16[32,96,256]{2,1,0:T(8,128)(2,1)} async-done(((bf16[1,96,256]{2,1,0:T(8,128)(2,1)}), bf16[32,96,256]{2,1,0:T(8,128)(2,1)}) %all-gather.5.cloned.1.call-update) | async-done | bytes 1572880 | tf_op jit(solution)/shard_map/all_gather | solution.py:87
  176.0 2.3 copy.93
  180.3 4.1 %reshape.377 = bf16[32,256,64]{2,1,0:T(8,128)(2,1)} reshape(bf16[32,16384]{1,0:T(8,128)(2,1)} %slice.97) | data formatting | bytes 2097152 | tf_op jit(solution)/shard_map/reshape | solution.py:92
  184.3 2.8 copy.63
  187.1 2.0 convolution_convert_fusion
  190.6 2.2 reshape.380
  195.3 2.7 fusion.37
  201.3 9.5 %all-to-all-start = ((bf16[8,512,256]{2,1,0:T(8,128)(2,1)}), bf16[8,512,256]{2,1,0:T(8,128)(2,1)}, u32[]{:S(2)}, u32[]{:S(2)}) async-start(bf16[8,512,256]{2,1,0:T(8,128)(2,1)} %bitcast.107), calls=%async_computation | async-start | bytes 4194304 | tf_op jit(solution)/shard_map/all_to_all | solution.py:162
  211.6 2.8 %fusion.52 = f32[48,2,1,128]{3,2,1,0:T(1,128)S(1)} fusion(bf16[48,128,2,128]{1,3,2,0:T(8,128)(2,1)} %bitcast.103, bf16[48,2,128,1]{2,1,0,3:T(2,128)(2,1)S(1)} %fusion.57), kind=kOutput, calls=%fused_computation.96 | convolution fusion | flops 3145728 | bytes 3219456 | tf_op jit(solution)/shard_map/phd,pkhd->phk/dot_general | solution.py:196
  216.4 2.5 fusion.10
  219.4 17.7 %all-to-all-done = bf16[8,512,256]{2,1,0:T(8,128)(2,1)} async-done(((bf16[8,512,256]{2,1,0:T(8,128)(2,1)}), bf16[8,512,256]{2,1,0:T(8,128)(2,1)}, u32[]{:S(2)}, u32[]{:S(2)}) %all-to-all-start) | async-done | bytes 2097184 | tf_op jit(solution)/shard_map/all_to_all | solution.py:162
  237.9 5.6 %all-to-all-start.1 = ((f32[32,4,260]{2,1,0:T(4,128)}), f32[32,4,260]{2,1,0:T(4,128)S(1)}, u32[]{:S(2)}, u32[]{:S(2)}) async-start(f32[32,4,260]{2,1,0:T(4,128)} %reshape.385), calls=%async_computation.1 | async-start | bytes 393216 | tf_op jit(solution)/shard_map/all_to_all | solution.py:219
  244.5 2.7 convert_reduce_fusion.1
  247.2 5.7 %all-to-all-done.1 = f32[32,4,260]{2,1,0:T(4,128)S(1)} async-done(((f32[32,4,260]{2,1,0:T(4,128)}), f32[32,4,260]{2,1,0:T(4,128)S(1)}, u32[]{:S(2)}, u32[]{:S(2)}) %all-to-all-start.1) | async-done | bytes 133152 | tf_op jit(solution)/shard_map/all_to_all | solution.py:219
  255.3 2.2 convolution_convert_fusion.1
  257.5 6.1 %all-to-all-start.2 = ((bf16[8,4,256]{2,1,0:T(4,128)(2,1)}), bf16[8,4,256]{2,1,0:T(4,128)(2,1)S(1)}, u32[]{:S(2)}, u32[]{:S(2)}) async-start(bf16[8,4,256]{2,1,0:T(4,128)(2,1)} %bitcast.18), calls=%async_computation.2 | async-start | bytes 32768 | tf_op jit(solution)/shard_map/all_to_all | solution.py:162
  263.6 1.9 add_convert_fusion
  265.5 2.8 %all-to-all-done.2 = bf16[8,4,256]{2,1,0:T(4,128)(2,1)S(1)} async-done(((bf16[8,4,256]{2,1,0:T(4,128)(2,1)}), bf16[8,4,256]{2,1,0:T(4,128)(2,1)S(1)}, u32[]{:S(2)}, u32[]{:S(2)}) %all-to-all-start.2) | async-done | bytes 16416 | tf_op jit(solution)/shard_map/all_to_all | solution.py:162
  (126 shorter events, 34.4 us)
Async XLA Ops:
  7.2 209.2 %copy-start = (bf16[48,128,256]{2,1,0:T(8,128)(2,1)S(1)}, bf16[48,128,256]{2,1,0:T(8,128)(2,1)}, u32[]{:S(2)}) copy-start(bf16[48,128,256]{2,1,0:T(8,128)(2,1)} %param.27) | copy-start | bytes 9437188
  7.2 8.6 %copy-start.13 = (s32[128]{0:T(128)S(1)}, s32[128]{0:T(128)}, u32[]{:S(2)}) copy-start(s32[128]{0:T(128)} %param.29) | copy-start | bytes 1540
  7.2 9.0 %copy-start.11 = (s32[1536]{0:T(1024)S(1)}, s32[1536]{0:T(1024)}, u32[]{:S(2)}) copy-start(s32[1536]{0:T(1024)} %param.28) | copy-start | bytes 18436
  7.2 9.2 %copy-start.14 = (s32[128]{0:T(128)S(1)}, s32[128]{0:T(128)}, u32[]{:S(2)}) copy-start(s32[128]{0:T(128)} %param.30) | copy-start | bytes 1540
  7.2 11.0 %copy-start.15 = (s32[128]{0:T(128)S(1)}, s32[128]{0:T(128)}, u32[]{:S(2)}) copy-start(s32[128]{0:T(128)} %param.31) | copy-start | bytes 1540
  7.2 82.8 %all-gather.3.cloned.1.call-start = ((), (), s32[]{:S(2)}) async-start(), calls=%async_computation.3 | async-start | bytes 3244032 | tf_op jit(solution)/shard_map/all_gather | solution.py:83
  8.9 167.1 %all-gather.5.cloned.1.call-start = ((), (), s32[]{:S(2)}) async-start(), calls=%async_computation.4 | async-start | bytes 1622016 | tf_op jit(solution)/shard_map/all_gather | solution.py:87
  25.0 3.3 %copy-start.1 = (bf16[512,2048]{1,0:T(8,128)(2,1)S(1)}, bf16[512,2048]{1,0:T(8,128)(2,1)}, u32[]{:S(2)}) copy-start(bf16[512,2048]{1,0:T(8,128)(2,1)} %param.17) | copy-start | bytes 6291460
  25.6 68.8 %copy-start.9 = (s32[48]{0:T(128)}, s32[48]{0:T(128)S(1)}, u32[]{:S(2)}) copy-start(s32[48]{0:T(128)S(1)} %get-tuple-element.21) | copy-start | bytes 580
  102.9 2.7 copy-start.4
  102.9 2.7 copy-start.5
  105.6 1.2 copy-start.2
  108.9 2.1 copy-start.6
  111.0 2.1 copy-start.7
  180.2 6.8 %copy-start.8 = (bf16[512,2,128]{0,2,1:T(8,128)(2,1)S(1)}, bf16[512,2,128]{0,2,1:T(8,128)(2,1)}, u32[]{:S(2)}) copy-start(bf16[512,2,128]{0,2,1:T(8,128)(2,1)} %fusion.27) | copy-start | bytes 786436
  198.0 0.7 copy-start.3
  201.3 14.2 %copy-start.12 = (pred[48]{0:T(512)(128)(4,1)S(1)}, pred[48]{0:T(512)(128)(4,1)}, u32[]{:S(2)}) copy-start(pred[48]{0:T(512)(128)(4,1)} %get-tuple-element.20) | copy-start | bytes 148
  201.3 14.7 %copy-start.10 = (s32[48]{0:T(128)S(1)}, s32[48]{0:T(128)}, u32[]{:S(2)}) copy-start(s32[48]{0:T(128)} %copy-done.9) | copy-start | bytes 580
  201.3 35.8 %all-to-all-start = ((bf16[8,512,256]{2,1,0:T(8,128)(2,1)}), bf16[8,512,256]{2,1,0:T(8,128)(2,1)}, u32[]{:S(2)}, u32[]{:S(2)}) async-start(bf16[8,512,256]{2,1,0:T(8,128)(2,1)} %bitcast.107), calls=%async_computation | async-start | bytes 4194304 | tf_op jit(solution)/shard_map/all_to_all | solution.py:162
  237.9 15.0 %all-to-all-start.1 = ((f32[32,4,260]{2,1,0:T(4,128)}), f32[32,4,260]{2,1,0:T(4,128)S(1)}, u32[]{:S(2)}, u32[]{:S(2)}) async-start(f32[32,4,260]{2,1,0:T(4,128)} %reshape.385), calls=%async_computation.1 | async-start | bytes 393216 | tf_op jit(solution)/shard_map/all_to_all | solution.py:219
  257.5 10.8 %all-to-all-start.2 = ((bf16[8,4,256]{2,1,0:T(4,128)(2,1)}), bf16[8,4,256]{2,1,0:T(4,128)(2,1)S(1)}, u32[]{:S(2)}, u32[]{:S(2)}) async-start(bf16[8,4,256]{2,1,0:T(4,128)(2,1)} %bitcast.18), calls=%async_computation.2 | async-start | bytes 32768 | tf_op jit(solution)/shard_map/all_to_all | solution.py:162
Sparse Core Ops, SparseCore 0:
  10.6 79.3 all-gather.2
  103.0 72.9 all-gather.4

commit v4 on v3

--- a/solution.py
+++ b/solution.py
@@ -79,23 +79,25 @@
     data_index = lax.axis_index("dp")
     model_index = lax.axis_index("fsdp")
 
-    projection_piece = jnp.concatenate([query_weight, key_weight, value_weight], axis=1)
-    projection_weight = lax.all_gather(projection_piece, "dp", axis=0, tiled=True)
-    out_size = out_weight.size
-    late_piece = jnp.concatenate([decode_tokens.reshape(-1), out_weight.reshape(-1)])
-    projection_weight, late_piece = lax.optimization_barrier((projection_weight, late_piece))
-    late = lax.all_gather(late_piece.reshape(-1, local_width), "dp", axis=0, tiled=False)
-    late = late.reshape(dp_size, -1)
+    decode_piece = decode_tokens.reshape(-1, local_width)
+    decode_piece = jnp.pad(decode_piece, ((0, weight_rows - decode_piece.shape[0]), (0, 0)))
+    bundle = jnp.stack(
+        [query_weight, key_weight, value_weight, jnp.transpose(out_weight), decode_piece]
+    )
+    gathered = lax.all_gather(bundle, "dp", axis=1, tiled=False)
+    projection_weights = [gathered[p].reshape(-1, local_width) for p in range(3)]
+    out_columns = gathered[3].reshape(-1, local_width)
     decode_size = decode_tokens.size
-    all_decode = late[:, :decode_size].reshape(dp_size * decode_rows, -1)
-    out_full = jnp.transpose(
-        late[:, decode_size:].reshape(dp_size, out_weight.shape[0], out_weight.shape[1]),
-        (1, 0, 2),
-    ).reshape(out_weight.shape[0], -1)
+    all_decode = (
+        gathered[4].reshape(dp_size, -1)[:, :decode_size].reshape(dp_size * decode_rows, -1)
+    )
 
     def project(rows_in):
-        raw = jnp.dot(layer_norm(rows_in), projection_weight, preferred_element_type=jnp.float32)
-        return raw[:, :local_width], raw[:, local_width : 2 * local_width], raw[:, 2 * local_width :]
+        normed = layer_norm(rows_in)
+        return tuple(
+            jnp.dot(normed, weight, preferred_element_type=jnp.float32)
+            for weight in projection_weights
+        )
 
     cache_length = (page_counts - 1) * PAGE + last_fill
     first_page = jnp.cumsum(page_counts) - page_counts
@@ -151,11 +153,13 @@
         .astype(jnp.bfloat16)
     )
 
-    model_size = out_full.shape[1] // local_width
+    model_size = out_columns.shape[0] // local_width
     column_start = model_index * local_width
 
     def send_shares(attended):
-        terms = jnp.dot(attended, out_full, preferred_element_type=jnp.float32).astype(jnp.bfloat16)
+        terms = lax.dot_general(
+            attended, out_columns, (((1,), (1,)), ((), ())), preferred_element_type=jnp.float32
+        ).astype(jnp.bfloat16)
         return jnp.transpose(terms.reshape(terms.shape[0], model_size, local_width), (1, 0, 2))
 
     def exchange(shares):

time: 278 us -> 212 us (0.76)
  waiting for transfers between devices: 146 us -> 88.3 us
  local copies, waits for them, and re-layouts: 47.2 us -> 38.7 us
  matrix products: 23 us -> 27 us
    all_gather x2 -> x1, waiting for transfers between devices: 120 us -> 62.7 us  [per_device(): gathered = lax.all_gather(bundle, 'dp', axis=1, tiled=False)]
    reshape x10 -> x2, local copies, waits for them, and re-layouts: 12.6 us -> 3.03 us  [the longest x1 2.27 us: per_device(): gathered[4].reshape(dp_size, -1)[:, :decode_size]]
    dot_general x0 -> x3, local copies, waits for them, and re-layouts: none -> 4.67 us  [the longest x2 4.58 us: project(): jnp.dot(normed, weight, preferred_element_type=jnp.float32)]
    dot_general x4 -> x8, matrix products: 11.2 us -> 15.9 us  [the longest x6 11.7 us: project(): jnp.dot(normed, weight, preferred_element_type=jnp.float32)]
    slice x7 -> x2, local copies, waits for them, and re-layouts: 7.41 us -> 5.44 us  [per_device(): gathered[4].reshape(dp_size, -1)[:, :decode_size]]
  transfers between devices with their start and end apart: 5 -> 4, of which waited for: 5 -> 4; matrix products, arithmetic and copies ran while one was open for 17% -> 18% of each run, Pallas kernels for 0% -> 0%
where the time goes in v4:
time: 212 us; the launch traced here: 210 us
  waiting for transfers between devices  88.3 us (42%)
  local copies, waits for them, and re-layouts  38.7 us (18%)
  matrix products  27 us (13%)
  other arithmetic  21.8 us (10%)
  starting transfers between devices  19.5 us (9%)
  between operations  15.2 us (7%)
    all_gather x1, waiting for transfers between devices, per_device(): gathered = lax.all_gather(bundle, 'dp', axis=1, tiled=False)  62.7 us
    all_to_all x2, waiting for transfers between devices, exchange(): return lax.all_to_all(shares, 'fsdp', 0, 0, tiled=False)  21.5 us
    all_to_all x2, starting transfers between devices, exchange(): return lax.all_to_all(shares, 'fsdp', 0, 0, tiled=False)  14.1 us
    dot_general x6, matrix products, project(): jnp.dot(normed, weight, preferred_element_type=jnp.float32)  11.7 us
    slice x2, local copies, waits for them, and re-layouts, per_device(): gathered[4].reshape(dp_size, -1)[:, :decode_size]  5.44 us
    all_to_all x1, starting transfers between devices, per_device(): lax.all_to_all(partials.reshape(dp_size, decode_rows, -1), 'dp', 0, 0, ti...  5.29 us
    reshape x1, local copies, waits for them, and re-layouts, per_device(): page_keys = pool_keys.reshape(pool_local, PAGE, head_count, HEAD)  4.67 us
    dot_general x2, local copies, waits for them, and re-layouts, project(): jnp.dot(normed, weight, preferred_element_type=jnp.float32)  4.58 us
  transfers between devices with their start and end apart: 4, of which 4 were waited for; matrix products, arithmetic and copies ran while one was open for 18% of the time, Pallas kernels for 0%

profile of v4, /device:TPU:1, one launch (start us, length us, event | category | flops | bytes accessed | tf_op | source)
XLA Modules:
  0.0 210.4 jit_solution(8586548980546325630)
XLA Ops:
  12.6 2.1 %reshape_squeeze.22 = bf16[2048,2,128]{2,1,0:T(2,128)(2,1)} reshape(bf16[1,2048,256]{2,1,0:T(8,128)(2,1)} %param.23) | data formatting | bytes 2097152 | tf_op jit(solution)/shard_map/reshape;squeeze | solution.py:118
  14.7 2.3 %copy.84 = bf16[1,2048,256]{1,2,0:T(8,128)(2,1)} copy(bf16[1,2048,256]{2,1,0:T(8,128)(2,1)} %param.24) | data formatting | bytes 2097152 | tf_op jit(solution)/shard_map/reshape;squeeze | solution.py:119
  21.5 4.7 %copy.85 = bf16[48,128,256]{1,2,0:T(8,128)(2,1)} copy(bf16[48,128,256]{2,1,0:T(8,128)(2,1)} %param.26) | data formatting | bytes 6291456 | tf_op jit(solution)/shard_map/reshape | solution.py:198
  27.5 2.0 convert_reduce_fusion
  32.9 1.9 fusion.6
  34.9 62.7 %all-gather.3.cloned.1.call-done = bf16[5,2048,256]{2,1,0:T(8,128)(2,1)} async-done(((bf16[5,64,256]{2,1,0:T(8,128)(2,1)}), bf16[5,2048,256]{2,1,0:T(8,128)(2,1)}) %all-gather.3.cloned.1.call-update) | async-done | bytes 5242896 | tf_op jit(solution)/shard_map/all_gather | solution.py:87
  97.6 3.6 %fusion.84 = (bf16[1,2048,256]{2,1,0:T(8,128)(2,1)}, bf16[256,2048]{0,1:T(8,128)(2,1)}, bf16[256,2048]{0,1:T(8,128)(2,1)}) fusion(bf16[5,2048,256]{2,1,0:T(8,128)(2,1)} %all-gather.3.cloned.1.call-done), kind=kLoop, calls=%fused_computation.172 | loop fusion | bytes 6291456 | tf_op jit(solution)/shard_map/slice | solution.py:92
  101.2 2.3 %copy.56 = bf16[256,2048]{1,0:T(8,128)(2,1)} copy(bf16[256,2048]{0,1:T(8,128)(2,1)} %get-tuple-element.19) | data formatting | bytes 2097152 | tf_op jit(solution)/shard_map/dot_general | solution.py:98
  103.5 2.3 %copy.53 = bf16[256,2048]{1,0:T(8,128)(2,1)} copy(bf16[256,2048]{0,1:T(8,128)(2,1)} %get-tuple-element.20) | data formatting | bytes 2097152 | tf_op jit(solution)/shard_map/dot_general | solution.py:98
  105.8 2.8 %fusion.13 = f32[512,2,128]{0,2,1:T(8,128)S(1)} fusion(bf16[2,128,2048]{2,1,0:T(8,128)(2,1)} %bitcast.140, bf16[512,2048]{1,0:T(8,128)(2,1)} %fusion.6), kind=kOutput, calls=%fused_computation.26 | convolution fusion | flops 536870912 | bytes 3670016 | tf_op jit(solution)/shard_map/dot_general | solution.py:98
  109.8 1.7 fusion
  112.7 2.1 fusion.1
  114.8 2.0 fusion.22
  116.9 2.0 convolution_convert_fusion.2
  119.6 2.0 convolution_convert_fusion
  123.1 2.3 %reshape_squeeze.27 = bf16[32,16384]{1,0:T(8,128)(2,1)} reshape(bf16[1,2048,256]{2,1,0:T(8,128)(2,1)} %get-tuple-element.18) | data formatting | bytes 2097152 | tf_op jit(solution)/shard_map/reshape;squeeze | solution.py:92
  125.5 1.9 slice.94
  127.4 2.3 %reshape.358 = bf16[128,2048]{1,0:T(8,128)(2,1)} reshape(bf16[32,8192]{1,0:T(8,128)(2,1)} %slice.94) | data formatting | bytes 1048576 | tf_op jit(solution)/shard_map/reshape | solution.py:92
  132.2 1.9 fusion.40
  134.1 1.9 fusion.38
  137.0 8.0 %all-to-all-start = ((bf16[8,512,256]{2,1,0:T(8,128)(2,1)}), bf16[8,512,256]{2,1,0:T(8,128)(2,1)}, u32[]{:S(2)}, u32[]{:S(2)}) async-start(bf16[8,512,256]{2,1,0:T(8,128)(2,1)} %bitcast.137), calls=%async_computation | async-start | bytes 4194304 | tf_op jit(solution)/shard_map/all_to_all | solution.py:166
  145.2 2.8 %fusion.54 = f32[48,2,1,128]{3,2,1,0:T(1,128)S(1)} fusion(bf16[48,128,2,128]{1,3,2,0:T(8,128)(2,1)} %bitcast.136, bf16[48,2,128,1]{2,1,0,3:T(2,128)(2,1)S(1)} %fusion.59), kind=kOutput, calls=%fused_computation.99 | convolution fusion | flops 3145728 | bytes 3219456 | tf_op jit(solution)/shard_map/phd,pkhd->phk/dot_general | solution.py:200
  149.7 2.5 %fusion.10 = f32[48,2,1,128]{3,2,1,0:T(1,128)S(1)} fusion(f32[48,2,128,1]{2,0,1,3:T(8,128)S(1)} %get-tuple-element.34, bf16[48,128,256]{2,1,0:T(8,128)(2,1)S(1)} %copy-done), kind=kOutput, calls=%fused_computation.20 | convolution fusion | flops 18874368 | bytes 3244032 | tf_op jit(solution)/shard_map/phk,pkhd->phd/dot_general | solution.py:215
  152.7 18.7 %all-to-all-done = bf16[8,512,256]{2,1,0:T(8,128)(2,1)} async-done(((bf16[8,512,256]{2,1,0:T(8,128)(2,1)}), bf16[8,512,256]{2,1,0:T(8,128)(2,1)}, u32[]{:S(2)}, u32[]{:S(2)}) %all-to-all-start) | async-done | bytes 2097184 | tf_op jit(solution)/shard_map/all_to_all | solution.py:166
  172.2 5.3 %all-to-all-start.1 = ((f32[32,4,260]{2,1,0:T(4,128)}), f32[32,4,260]{2,1,0:T(4,128)S(1)}, u32[]{:S(2)}, u32[]{:S(2)}) async-start(f32[32,4,260]{2,1,0:T(4,128)} %reshape.362), calls=%async_computation.1 | async-start | bytes 393216 | tf_op jit(solution)/shard_map/all_to_all | solution.py:223
  177.5 2.4 %fusion.37 = bf16[128,256]{1,0:T(8,128)(2,1)} fusion(bf16[5,2048,256]{2,1,0:T(8,128)(2,1)} %all-gather.3.cloned.1.call-done, bf16[128,2048]{1,0:T(8,128)(2,1)} %reshape.358, f32[128]{0:T(128)} %copy-done.17, f32[128]{0:T(128)} %copy-done.15), kind=kOutput, calls=%fused_computation.58 | convolution fusion | flops 135266304 | bytes 1639424 | tf_op jit(solution)/shard_map/dot_general | solution.py:98
  180.1 2.7 %convert_reduce_fusion.1 = f32[512,256]{1,0:T(8,128)} fusion(bf16[8,512,256]{2,1,0:T(8,128)(2,1)} %all-to-all-done), kind=kLoop, calls=%fused_computation.17 | loop fusion | flops 1966080 | bytes 2621440 | tf_op jit(solution)/shard_map/reduce_sum | solution.py:169
  182.8 4.1 %all-to-all-done.1 = f32[32,4,260]{2,1,0:T(4,128)S(1)} async-done(((f32[32,4,260]{2,1,0:T(4,128)}), f32[32,4,260]{2,1,0:T(4,128)S(1)}, u32[]{:S(2)}, u32[]{:S(2)}) %all-to-all-start.1) | async-done | bytes 133152 | tf_op jit(solution)/shard_map/all_to_all | solution.py:223
  189.3 2.2 %convolution_convert_fusion.1 = bf16[4,2048]{1,0:T(4,128)(2,1)} fusion(bf16[5,2048,256]{2,1,0:T(8,128)(2,1)} %all-gather.3.cloned.1.call-done, f32[1,4,2,128]{3,2,1,0:T(2,128)S(1)} %broadcast_bitcast_fusion, f32[1,4,2,128]{3,2,1,0:T(2,128)S(1)} %broadcast_bitcast_fusion.1, f32[4,256]{1,0:T(4,128)S(1)} %fusion.46, ...), kind=kOutput, calls=%fused_computation.24 | convolution fusion | flops 4208640 | bytes 1083396 | tf_op jit(solution)/shard_map/dot_general | solution.py:160
  191.5 6.1 %all-to-all-start.2 = ((bf16[8,4,256]{2,1,0:T(4,128)(2,1)}), bf16[8,4,256]{2,1,0:T(4,128)(2,1)S(1)}, u32[]{:S(2)}, u32[]{:S(2)}) async-start(bf16[8,4,256]{2,1,0:T(4,128)(2,1)} %bitcast.36), calls=%async_computation.2 | async-start | bytes 32768 | tf_op jit(solution)/shard_map/all_to_all | solution.py:166
  197.6 1.9 add_convert_fusion
  199.5 2.8 %all-to-all-done.2 = bf16[8,4,256]{2,1,0:T(4,128)(2,1)S(1)} async-done(((bf16[8,4,256]{2,1,0:T(4,128)(2,1)}), bf16[8,4,256]{2,1,0:T(4,128)(2,1)S(1)}, u32[]{:S(2)}, u32[]{:S(2)}) %all-to-all-start.2) | async-done | bytes 16416 | tf_op jit(solution)/shard_map/all_to_all | solution.py:166
  (117 shorter events, 29.0 us)
Async XLA Ops:
  7.2 142.5 %copy-start = (bf16[48,128,256]{2,1,0:T(8,128)(2,1)S(1)}, bf16[48,128,256]{2,1,0:T(8,128)(2,1)}, u32[]{:S(2)}) copy-start(bf16[48,128,256]{2,1,0:T(8,128)(2,1)} %param.27) | copy-start | bytes 9437188
  7.2 9.8 %copy-start.13 = (s32[128]{0:T(128)S(1)}, s32[128]{0:T(128)}, u32[]{:S(2)}) copy-start(s32[128]{0:T(128)} %param.29) | copy-start | bytes 1540
  7.2 10.2 %copy-start.11 = (s32[1536]{0:T(1024)S(1)}, s32[1536]{0:T(1024)}, u32[]{:S(2)}) copy-start(s32[1536]{0:T(1024)} %param.28) | copy-start | bytes 18436
  7.2 10.4 %copy-start.14 = (s32[128]{0:T(128)S(1)}, s32[128]{0:T(128)}, u32[]{:S(2)}) copy-start(s32[128]{0:T(128)} %param.30) | copy-start | bytes 1540
  7.2 12.2 %copy-start.16 = (s32[128]{0:T(128)S(1)}, s32[128]{0:T(128)}, u32[]{:S(2)}) copy-start(s32[128]{0:T(128)} %param.31) | copy-start | bytes 1540
  7.2 90.4 %all-gather.3.cloned.1.call-start = ((), (), s32[]{:S(2)}) async-start(), calls=%async_computation.3 | async-start | bytes 5406720 | tf_op jit(solution)/shard_map/all_gather | solution.py:87
  11.2 0.7 copy-start.7
  26.2 3.3 %copy-start.1 = (bf16[512,2048]{1,0:T(8,128)(2,1)S(1)}, bf16[512,2048]{1,0:T(8,128)(2,1)}, u32[]{:S(2)}) copy-start(bf16[512,2048]{1,0:T(8,128)(2,1)} %param.17) | copy-start | bytes 6291460
  105.8 2.8 %copy-start.3 = (bf16[512,2048]{1,0:T(8,128)(2,1)S(1)}, bf16[512,2048]{1,0:T(8,128)(2,1)}, u32[]{:S(2)}) copy-start(bf16[512,2048]{1,0:T(8,128)(2,1)} %fusion.6) | copy-start | bytes 6291460
  105.8 2.8 %copy-start.5 = (bf16[256,2048]{1,0:T(8,128)(2,1)S(1)}, bf16[256,2048]{1,0:T(8,128)(2,1)}, u32[]{:S(2)}) copy-start(bf16[256,2048]{1,0:T(8,128)(2,1)} %copy.53) | copy-start | bytes 3145732
  108.5 0.9 copy-start.6
  108.6 1.2 copy-start.2
  112.7 2.1 copy-start.4
  127.4 8.7 %copy-start.8 = (f32[128,64]{0,1:T(8,128)S(1)}, f32[128,64]{0,1:T(8,128)}, u32[]{:S(2)}) copy-start(f32[128,64]{0,1:T(8,128)} %get-tuple-element.37) | copy-start | bytes 98308
  127.4 8.7 %copy-start.9 = (f32[128,64]{0,1:T(8,128)S(1)}, f32[128,64]{0,1:T(8,128)}, u32[]{:S(2)}) copy-start(f32[128,64]{0,1:T(8,128)} %get-tuple-element.38) | copy-start | bytes 98308
  130.8 5.2 %copy-start.15 = (f32[128]{0:T(128)}, f32[128]{0:T(128)S(1)}, u32[]{:S(2)}) copy-start(f32[128]{0:T(128)S(1)} %broadcast_multiply_fusion.1) | copy-start | bytes 1540
  132.2 3.8 %copy-start.17 = (f32[128]{0:T(128)}, f32[128]{0:T(128)S(1)}, u32[]{:S(2)}) copy-start(f32[128]{0:T(128)S(1)} %add_rsqrt_fusion.1) | copy-start | bytes 1540
  134.1 11.0 %copy-start.12 = (pred[48]{0:T(512)(128)(4,1)S(1)}, pred[48]{0:T(512)(128)(4,1)}, u32[]{:S(2)}) copy-start(pred[48]{0:T(512)(128)(4,1)} %get-tuple-element.16) | copy-start | bytes 148
  137.0 11.1 %copy-start.10 = (pred[48,128]{1,0:T(8,128)(4,1)S(1)}, pred[48,128]{1,0:T(8,128)(4,1)}, u32[]{:S(2)}) copy-start(pred[48,128]{1,0:T(8,128)(4,1)} %iota_compare_fusion.2) | copy-start | bytes 18436
  137.0 34.4 %all-to-all-start = ((bf16[8,512,256]{2,1,0:T(8,128)(2,1)}), bf16[8,512,256]{2,1,0:T(8,128)(2,1)}, u32[]{:S(2)}, u32[]{:S(2)}) async-start(bf16[8,512,256]{2,1,0:T(8,128)(2,1)} %bitcast.137), calls=%async_computation | async-start | bytes 4194304 | tf_op jit(solution)/shard_map/all_to_all | solution.py:166
  172.2 14.7 %all-to-all-start.1 = ((f32[32,4,260]{2,1,0:T(4,128)}), f32[32,4,260]{2,1,0:T(4,128)S(1)}, u32[]{:S(2)}, u32[]{:S(2)}) async-start(f32[32,4,260]{2,1,0:T(4,128)} %reshape.362), calls=%async_computation.1 | async-start | bytes 393216 | tf_op jit(solution)/shard_map/all_to_all | solution.py:223
  191.5 10.8 %all-to-all-start.2 = ((bf16[8,4,256]{2,1,0:T(4,128)(2,1)}), bf16[8,4,256]{2,1,0:T(4,128)(2,1)S(1)}, u32[]{:S(2)}, u32[]{:S(2)}) async-start(bf16[8,4,256]{2,1,0:T(4,128)(2,1)} %bitcast.36), calls=%async_computation.2 | async-start | bytes 32768 | tf_op jit(solution)/shard_map/all_to_all | solution.py:166
Sparse Core Ops, SparseCore 0:
  12.0 85.5 all-gather.2

commit v5 on v4

--- a/solution.py
+++ b/solution.py
@@ -3,7 +3,7 @@
 import jax
 import jax.numpy as jnp
 from jax import lax
-from jax.sharding import PartitionSpec as P
+from jax.sharding import Mesh, PartitionSpec as P
 
 HEAD = 128
 PAGE = 128
@@ -12,6 +12,7 @@
 EPSILON = 1e-05
 ROPE_BASE = 10000.0
 NEG_FILL = -1e30
+DP = ("dy", "dz")
 
 
 def layer_norm(rows_in):
@@ -76,7 +77,7 @@
     local_width = query_weight.shape[1]
     head_count = local_width // HEAD
     score_scale = HEAD ** (-0.5)
-    data_index = lax.axis_index("dp")
+    data_index = lax.axis_index(DP)
     model_index = lax.axis_index("fsdp")
 
     decode_piece = decode_tokens.reshape(-1, local_width)
@@ -84,9 +85,12 @@
     bundle = jnp.stack(
         [query_weight, key_weight, value_weight, jnp.transpose(out_weight), decode_piece]
     )
-    gathered = lax.all_gather(bundle, "dp", axis=1, tiled=False)
-    projection_weights = [gathered[p].reshape(-1, local_width) for p in range(3)]
-    out_columns = gathered[3].reshape(-1, local_width)
+    across_y = lax.all_gather(bundle, "dy", axis=1, tiled=False)
+    gathered = lax.all_gather(across_y, "dz", axis=2, tiled=False).reshape(
+        bundle.shape[0], dp_size * weight_rows, local_width
+    )
+    projection_weights = [gathered[p] for p in range(3)]
+    out_columns = gathered[3]
     decode_size = decode_tokens.size
     all_decode = (
         gathered[4].reshape(dp_size, -1)[:, :decode_size].reshape(dp_size * decode_rows, -1)
@@ -221,7 +225,7 @@
     partials = jnp.concatenate([slot_top, slot_total, slot_mix], axis=1)
     partials, prefill_received = lax.optimization_barrier((partials, prefill_received))
     received = lax.all_to_all(
-        partials.reshape(dp_size, decode_rows, -1), "dp", 0, 0, tiled=False
+        partials.reshape(dp_size, decode_rows, -1), DP, 0, 0, tiled=False
     )
     source_top = received[:, :, :head_count]
     source_total = received[:, :, head_count : 2 * head_count]
@@ -256,27 +260,31 @@
 
 
 def solution(mesh):
+    dp_size = mesh.shape["dp"]
+    split_mesh = Mesh(
+        mesh.devices.reshape(4, dp_size // 4, mesh.shape["fsdp"]), ("dy", "dz", "fsdp")
+    )
     in_specs = (
-        P("dp", None),
-        P("dp", None),
-        P("dp", "fsdp"),
-        P("dp", "fsdp"),
-        P("dp", "fsdp"),
-        P("fsdp", "dp"),
-        P("dp", None, "fsdp"),
-        P("dp", None, "fsdp"),
-        P("dp"),
-        P("dp", None, "fsdp"),
-        P("dp", None, "fsdp"),
-        P(),
-        P(),
-        P(),
-        P(),
-    )
-    out_specs = (P("dp", "fsdp"), P("dp", "fsdp"))
+        P(DP, None),
+        P(DP, None),
+        P(DP, "fsdp"),
+        P(DP, "fsdp"),
+        P(DP, "fsdp"),
+        P("fsdp", DP),
+        P(DP, None, "fsdp"),
+        P(DP, None, "fsdp"),
+        P(DP),
+        P(DP, None, "fsdp"),
+        P(DP, None, "fsdp"),
+        P(),
+        P(),
+        P(),
+        P(),
+    )
+    out_specs = (P(DP, "fsdp"), P(DP, "fsdp"))
     return jax.shard_map(
-        functools.partial(per_device, dp_size=mesh.shape["dp"]),
-        mesh=mesh,
+        functools.partial(per_device, dp_size=dp_size),
+        mesh=split_mesh,
         in_specs=in_specs,
         out_specs=out_specs,
         check_vma=False,

time: 212 us -> 206 us (0.972)
  waiting for transfers between devices: 88.3 us -> 71.8 us
  blocking collectives: 0 us -> 13.3 us
  matrix products: 27 us -> 24.6 us
    all_gather x1, waiting for transfers between devices: 62.7 us -> 46.2 us  [per_device(): lax.all_gather(across_y, 'dz', axis=2, tiled=False)]
    all_gather x0 -> x1, blocking collectives: none -> 13.3 us  [per_device(): across_y = lax.all_gather(bundle, 'dy', axis=1, tiled=False)]
    dot_general x2 -> x0, local copies, waits for them, and re-layouts: 4.58 us -> none  [project(): jnp.dot(normed, weight, preferred_element_type=jnp.float32)]
    squeeze x0 -> x2, local copies, waits for them, and re-layouts: none -> 4.56 us  [per_device(): projection_weights = [gathered[p] for p in range(3)]]
    all_to_all x2, starting transfers between devices: 14.1 us -> 11.2 us  [exchange(): return lax.all_to_all(shares, 'fsdp', 0, 0, tiled=False)]
    unnamed x43 -> x45, local copies, waits for them, and re-layouts: 4.45 us -> 4.22 us
where the time goes in v5:
time: 206 us; the launch traced here: 205 us
  waiting for transfers between devices  71.8 us (35%)
  local copies, waits for them, and re-layouts  39.7 us (19%)
  matrix products  24.6 us (12%)
  other arithmetic  21.9 us (11%)
  starting transfers between devices  18.1 us (9%)
  between operations  15.2 us (7%)
  blocking collectives  13.3 us (6%)
    all_gather x1, waiting for transfers between devices, per_device(): lax.all_gather(across_y, 'dz', axis=2, tiled=False)  46.2 us
    all_to_all x2, waiting for transfers between devices, exchange(): return lax.all_to_all(shares, 'fsdp', 0, 0, tiled=False)  21.5 us
    all_gather x1, blocking collectives, per_device(): across_y = lax.all_gather(bundle, 'dy', axis=1, tiled=False)  13.3 us
    all_to_all x2, starting transfers between devices, exchange(): return lax.all_to_all(shares, 'fsdp', 0, 0, tiled=False)  11.2 us
    dot_general x6, matrix products, project(): jnp.dot(normed, weight, preferred_element_type=jnp.float32)  10.4 us
    all_to_all x1, starting transfers between devices, per_device(): lax.all_to_all(partials.reshape(dp_size, decode_rows, -1), DP, 0, 0, tile...  6.87 us
    slice x2, local copies, waits for them, and re-layouts, per_device(): gathered[4].reshape(dp_size, -1)[:, :decode_size]  6.73 us
    reshape x1, local copies, waits for them, and re-layouts, per_device(): page_keys = pool_keys.reshape(pool_local, PAGE, head_count, HEAD)  4.67 us
  transfers between devices with their start and end apart: 4, of which 4 were waited for; matrix products, arithmetic and copies ran while one was open for 18% of the time, Pallas kernels for 0%

profile of v5, /device:TPU:1, one launch (start us, length us, event | category | flops | bytes accessed | tf_op | source)
XLA Modules:
  0.0 204.6 jit_solution(17223545790402161234)
XLA Ops:
  11.2 13.3 %all-gather = bf16[5,256,256]{2,1,0:T(8,128)(2,1)} all-gather(bf16[5,64,256]{2,1,0:T(8,128)(2,1)S(1)} %bitcast_dynamic-update-slice_fusion.1), channel_id=2, replica_groups=mesh['dy'=4,'dz'=8,'fsdp'=8] {'dy'}, dimensions={1}, use_global_device_ids=true | all-gather | bytes 819200 | tf_op jit(solution)/shard_map/all_gather | solution.py:88
  25.2 2.1 %reshape_squeeze.9 = bf16[2048,2,128]{2,1,0:T(2,128)(2,1)} reshape(bf16[1,2048,256]{2,1,0:T(8,128)(2,1)} %param.23) | data formatting | bytes 2097152 | tf_op jit(solution)/shard_map/reshape;squeeze | solution.py:122
  27.3 2.3 %copy.86 = bf16[1,2048,256]{1,2,0:T(8,128)(2,1)} copy(bf16[1,2048,256]{2,1,0:T(8,128)(2,1)} %param.24) | data formatting | bytes 2097152 | tf_op jit(solution)/shard_map/reshape;squeeze | solution.py:123
  34.2 4.7 %copy.87 = bf16[48,128,256]{1,2,0:T(8,128)(2,1)} copy(bf16[48,128,256]{2,1,0:T(8,128)(2,1)} %param.26) | data formatting | bytes 6291456 | tf_op jit(solution)/shard_map/reshape | solution.py:202
  40.1 2.1 %convert_reduce_fusion = f32[512]{0:T(512)S(1)} fusion(bf16[512,2048]{1,0:T(8,128)(2,1)} %param.17), kind=kLoop, calls=%fused_computation.12 | loop fusion | flops 2096640 | bytes 2099200 | tf_op jit(solution)/shard_map/reduce_sum | solution.py:20
  45.8 1.9 fusion.6
  47.7 46.2 %all-gather.4.cloned.1.call-done = bf16[5,4,512,256]{3,2,1,0:T(8,128)(2,1)} async-done(((bf16[5,4,64,256]{3,2,1,0:T(8,128)(2,1)}), bf16[5,4,512,256]{3,2,1,0:T(8,128)(2,1)}) %all-gather.4.cloned.1.call-update) | async-done | bytes 5242896 | tf_op jit(solution)/shard_map/all_gather | solution.py:89
  93.9 4.8 %fusion.84 = (bf16[1,4,512,256]{3,2,1,0:T(8,128)(2,1)}, bf16[1,4,512,256]{3,2,1,0:T(8,128)(2,1)}, bf16[1,4,512,256]{3,2,1,0:T(8,128)(2,1)}, bf16[1,4,512,256]{3,2,1,0:T(8,128)(2,1)}, bf16[1,4,512,256]{3,2,1,0:T(8,128)(2,1)}) fusion(bf16[5,4,512,256]{3,2,1,0:T(8,128)(2,1)} %all-gather.4.cloned.1.call-done), kind=kLoop, calls=%fused_computation.168 | loop fusion | bytes 10485760 | tf_op jit(solution)/shard_map/slice | solution.py:96
  98.7 2.3 %copy.85 = bf16[2048,256]{0,1:T(8,128)(2,1)} copy(bf16[2048,256]{1,0:T(8,128)(2,1)} %bitcast.141) | data formatting | bytes 2097152 | tf_op jit(solution)/shard_map/squeeze | solution.py:92
  101.0 2.3 %copy.84 = bf16[2048,256]{0,1:T(8,128)(2,1)} copy(bf16[2048,256]{1,0:T(8,128)(2,1)} %bitcast.140) | data formatting | bytes 2097152 | tf_op jit(solution)/shard_map/squeeze | solution.py:92
  103.3 2.8 %fusion.13 = f32[512,2,128]{0,2,1:T(8,128)S(1)} fusion(bf16[2,128,2048]{2,1,0:T(8,128)(2,1)} %bitcast.146, bf16[512,2048]{1,0:T(8,128)(2,1)} %fusion.6), kind=kOutput, calls=%fused_computation.26 | convolution fusion | flops 536870912 | bytes 3670016 | tf_op jit(solution)/shard_map/dot_general | solution.py:102
  107.3 1.7 fusion
  110.3 2.1 %fusion.1 = f32[2,512]{1,0:T(2,128)S(1)} fusion(f32[2,512,2048]{2,1,0:T(8,128)S(1)} %get-tuple-element.46, f32[2,512]{1,0:T(2,128)S(1)} %max.11, pred[2048]{0:T(1024)(128)(4,1)S(1)} %iota_compare_fusion.4), kind=kLoop, calls=%fused_computation.9 | loop fusion | flops 8387584 | bytes 8398848 | tf_op jit(solution)/shard_map/reduce_sum | solution.py:141
  112.4 2.1 %fusion.22 = f32[512,2,128]{0,2,1:T(8,128)S(1)} fusion(bf16[2048,2,128]{0,2,1:T(8,128)(2,1)S(1)} %bitcast.145, f32[2,512,2048]{2,1,0:T(8,128)S(1)} %get-tuple-element.46, f32[2,512]{1,0:T(2,128)S(1)} %max.11, pred[2048]{0:T(1024)(128)(4,1)S(1)} %iota_compare_fusion.4), kind=kOutput, calls=%fused_computation.39 | convolution fusion | flops 545259520 | bytes 9967616 | tf_op jit(solution)/shard_map/hqk,khd->qhd/dot_general | solution.py:142
  117.2 1.5 copy.125
  118.7 2.4 %reshape_squeeze.11 = bf16[32,16384]{1,0:T(8,128)(2,1)} reshape(bf16[1,4,512,256]{3,2,1,0:T(8,128)(2,1)} %get-tuple-element.18) | data formatting | bytes 2097152 | tf_op jit(solution)/shard_map/reshape;squeeze | solution.py:96
  121.0 1.9 slice.99
  122.9 2.2 %reshape.369 = bf16[128,2048]{1,0:T(8,128)(2,1)} reshape(bf16[32,8192]{1,0:T(8,128)(2,1)} %slice.99) | data formatting | bytes 1048576 | tf_op jit(solution)/shard_map/reshape | solution.py:96
  127.7 1.9 fusion.39
  129.7 1.9 fusion.37
  132.6 5.1 %all-to-all-start = ((bf16[8,512,256]{2,1,0:T(8,128)(2,1)}), bf16[8,512,256]{2,1,0:T(8,128)(2,1)}, u32[]{:S(2)}, u32[]{:S(2)}) async-start(bf16[8,512,256]{2,1,0:T(8,128)(2,1)} %bitcast.138), calls=%async_computation | async-start | bytes 4194304 | tf_op jit(solution)/shard_map/all_to_all | solution.py:170
  137.8 2.8 %fusion.53 = f32[48,2,1,128]{3,2,1,0:T(1,128)S(1)} fusion(bf16[48,128,2,128]{1,3,2,0:T(8,128)(2,1)} %bitcast.135, bf16[48,2,128,1]{2,1,0,3:T(2,128)(2,1)S(1)} %fusion.58), kind=kOutput, calls=%fused_computation.94 | convolution fusion | flops 3145728 | bytes 3219456 | tf_op jit(solution)/shard_map/phd,pkhd->phk/dot_general | solution.py:204
  142.3 2.5 %fusion.10 = f32[48,2,1,128]{3,2,1,0:T(1,128)S(1)} fusion(f32[48,2,128,1]{2,0,1,3:T(8,128)S(1)} %get-tuple-element.36, bf16[48,128,256]{2,1,0:T(8,128)(2,1)S(1)} %copy-done), kind=kOutput, calls=%fused_computation.20 | convolution fusion | flops 18874368 | bytes 3244032 | tf_op jit(solution)/shard_map/phk,pkhd->phd/dot_general | solution.py:219
  145.4 18.7 %all-to-all-done = bf16[8,512,256]{2,1,0:T(8,128)(2,1)} async-done(((bf16[8,512,256]{2,1,0:T(8,128)(2,1)}), bf16[8,512,256]{2,1,0:T(8,128)(2,1)}, u32[]{:S(2)}, u32[]{:S(2)}) %all-to-all-start) | async-done | bytes 2097184 | tf_op jit(solution)/shard_map/all_to_all | solution.py:170
  164.8 6.9 %all-to-all-start.1 = ((f32[32,4,260]{2,1,0:T(4,128)}), f32[32,4,260]{2,1,0:T(4,128)S(1)}, u32[]{:S(2)}, u32[]{:S(2)}) async-start(f32[32,4,260]{2,1,0:T(4,128)} %reshape.373), calls=%async_computation.1 | async-start | bytes 393216 | tf_op jit(solution)/shard_map/all_to_all | solution.py:227
  171.7 2.4 %fusion.79 = bf16[128,256]{1,0:T(8,128)(2,1)} fusion(bf16[2048,256]{1,0:T(8,128)(2,1)} %bitcast.143, bf16[128,2048]{1,0:T(8,128)(2,1)} %reshape.369, f32[128]{0:T(128)} %copy-done.18, f32[128]{0:T(128)} %copy-done.16), kind=kOutput, calls=%fused_computation.167 | convolution fusion | flops 135266304 | bytes 1639424 | tf_op jit(solution)/shard_map/dot_general | solution.py:102
  174.3 2.7 %convert_reduce_fusion.1 = f32[512,256]{1,0:T(8,128)} fusion(bf16[8,512,256]{2,1,0:T(8,128)(2,1)} %all-to-all-done), kind=kLoop, calls=%fused_computation.17 | loop fusion | flops 1966080 | bytes 2621440 | tf_op jit(solution)/shard_map/reduce_sum | solution.py:173
  177.0 4.1 %all-to-all-done.1 = f32[32,4,260]{2,1,0:T(4,128)S(1)} async-done(((f32[32,4,260]{2,1,0:T(4,128)}), f32[32,4,260]{2,1,0:T(4,128)S(1)}, u32[]{:S(2)}, u32[]{:S(2)}) %all-to-all-start.1) | async-done | bytes 133152 | tf_op jit(solution)/shard_map/all_to_all | solution.py:227
  183.5 2.2 %convolution_convert_fusion.1 = bf16[4,2048]{1,0:T(4,128)(2,1)} fusion(bf16[2048,256]{1,0:T(8,128)(2,1)} %bitcast.136, f32[1,4,2,128]{3,2,1,0:T(2,128)S(1)} %broadcast_bitcast_fusion, f32[1,4,2,128]{3,2,1,0:T(2,128)S(1)} %broadcast_bitcast_fusion.1, f32[4,256]{1,0:T(4,128)S(1)} %fusion.45, f32[1,4,2,128]{3,2,1,0:T(2,128)S(1)} %broadcast_bitcast_fusion.2, ...), kind=kOutput, calls=%fused_computation.24 | convolution fusion | flops 4208640 | bytes 1083396 | tf_op jit(solution)/shard_map/dot_general | solution.py:164
  185.7 6.1 %all-to-all-start.2 = ((bf16[8,4,256]{2,1,0:T(4,128)(2,1)}), bf16[8,4,256]{2,1,0:T(4,128)(2,1)S(1)}, u32[]{:S(2)}, u32[]{:S(2)}) async-start(bf16[8,4,256]{2,1,0:T(4,128)(2,1)} %bitcast.38), calls=%async_computation.2 | async-start | bytes 32768 | tf_op jit(solution)/shard_map/all_to_all | solution.py:170
  191.8 1.9 add_convert_fusion
  193.7 2.8 %all-to-all-done.2 = bf16[8,4,256]{2,1,0:T(4,128)(2,1)S(1)} async-done(((bf16[8,4,256]{2,1,0:T(4,128)(2,1)}), bf16[8,4,256]{2,1,0:T(4,128)(2,1)S(1)}, u32[]{:S(2)}, u32[]{:S(2)}) %all-to-all-start.2) | async-done | bytes 16416 | tf_op jit(solution)/shard_map/all_to_all | solution.py:170
  (120 shorter events, 28.8 us)
Async XLA Ops:
  7.2 135.2 %copy-start = (bf16[48,128,256]{2,1,0:T(8,128)(2,1)S(1)}, bf16[48,128,256]{2,1,0:T(8,128)(2,1)}, u32[]{:S(2)}) copy-start(bf16[48,128,256]{2,1,0:T(8,128)(2,1)} %param.27) | copy-start | bytes 9437188
  7.2 22.5 %copy-start.14 = (s32[128]{0:T(128)S(1)}, s32[128]{0:T(128)}, u32[]{:S(2)}) copy-start(s32[128]{0:T(128)} %param.29) | copy-start | bytes 1540
  7.2 22.9 %copy-start.12 = (s32[1536]{0:T(1024)S(1)}, s32[1536]{0:T(1024)}, u32[]{:S(2)}) copy-start(s32[1536]{0:T(1024)} %param.28) | copy-start | bytes 18436
  7.2 23.1 %copy-start.15 = (s32[128]{0:T(128)S(1)}, s32[128]{0:T(128)}, u32[]{:S(2)}) copy-start(s32[128]{0:T(128)} %param.30) | copy-start | bytes 1540
  7.2 86.7 %all-gather.4.cloned.1.call-start = ((), (), s32[]{:S(2)}) async-start(), calls=%async_computation.3 | async-start | bytes 5898240 | tf_op jit(solution)/shard_map/all_gather | solution.py:89
  24.5 7.5 %copy-start.17 = (s32[128]{0:T(128)S(1)}, s32[128]{0:T(128)}, u32[]{:S(2)}) copy-start(s32[128]{0:T(128)} %param.31) | copy-start | bytes 1540
  38.9 3.4 %copy-start.1 = (bf16[512,2048]{1,0:T(8,128)(2,1)S(1)}, bf16[512,2048]{1,0:T(8,128)(2,1)}, u32[]{:S(2)}) copy-start(bf16[512,2048]{1,0:T(8,128)(2,1)} %param.17) | copy-start | bytes 6291460
  103.3 2.8 %copy-start.4 = (bf16[512,2048]{1,0:T(8,128)(2,1)S(1)}, bf16[512,2048]{1,0:T(8,128)(2,1)}, u32[]{:S(2)}) copy-start(bf16[512,2048]{1,0:T(8,128)(2,1)} %fusion.6) | copy-start | bytes 6291460
  103.3 2.8 %copy-start.7 = (bf16[2048,256]{0,1:T(8,128)(2,1)S(1)}, bf16[2048,256]{0,1:T(8,128)(2,1)}, u32[]{:S(2)}) copy-start(bf16[2048,256]{0,1:T(8,128)(2,1)} %copy.84) | copy-start | bytes 3145732
  106.1 0.9 copy-start.8
  106.1 1.2 copy-start.3
  110.2 2.1 %copy-start.6 = (bf16[1,2048,256]{1,2,0:T(8,128)(2,1)S(1)}, bf16[1,2048,256]{1,2,0:T(8,128)(2,1)}, u32[]{:S(2)}) copy-start(bf16[1,2048,256]{1,2,0:T(8,128)(2,1)} %copy.86) | copy-start | bytes 3145732
  112.3 2.1 %copy-start.5 = (bf16[1,4,512,256]{3,2,1,0:T(8,128)(2,1)S(1)}, bf16[1,4,512,256]{3,2,1,0:T(8,128)(2,1)}, u32[]{:S(2)}) copy-start(bf16[1,4,512,256]{3,2,1,0:T(8,128)(2,1)} %get-tuple-element.20) | copy-start | bytes 3145732
  115.2 1.2 copy-start.2
  122.9 8.7 %copy-start.9 = (f32[128,64]{0,1:T(8,128)S(1)}, f32[128,64]{0,1:T(8,128)}, u32[]{:S(2)}) copy-start(f32[128,64]{0,1:T(8,128)} %get-tuple-element.39) | copy-start | bytes 98308
  122.9 8.7 %copy-start.10 = (f32[128,64]{0,1:T(8,128)S(1)}, f32[128,64]{0,1:T(8,128)}, u32[]{:S(2)}) copy-start(f32[128,64]{0,1:T(8,128)} %get-tuple-element.40) | copy-start | bytes 98308
  126.4 5.2 %copy-start.16 = (f32[128]{0:T(128)}, f32[128]{0:T(128)S(1)}, u32[]{:S(2)}) copy-start(f32[128]{0:T(128)S(1)} %broadcast_multiply_fusion.1) | copy-start | bytes 1540
  127.7 3.8 %copy-start.18 = (f32[128]{0:T(128)}, f32[128]{0:T(128)S(1)}, u32[]{:S(2)}) copy-start(f32[128]{0:T(128)S(1)} %add_rsqrt_fusion.1) | copy-start | bytes 1540
  129.7 8.1 %copy-start.13 = (pred[48]{0:T(512)(128)(4,1)S(1)}, pred[48]{0:T(512)(128)(4,1)}, u32[]{:S(2)}) copy-start(pred[48]{0:T(512)(128)(4,1)} %get-tuple-element.16) | copy-start | bytes 148
  132.6 8.2 %copy-start.11 = (pred[48,128]{1,0:T(8,128)(4,1)S(1)}, pred[48,128]{1,0:T(8,128)(4,1)}, u32[]{:S(2)}) copy-start(pred[48,128]{1,0:T(8,128)(4,1)} %iota_compare_fusion.2) | copy-start | bytes 18436
  132.6 31.4 %all-to-all-start = ((bf16[8,512,256]{2,1,0:T(8,128)(2,1)}), bf16[8,512,256]{2,1,0:T(8,128)(2,1)}, u32[]{:S(2)}, u32[]{:S(2)}) async-start(bf16[8,512,256]{2,1,0:T(8,128)(2,1)} %bitcast.138), calls=%async_computation | async-start | bytes 4194304 | tf_op jit(solution)/shard_map/all_to_all | solution.py:170
  164.8 16.3 %all-to-all-start.1 = ((f32[32,4,260]{2,1,0:T(4,128)}), f32[32,4,260]{2,1,0:T(4,128)S(1)}, u32[]{:S(2)}, u32[]{:S(2)}) async-start(f32[32,4,260]{2,1,0:T(4,128)} %reshape.373), calls=%async_computation.1 | async-start | bytes 393216 | tf_op jit(solution)/shard_map/all_to_all | solution.py:227
  185.7 10.8 %all-to-all-start.2 = ((bf16[8,4,256]{2,1,0:T(4,128)(2,1)}), bf16[8,4,256]{2,1,0:T(4,128)(2,1)S(1)}, u32[]{:S(2)}, u32[]{:S(2)}) async-start(bf16[8,4,256]{2,1,0:T(4,128)(2,1)} %bitcast.38), calls=%async_computation.2 | async-start | bytes 32768 | tf_op jit(solution)/shard_map/all_to_all | solution.py:170
Sparse Core Ops, SparseCore 0:
  24.7 69.2 all-gather.3

commit v6 on v5

--- a/solution.py
+++ b/solution.py
@@ -115,48 +115,6 @@
     group_keys = rotary(prefill_k, prefill_positions, HEAD).astype(jnp.bfloat16)
     group_values = prefill_v.astype(jnp.bfloat16)
 
-    prior_slots = prior_keys.shape[1]
-    group_queries = group_queries.reshape(group_rows, head_count, HEAD)
-    group_keys = group_keys.reshape(group_rows, head_count, HEAD)
-    group_values = group_values.reshape(group_rows, head_count, HEAD)
-    stored_keys = prior_keys[0].reshape(prior_slots, head_count, HEAD)
-    stored_values = prior_values[0].reshape(prior_slots, head_count, HEAD)
-    prior_scores = (
-        jnp.einsum("qhd,khd->hqk", group_queries, stored_keys, preferred_element_type=jnp.float32)
-        * score_scale
-    )
-    prior_live = jnp.arange(prior_slots, dtype=jnp.int32) < prior_length[0]
-    prior_scores = jnp.where(prior_live[None, None, :], prior_scores, NEG_FILL)
-    group_scores = (
-        jnp.einsum("qhd,khd->hqk", group_queries, group_keys, preferred_element_type=jnp.float32)
-        * score_scale
-    )
-    causal = jnp.arange(group_rows)[None, :] <= jnp.arange(group_rows)[:, None]
-    group_scores = jnp.where(causal[None], group_scores, NEG_FILL)
-    row_top = jnp.maximum(
-        jnp.max(prior_scores, axis=2, keepdims=True), jnp.max(group_scores, axis=2, keepdims=True)
-    )
-    prior_weights = jnp.exp(prior_scores - row_top)
-    group_weights = jnp.exp(group_scores - row_top)
-    weight_total = jnp.sum(prior_weights, axis=2) + jnp.sum(group_weights, axis=2)
-    combined = jnp.einsum(
-        "hqk,khd->qhd",
-        prior_weights.astype(jnp.bfloat16),
-        stored_values,
-        preferred_element_type=jnp.float32,
-    )
-    combined = combined + jnp.einsum(
-        "hqk,khd->qhd",
-        group_weights.astype(jnp.bfloat16),
-        group_values,
-        preferred_element_type=jnp.float32,
-    )
-    prefill_attended = (
-        (combined / jnp.transpose(weight_total)[:, :, None])
-        .reshape(group_rows, local_width)
-        .astype(jnp.bfloat16)
-    )
-
     model_size = out_columns.shape[0] // local_width
     column_start = model_index * local_width
 
@@ -174,10 +132,6 @@
         residual = lax.dynamic_slice_in_dim(own_tokens, column_start, local_width, 1)
         return (residual.astype(jnp.float32) + branch).astype(jnp.bfloat16)
 
-    prefill_shares, all_decode = lax.optimization_barrier(
-        (send_shares(prefill_attended), all_decode)
-    )
-    prefill_received = exchange(prefill_shares)
     decode_q, decode_k, decode_v = project(all_decode)
     slot_queries = rotary(decode_q, decode_positions, HEAD).astype(jnp.bfloat16)
     slot_keys = rotary(decode_k, decode_positions, HEAD).astype(jnp.bfloat16)
@@ -223,7 +177,51 @@
         member_weights.T, page_mix.reshape(pool_local, local_width), precision=lax.Precision.HIGHEST
     )
     partials = jnp.concatenate([slot_top, slot_total, slot_mix], axis=1)
-    partials, prefill_received = lax.optimization_barrier((partials, prefill_received))
+    partials, group_queries, group_keys, group_values = lax.optimization_barrier(
+        (partials, group_queries, group_keys, group_values)
+    )
+    prior_slots = prior_keys.shape[1]
+    group_queries = group_queries.reshape(group_rows, head_count, HEAD)
+    group_keys = group_keys.reshape(group_rows, head_count, HEAD)
+    group_values = group_values.reshape(group_rows, head_count, HEAD)
+    stored_keys = prior_keys[0].reshape(prior_slots, head_count, HEAD)
+    stored_values = prior_values[0].reshape(prior_slots, head_count, HEAD)
+    prior_scores = (
+        jnp.einsum("qhd,khd->hqk", group_queries, stored_keys, preferred_element_type=jnp.float32)
+        * score_scale
+    )
+    prior_live = jnp.arange(prior_slots, dtype=jnp.int32) < prior_length[0]
+    prior_scores = jnp.where(prior_live[None, None, :], prior_scores, NEG_FILL)
+    group_scores = (
+        jnp.einsum("qhd,khd->hqk", group_queries, group_keys, preferred_element_type=jnp.float32)
+        * score_scale
+    )
+    causal = jnp.arange(group_rows)[None, :] <= jnp.arange(group_rows)[:, None]
+    group_scores = jnp.where(causal[None], group_scores, NEG_FILL)
+    row_top = jnp.maximum(
+        jnp.max(prior_scores, axis=2, keepdims=True), jnp.max(group_scores, axis=2, keepdims=True)
+    )
+    prior_weights = jnp.exp(prior_scores - row_top)
+    group_weights = jnp.exp(group_scores - row_top)
+    weight_total = jnp.sum(prior_weights, axis=2) + jnp.sum(group_weights, axis=2)
+    combined = jnp.einsum(
+        "hqk,khd->qhd",
+        prior_weights.astype(jnp.bfloat16),
+        stored_values,
+        preferred_element_type=jnp.float32,
+    )
+    combined = combined + jnp.einsum(
+        "hqk,khd->qhd",
+        group_weights.astype(jnp.bfloat16),
+        group_values,
+        preferred_element_type=jnp.float32,
+    )
+    prefill_attended = (
+        (combined / jnp.transpose(weight_total)[:, :, None])
+        .reshape(group_rows, local_width)
+        .astype(jnp.bfloat16)
+    )
+
     received = lax.all_to_all(
         partials.reshape(dp_size, decode_rows, -1), DP, 0, 0, tiled=False
     )
@@ -253,10 +251,10 @@
         own_values.astype(jnp.float32), own_factor, HEAD
     )
     decode_attended = rescale(final_mix, 1.0 / final_total, HEAD).astype(jnp.bfloat16)
-    return (
-        mixed(prefill_received, prefill_tokens),
-        mixed(exchange(send_shares(decode_attended)), decode_tokens),
-    )
+    attended = jnp.concatenate([prefill_attended, decode_attended], axis=0)
+    own_tokens = jnp.concatenate([prefill_tokens, decode_tokens], axis=0)
+    result = mixed(exchange(send_shares(attended)), own_tokens)
+    return (result[:group_rows], result[group_rows:])
 
 
 def solution(mesh):

time: 206 us -> 222 us (1.078)
  local copies, waits for them, and re-layouts: 39.7 us -> 51.1 us
  other arithmetic: 21.9 us -> 30 us
  starting transfers between devices: 18.1 us -> 12.8 us
    convert_element_type x0 -> x4, local copies, waits for them, and re-layouts: none -> 7.14 us  [the longest x2 4.5 us: layer_norm(): return (centred * lax.rsqrt(variance + EPSILON)).astype(jnp.bfloat16)]
    all_to_all x2 -> x1, starting transfers between devices: 11.2 us -> 5.52 us  [exchange(): return lax.all_to_all(shares, 'fsdp', 0, 0, tiled=False)]
    all_to_all x2 -> x1, waiting for transfers between devices: 21.5 us -> 26.7 us  [exchange(): return lax.all_to_all(shares, 'fsdp', 0, 0, tiled=False)]
    all_to_all x1, waiting for transfers between devices: 4.09 us -> 0.01 us  [per_device(): lax.all_to_all(partials.reshape(dp_size, decode_rows, -1), DP, 0, 0, tile...]
    convert_element_type x2 -> x1, other arithmetic: 3.13 us -> 0.1 us  [mixed(): return (residual.astype(jnp.float32) + branch).astype(jnp.bfloat16)]
    unnamed x45 -> x60, local copies, waits for them, and re-layouts: 4.22 us -> 6.1 us
    slice x2 -> x3, local copies, waits for them, and re-layouts: 6.73 us -> 6.25 us  [the longest x1 4.95 us: per_device(): projection_weights = [gathered[p] for p in range(3)]]
  transfers between devices with their start and end apart: 4 -> 3, of which waited for: 4 -> 2; matrix products, arithmetic and copies ran while one was open for 18% -> 16% of each run, Pallas kernels for 0% -> 0%
where the time goes in v6:
time: 222 us; the launch traced here: 221 us
  waiting for transfers between devices  72.7 us (33%)
  local copies, waits for them, and re-layouts  51.1 us (23%)
  other arithmetic  30 us (14%)
  matrix products  25.5 us (11%)
  between operations  15.3 us (7%)
  blocking collectives  13.3 us (6%)
  starting transfers between devices  12.8 us (6%)
    all_gather x1, waiting for transfers between devices, per_device(): lax.all_gather(across_y, 'dz', axis=2, tiled=False)  46.1 us
    all_to_all x1, waiting for transfers between devices, exchange(): return lax.all_to_all(shares, 'fsdp', 0, 0, tiled=False)  26.7 us
    all_gather x1, blocking collectives, per_device(): across_y = lax.all_gather(bundle, 'dy', axis=1, tiled=False)  13.3 us
    dot_general x6, matrix products, project(): jnp.dot(normed, weight, preferred_element_type=jnp.float32)  9.3 us
    all_to_all x1, starting transfers between devices, per_device(): lax.all_to_all(partials.reshape(dp_size, decode_rows, -1), DP, 0, 0, tile...  7.21 us
    unnamed x60, local copies, waits for them, and re-layouts  6.1 us
    all_to_all x1, starting transfers between devices, exchange(): return lax.all_to_all(shares, 'fsdp', 0, 0, tiled=False)  5.52 us
    slice x1, local copies, waits for them, and re-layouts, per_device(): projection_weights = [gathered[p] for p in range(3)]  4.95 us
  transfers between devices with their start and end apart: 3, of which 2 were waited for; matrix products, arithmetic and copies ran while one was open for 16% of the time, Pallas kernels for 0%

profile of v6, /device:TPU:1, one launch (start us, length us, event | category | flops | bytes accessed | tf_op | source)
XLA Modules:
  0.0 220.6 jit_solution(10757766693366547893)
XLA Ops:
  11.2 13.3 %all-gather = bf16[5,256,256]{2,1,0:T(8,128)(2,1)} all-gather(bf16[5,64,256]{2,1,0:T(8,128)(2,1)S(1)} %bitcast_dynamic-update-slice_fusion.1), channel_id=2, replica_groups=mesh['dy'=4,'dz'=8,'fsdp'=8] {'dy'}, dimensions={1}, use_global_device_ids=true | all-gather | bytes 819200 | tf_op jit(solution)/shard_map/all_gather | solution.py:88
  24.5 4.7 %copy.92 = bf16[48,128,256]{1,2,0:T(8,128)(2,1)} copy(bf16[48,128,256]{2,1,0:T(8,128)(2,1)} %param.26) | data formatting | bytes 6291456 | tf_op jit(solution)/shard_map/reshape | solution.py:156
  34.4 2.3 %copy.94 = bf16[1,2048,256]{1,2,0:T(8,128)(2,1)} copy(bf16[1,2048,256]{2,1,0:T(8,128)(2,1)} %param.24) | data formatting | bytes 2097152 | tf_op jit(solution)/shard_map/reshape;squeeze | solution.py:188
  36.7 2.1 reshape_squeeze.10
  40.2 2.1 convert_reduce_fusion
  45.9 1.9 fusion.6
  47.8 46.1 %all-gather.4.cloned.1.call-done = bf16[5,4,512,256]{3,2,1,0:T(8,128)(2,1)} async-done(((bf16[5,4,64,256]{3,2,1,0:T(8,128)(2,1)}), bf16[5,4,512,256]{3,2,1,0:T(8,128)(2,1)}) %all-gather.4.cloned.1.call-update) | async-done | bytes 5242896 | tf_op jit(solution)/shard_map/all_gather | solution.py:89
  93.9 5.0 %fusion.69 = (bf16[1,4,512,256]{3,2,1,0:T(8,128)(2,1)}, bf16[1,4,512,256]{3,2,1,0:T(8,128)(2,1)}, bf16[1,4,512,256]{3,2,1,0:T(8,128)(2,1)}, bf16[1,4,512,256]{3,2,1,0:T(8,128)(2,1)}, bf16[1,4,512,256]{3,2,1,0:T(8,128)(2,1)}) fusion(bf16[5,4,512,256]{3,2,1,0:T(8,128)(2,1)} %all-gather.4.cloned.1.call-done), kind=kLoop, calls=%fused_computation.158 | loop fusion | bytes 10485760 | tf_op jit(solution)/shard_map/slice | solution.py:92
  98.8 2.3 %reshape_squeeze.9 = bf16[32,16384]{1,0:T(8,128)(2,1)} reshape(bf16[1,4,512,256]{3,2,1,0:T(8,128)(2,1)} %get-tuple-element.21) | data formatting | bytes 2097152 | tf_op jit(solution)/shard_map/reshape;squeeze | solution.py:96
  101.2 2.1 slice_convert_fusion
  103.3 2.5 %reshape.410 = f32[128,2048]{1,0:T(8,128)} reshape(f32[32,8192]{1,0:T(8,128)} %slice_convert_fusion) | data formatting | bytes 2097152 | tf_op jit(solution)/shard_map/convert_element_type | solution.py:19
  111.5 2.3 %reshape.483 = bf16[128,2048,1]{1,0,2:T(8,128)(2,1)} reshape(bf16[32,8192]{1,0:T(8,128)(2,1)} %multiply_convert_fusion) | data formatting | bytes 1048576 | tf_op jit(solution)/shard_map/convert_element_type | solution.py:23
  113.7 2.3 %copy.93 = bf16[2048,256]{0,1:T(8,128)(2,1)} copy(bf16[2048,256]{1,0:T(8,128)(2,1)} %bitcast.142) | data formatting | bytes 2097152 | tf_op jit(solution)/shard_map/squeeze | solution.py:92
  116.0 2.3 %copy.91 = bf16[2048,256]{0,1:T(8,128)(2,1)} copy(bf16[2048,256]{1,0:T(8,128)(2,1)} %bitcast.141) | data formatting | bytes 2097152 | tf_op jit(solution)/shard_map/squeeze | solution.py:92
  118.3 2.0 fusion.72
  120.3 2.5 %fusion.71 = f32[128,2,128]{0,2,1:T(8,128)} fusion(bf16[128,2048,1]{1,0,2:T(8,128)(2,1)} %reshape.483, bf16[2,128,2048]{2,1,0:T(8,128)(2,1)} %bitcast.150), kind=kOutput, calls=%fused_computation.160 | convolution fusion | flops 134217728 | bytes 1703936 | tf_op jit(solution)/shard_map/dot_general | solution.py:102
  122.8 1.6 fusion.13
  124.3 1.6 fusion.15
  125.9 2.2 %convert_element_type.104 = bf16[128,2048]{1,0:T(8,128)(2,1)} reshape(bf16[32,8192]{1,0:T(8,128)(2,1)} %multiply_convert_fusion) | data formatting | bytes 1048576 | tf_op jit(solution)/shard_map/convert_element_type | solution.py:23
  132.8 2.8 %fusion.45 = f32[48,2,1,128]{3,2,1,0:T(1,128)S(1)} fusion(bf16[48,128,2,128]{1,3,2,0:T(8,128)(2,1)} %bitcast.136, bf16[48,2,128,1]{2,1,0,3:T(2,128)(2,1)S(1)} %fusion.50), kind=kOutput, calls=%fused_computation.89 | convolution fusion | flops 3145728 | bytes 3219456 | tf_op jit(solution)/shard_map/phd,pkhd->phk/dot_general | solution.py:158
  143.6 2.5 %fusion.10 = f32[48,2,1,128]{3,2,1,0:T(1,128)S(1)} fusion(f32[48,2,128,1]{2,0,1,3:T(8,128)S(1)} %get-tuple-element.36, bf16[48,128,256]{2,1,0:T(8,128)(2,1)S(1)} %copy-done), kind=kOutput, calls=%fused_computation.20 | convolution fusion | flops 18874368 | bytes 3244032 | tf_op jit(solution)/shard_map/phk,pkhd->phd/dot_general | solution.py:173
  149.4 7.2 %all-to-all-start = ((f32[32,4,260]{2,1,0:T(4,128)}), f32[32,4,260]{2,1,0:T(4,128)}, u32[]{:S(2)}, u32[]{:S(2)}) async-start(f32[32,4,260]{2,1,0:T(4,128)} %reshape.406), calls=%async_computation | async-start | bytes 393216 | tf_op jit(solution)/shard_map/all_to_all | solution.py:225
  156.8 1.7 fusion
  159.2 1.9 fusion.1
  161.1 2.9 %fusion.20 = f32[512,2,128]{0,2,1:T(8,128)} fusion(bf16[2048,2,128]{0,2,1:T(8,128)(2,1)S(1)} %bitcast.153, f32[2,512,2048]{2,1,0:T(8,128)S(1)} %get-tuple-element.46, f32[2,512]{1,0:T(2,128)S(1)} %max.11, pred[2048]{0:T(1024)(128)(4,1)S(1)} %iota_compare_fusion.4), kind=kOutput, calls=%fused_computation.36 | convolution fusion | flops 545259520 | bytes 9967616 | tf_op jit(solution)/shard_map/hqk,khd->qhd/dot_general | solution.py:207
  164.0 1.8 copy.95
  166.3 2.7 %fusion.25 = bf16[512,2,128]{0,2,1:T(8,128)(2,1)} fusion(f32[512,2,128]{0,2,1:T(8,128)} %fusion.20, bf16[512,2,128]{0,2,1:T(8,128)(2,1)} %bitcast.157, f32[2,512,512]{1,2,0:T(8,128)S(1)} %get-tuple-element.48, f32[2,512]{1,0:T(2,128)S(1)} %max.11, pred[512,512]{0,1:T(8,128)(4,1)S(1)} %iota_compare_fusion, f32[512,2]{0,1:T(2,128)S(1)} %add_bitcast_fusion), kind=kOutput, calls=%fused_computation.40 | convolution fusion | flops 136708096 | bytes 3416064 | tf_op jit(solution)/shard_map/hqk,khd->qhd/dot_general | solution.py:213
  173.1 2.3 %convolution_convert_fusion = bf16[516,2048]{1,0:T(8,128)(2,1)S(1)} fusion(bf16[2048,256]{1,0:T(8,128)(2,1)} %bitcast.145, bf16[4,256]{0,1:T(8,128)(2,1)S(1)} %copy.73, bf16[512,256]{0,1:T(8,128)(2,1)} %bitcast.156), kind=kOutput, calls=%fused_computation.23 | convolution fusion | flops 542650368 | bytes 3426304 | tf_op jit(solution)/shard_map/dot_general | solution.py:122
  176.2 1.8 copy.132
  178.0 5.5 %all-to-all-start.1 = ((bf16[8,516,256]{2,1,0:T(8,128)(2,1)}), bf16[8,516,256]{2,1,0:T(8,128)(2,1)}, u32[]{:S(2)}, u32[]{:S(2)}) async-start(bf16[8,516,256]{2,1,0:T(8,128)(2,1)} %bitcast.137), calls=%async_computation.1 | async-start | bytes 4259840 | tf_op jit(solution)/shard_map/all_to_all | solution.py:128
  183.5 26.7 %all-to-all-done.1 = bf16[8,516,256]{2,1,0:T(8,128)(2,1)} async-done(((bf16[8,516,256]{2,1,0:T(8,128)(2,1)}), bf16[8,516,256]{2,1,0:T(8,128)(2,1)}, u32[]{:S(2)}, u32[]{:S(2)}) %all-to-all-start.1) | async-done | bytes 2113568 | tf_op jit(solution)/shard_map/all_to_all | solution.py:128
  210.1 2.1 convert_reduce_fusion.1
  (144 shorter events, 42.4 us)
Async XLA Ops:
  7.2 136.4 %copy-start = (bf16[48,128,256]{2,1,0:T(8,128)(2,1)S(1)}, bf16[48,128,256]{2,1,0:T(8,128)(2,1)}, u32[]{:S(2)}) copy-start(bf16[48,128,256]{2,1,0:T(8,128)(2,1)} %param.27) | copy-start | bytes 9437188
  7.2 86.7 %all-gather.4.cloned.1.call-start = ((), (), s32[]{:S(2)}) async-start(), calls=%async_computation.2 | async-start | bytes 5898240 | tf_op jit(solution)/shard_map/all_gather | solution.py:89
  24.5 4.7 %copy-start.22 = (s32[128]{0:T(128)S(1)}, s32[128]{0:T(128)}, u32[]{:S(2)}) copy-start(s32[128]{0:T(128)} %param.29) | copy-start | bytes 1540
  24.5 5.1 %copy-start.21 = (s32[1536]{0:T(1024)S(1)}, s32[1536]{0:T(1024)}, u32[]{:S(2)}) copy-start(s32[1536]{0:T(1024)} %param.28) | copy-start | bytes 18436
  24.5 5.3 %copy-start.23 = (s32[128]{0:T(128)S(1)}, s32[128]{0:T(128)}, u32[]{:S(2)}) copy-start(s32[128]{0:T(128)} %param.30) | copy-start | bytes 1540
  24.5 7.1 %copy-start.24 = (s32[128]{0:T(128)S(1)}, s32[128]{0:T(128)}, u32[]{:S(2)}) copy-start(s32[128]{0:T(128)} %param.31) | copy-start | bytes 1540
  38.8 3.5 %copy-start.2 = (bf16[512,2048]{1,0:T(8,128)(2,1)S(1)}, bf16[512,2048]{1,0:T(8,128)(2,1)}, u32[]{:S(2)}) copy-start(bf16[512,2048]{1,0:T(8,128)(2,1)} %param.17) | copy-start | bytes 6291460
  108.9 1.7 copy-start.6
  118.3 4.5 %copy-start.7 = (bf16[2048,256]{0,1:T(8,128)(2,1)S(1)}, bf16[2048,256]{0,1:T(8,128)(2,1)}, u32[]{:S(2)}) copy-start(bf16[2048,256]{0,1:T(8,128)(2,1)} %copy.93) | copy-start | bytes 3145732
  118.3 4.5 %copy-start.10 = (bf16[512,2048]{1,0:T(8,128)(2,1)S(1)}, bf16[512,2048]{1,0:T(8,128)(2,1)}, u32[]{:S(2)}) copy-start(bf16[512,2048]{1,0:T(8,128)(2,1)} %fusion.6) | copy-start | bytes 6291460
  122.8 1.6 copy-start.8
  135.6 0.6 copy-start.18
  142.4 4.4 %copy-start.4 = (bf16[1,4,512,256]{3,2,1,0:T(8,128)(2,1)S(1)}, bf16[1,4,512,256]{3,2,1,0:T(8,128)(2,1)}, u32[]{:S(2)}) copy-start(bf16[1,4,512,256]{3,2,1,0:T(8,128)(2,1)} %get-tuple-element.18) | copy-start | bytes 3145732
  142.4 4.4 %copy-start.11 = (bf16[512,2048]{1,0:T(8,128)(2,1)S(1)}, bf16[512,2048]{1,0:T(8,128)(2,1)}, u32[]{:S(2)}) copy-start(bf16[512,2048]{1,0:T(8,128)(2,1)} %fusion.6) | copy-start | bytes 6291460
  143.5 4.8 %copy-start.14 = (f32[512,64]{0,1:T(8,128)S(1)}, f32[512,64]{0,1:T(8,128)}, u32[]{:S(2)}) copy-start(f32[512,64]{0,1:T(8,128)} %get-tuple-element.37) | copy-start | bytes 393220
  143.5 4.8 %copy-start.15 = (f32[512,64]{0,1:T(8,128)S(1)}, f32[512,64]{0,1:T(8,128)}, u32[]{:S(2)}) copy-start(f32[512,64]{0,1:T(8,128)} %get-tuple-element.38) | copy-start | bytes 393220
  143.6 4.8 %copy-start.16 = (f32[512,2,128]{0,2,1:T(8,128)S(1)}, f32[512,2,128]{0,2,1:T(8,128)}, u32[]{:S(2)}) copy-start(f32[512,2,128]{0,2,1:T(8,128)} %fusion.13) | copy-start | bytes 1572868
  143.6 4.8 %copy-start.17 = (f32[512,2,128]{0,2,1:T(8,128)S(1)}, f32[512,2,128]{0,2,1:T(8,128)}, u32[]{:S(2)}) copy-start(f32[512,2,128]{0,2,1:T(8,128)} %fusion.15) | copy-start | bytes 1572868
  146.8 9.8 %copy-start.19 = (bf16[128,2,128]{0,2,1:T(8,128)(2,1)S(1)}, bf16[128,2,128]{0,2,1:T(8,128)(2,1)}, u32[]{:S(2)}) copy-start(bf16[128,2,128]{0,2,1:T(8,128)(2,1)} %get-tuple-element.51) | copy-start | bytes 196612
  146.8 10.0 %copy-start.9 = (bf16[2048,2,128]{2,1,0:T(2,128)(2,1)S(1)}, bf16[2048,2,128]{2,1,0:T(2,128)(2,1)}, u32[]{:S(2)}) copy-start(bf16[2048,2,128]{2,1,0:T(2,128)(2,1)} %reshape_squeeze.10) | copy-start | bytes 3145732
  149.4 19.9 %all-to-all-start = ((f32[32,4,260]{2,1,0:T(4,128)}), f32[32,4,260]{2,1,0:T(4,128)}, u32[]{:S(2)}, u32[]{:S(2)}) async-start(f32[32,4,260]{2,1,0:T(4,128)} %reshape.406), calls=%async_computation | async-start | bytes 393216 | tf_op jit(solution)/shard_map/all_to_all | solution.py:225
  159.2 1.9 copy-start.13
  166.3 2.7 %copy-start.5 = (bf16[1,4,512,256]{3,2,1,0:T(8,128)(2,1)S(1)}, bf16[1,4,512,256]{3,2,1,0:T(8,128)(2,1)}, u32[]{:S(2)}) copy-start(bf16[1,4,512,256]{3,2,1,0:T(8,128)(2,1)} %get-tuple-element.18) | copy-start | bytes 3145732
  166.3 2.7 %copy-start.12 = (bf16[128,2048]{1,0:T(8,128)(2,1)S(1)}, bf16[128,2048]{1,0:T(8,128)(2,1)}, u32[]{:S(2)}) copy-start(bf16[128,2048]{1,0:T(8,128)(2,1)} %convert_element_type.104) | copy-start | bytes 1572868
  178.0 34.3 %copy-start.20 = (bf16[4,2048]{1,0:T(4,128)(2,1)S(1)}, bf16[4,2048]{1,0:T(4,128)(2,1)}, u32[]{:S(2)}) copy-start(bf16[4,2048]{1,0:T(4,128)(2,1)} %param.18) | copy-start | bytes 49156
  178.0 32.2 %all-to-all-start.1 = ((bf16[8,516,256]{2,1,0:T(8,128)(2,1)}), bf16[8,516,256]{2,1,0:T(8,128)(2,1)}, u32[]{:S(2)}, u32[]{:S(2)}) async-start(bf16[8,516,256]{2,1,0:T(8,128)(2,1)} %bitcast.137), calls=%async_computation.1 | async-start | bytes 4259840 | tf_op jit(solution)/shard_map/all_to_all | solution.py:128
  183.5 30.3 %copy-start.1 = (bf16[48,128,256]{2,1,0:T(8,128)(2,1)S(1)}, bf16[48,128,256]{2,1,0:T(8,128)(2,1)}, u32[]{:S(2)}) copy-start(bf16[48,128,256]{2,1,0:T(8,128)(2,1)} %param.27) | copy-start | bytes 9437188
  210.1 2.2 %copy-start.3 = (bf16[512,2048]{1,0:T(8,128)(2,1)S(1)}, bf16[512,2048]{1,0:T(8,128)(2,1)}, u32[]{:S(2)}) copy-start(bf16[512,2048]{1,0:T(8,128)(2,1)} %param.17) | copy-start | bytes 6291460
Sparse Core Ops, SparseCore 0:
  24.6 69.2 all-gather.3

commit v7 on v5

--- a/solution.py
+++ b/solution.py
@@ -115,6 +115,13 @@
     group_keys = rotary(prefill_k, prefill_positions, HEAD).astype(jnp.bfloat16)
     group_values = prefill_v.astype(jnp.bfloat16)
 
+    decode_q, decode_k, decode_v = project(all_decode)
+    slot_queries = rotary(decode_q, decode_positions, HEAD).astype(jnp.bfloat16)
+    slot_keys = rotary(decode_k, decode_positions, HEAD).astype(jnp.bfloat16)
+    slot_values = decode_v.astype(jnp.bfloat16)
+    group_queries, group_keys, group_values, slot_queries = lax.optimization_barrier(
+        (group_queries, group_keys, group_values, slot_queries)
+    )
     prior_slots = prior_keys.shape[1]
     group_queries = group_queries.reshape(group_rows, head_count, HEAD)
     group_keys = group_keys.reshape(group_rows, head_count, HEAD)
@@ -174,14 +181,10 @@
         residual = lax.dynamic_slice_in_dim(own_tokens, column_start, local_width, 1)
         return (residual.astype(jnp.float32) + branch).astype(jnp.bfloat16)
 
-    prefill_shares, all_decode = lax.optimization_barrier(
-        (send_shares(prefill_attended), all_decode)
+    prefill_shares, slot_queries = lax.optimization_barrier(
+        (send_shares(prefill_attended), slot_queries)
     )
     prefill_received = exchange(prefill_shares)
-    decode_q, decode_k, decode_v = project(all_decode)
-    slot_queries = rotary(decode_q, decode_positions, HEAD).astype(jnp.bfloat16)
-    slot_keys = rotary(decode_k, decode_positions, HEAD).astype(jnp.bfloat16)
-    slot_values = decode_v.astype(jnp.bfloat16)
     own_start = data_index * decode_rows
     own_queries = lax.dynamic_slice_in_dim(slot_queries, own_start, decode_rows, 0)
     own_keys = lax.dynamic_slice_in_dim(slot_keys, own_start, decode_rows, 0)

time: 206 us -> 217 us (1.053)
  local copies, waits for them, and re-layouts: 39.7 us -> 47.3 us
  other arithmetic: 21.9 us -> 27.7 us
  waiting for transfers between devices: 71.8 us -> 68.3 us
    convert_element_type x1 -> x3, local copies, waits for them, and re-layouts: 0.11 us -> 7.03 us  [the longest x2 4.53 us: layer_norm(): return (centred * lax.rsqrt(variance + EPSILON)).astype(jnp.bfloat16)]
    all_to_all x2, waiting for transfers between devices: 21.5 us -> 19.2 us  [exchange(): return lax.all_to_all(shares, 'fsdp', 0, 0, tiled=False)]
    slice x2 -> x1, local copies, waits for them, and re-layouts: 6.73 us -> 4.81 us  [per_device(): out_columns = gathered[3]]
  transfers between devices with their start and end apart: 4 -> 4, of which waited for: 4 -> 4; matrix products, arithmetic and copies ran while one was open for 18% -> 19% of each run, Pallas kernels for 0% -> 0%
where the time goes in v7:
time: 217 us; the launch traced here: 216 us
  waiting for transfers between devices  68.3 us (31%)
  local copies, waits for them, and re-layouts  47.3 us (22%)
  other arithmetic  27.7 us (13%)
  matrix products  25.7 us (12%)
  starting transfers between devices  18.1 us (8%)
  between operations  15.2 us (7%)
  blocking collectives  13.3 us (6%)
    all_gather x1, waiting for transfers between devices, per_device(): lax.all_gather(across_y, 'dz', axis=2, tiled=False)  44.9 us
    all_to_all x2, waiting for transfers between devices, exchange(): return lax.all_to_all(shares, 'fsdp', 0, 0, tiled=False)  19.2 us
    all_gather x1, blocking collectives, per_device(): across_y = lax.all_gather(bundle, 'dy', axis=1, tiled=False)  13.3 us
    all_to_all x2, starting transfers between devices, exchange(): return lax.all_to_all(shares, 'fsdp', 0, 0, tiled=False)  11.2 us
    dot_general x6, matrix products, project(): jnp.dot(normed, weight, preferred_element_type=jnp.float32)  9 us
    all_to_all x1, starting transfers between devices, per_device(): lax.all_to_all(partials.reshape(dp_size, decode_rows, -1), DP, 0, 0, tile...  6.88 us
    unnamed x45, local copies, waits for them, and re-layouts  5.91 us
    slice x1, local copies, waits for them, and re-layouts, per_device(): out_columns = gathered[3]  4.81 us
  transfers between devices with their start and end apart: 4, of which 4 were waited for; matrix products, arithmetic and copies ran while one was open for 19% of the time, Pallas kernels for 0%

profile of v7, /device:TPU:1, one launch (start us, length us, event | category | flops | bytes accessed | tf_op | source)
XLA Modules:
  0.0 215.6 jit_solution(12789567372728350530)
XLA Ops:
  11.2 13.3 %all-gather = bf16[5,256,256]{2,1,0:T(8,128)(2,1)} all-gather(bf16[5,64,256]{2,1,0:T(8,128)(2,1)S(1)} %bitcast_dynamic-update-slice_fusion.1), channel_id=2, replica_groups=mesh['dy'=4,'dz'=8,'fsdp'=8] {'dy'}, dimensions={1}, use_global_device_ids=true | all-gather | bytes 819200 | tf_op jit(solution)/shard_map/all_gather | solution.py:88
  30.8 2.1 reshape_squeeze.10
  33.0 2.3 %copy.87 = bf16[1,2048,256]{1,2,0:T(8,128)(2,1)} copy(bf16[1,2048,256]{2,1,0:T(8,128)(2,1)} %param.24) | data formatting | bytes 2097152 | tf_op jit(solution)/shard_map/reshape;squeeze | solution.py:130
  36.2 4.7 %copy.89 = bf16[48,128,256]{1,2,0:T(8,128)(2,1)} copy(bf16[48,128,256]{2,1,0:T(8,128)(2,1)} %param.26) | data formatting | bytes 6291456 | tf_op jit(solution)/shard_map/reshape | solution.py:205
  42.1 1.9 convert_reduce_fusion
  47.0 1.9 fusion.6
  48.9 44.9 %all-gather.4.cloned.1.call-done = bf16[5,4,512,256]{3,2,1,0:T(8,128)(2,1)} async-done(((bf16[5,4,64,256]{3,2,1,0:T(8,128)(2,1)}), bf16[5,4,512,256]{3,2,1,0:T(8,128)(2,1)}) %all-gather.4.cloned.1.call-update) | async-done | bytes 5242896 | tf_op jit(solution)/shard_map/all_gather | solution.py:89
  93.9 4.8 %fusion.66 = (bf16[1,4,512,256]{3,2,1,0:T(8,128)(2,1)}, bf16[1,4,512,256]{3,2,1,0:T(8,128)(2,1)}, bf16[1,4,512,256]{3,2,1,0:T(8,128)(2,1)}, bf16[1,4,512,256]{3,2,1,0:T(8,128)(2,1)}, bf16[1,4,512,256]{3,2,1,0:T(8,128)(2,1)}) fusion(bf16[5,4,512,256]{3,2,1,0:T(8,128)(2,1)} %all-gather.4.cloned.1.call-done), kind=kLoop, calls=%fused_computation.155 | loop fusion | bytes 10485760 | tf_op jit(solution)/shard_map/slice | solution.py:93
  98.7 2.3 %reshape_squeeze.9 = bf16[32,16384]{1,0:T(8,128)(2,1)} reshape(bf16[1,4,512,256]{3,2,1,0:T(8,128)(2,1)} %get-tuple-element.27) | data formatting | bytes 2097152 | tf_op jit(solution)/shard_map/reshape;squeeze | solution.py:96
  101.0 2.1 slice_convert_fusion
  103.2 2.5 %reshape.414 = f32[128,2048]{1,0:T(8,128)} reshape(f32[32,8192]{1,0:T(8,128)} %slice_convert_fusion) | data formatting | bytes 2097152 | tf_op jit(solution)/shard_map/convert_element_type | solution.py:19
  111.3 2.3 %reshape.488 = bf16[128,2048,1]{1,0,2:T(8,128)(2,1)} reshape(bf16[32,8192]{1,0:T(8,128)(2,1)} %multiply_convert_fusion) | data formatting | bytes 1048576 | tf_op jit(solution)/shard_map/convert_element_type | solution.py:23
  113.6 2.3 %copy.85 = bf16[2048,256]{0,1:T(8,128)(2,1)} copy(bf16[2048,256]{1,0:T(8,128)(2,1)} %bitcast.152) | data formatting | bytes 2097152 | tf_op jit(solution)/shard_map/squeeze | solution.py:92
  115.9 2.3 %copy.86 = bf16[2048,256]{0,1:T(8,128)(2,1)} copy(bf16[2048,256]{1,0:T(8,128)(2,1)} %bitcast.151) | data formatting | bytes 2097152 | tf_op jit(solution)/shard_map/squeeze | solution.py:92
  118.2 2.0 fusion.68
  120.1 1.8 fusion.69
  130.0 2.5 %fusion.1 = f32[2,512]{1,0:T(2,128)} fusion(f32[2,512,2048]{2,1,0:T(8,128)S(1)} %get-tuple-element.54, f32[2,512]{1,0:T(2,128)S(1)} %max.11, pred[2048]{0:T(1024)(128)(4,1)S(1)} %iota_compare_fusion.4), kind=kLoop, calls=%fused_computation.9 | loop fusion | flops 8387584 | bytes 8398848 | tf_op jit(solution)/shard_map/reduce_sum | solution.py:148
  132.4 2.9 %fusion.20 = f32[512,2,128]{0,2,1:T(8,128)} fusion(bf16[2048,2,128]{0,2,1:T(8,128)(2,1)S(1)} %bitcast.162, f32[2,512,2048]{2,1,0:T(8,128)S(1)} %get-tuple-element.54, f32[2,512]{1,0:T(2,128)S(1)} %max.11, pred[2048]{0:T(1024)(128)(4,1)S(1)} %iota_compare_fusion.4), kind=kOutput, calls=%fused_computation.35 | convolution fusion | flops 545259520 | bytes 9967616 | tf_op jit(solution)/shard_map/hqk,khd->qhd/dot_general | solution.py:149
  137.9 2.5 %fusion.25 = bf16[512,2,128]{0,2,1:T(8,128)(2,1)S(1)} fusion(f32[512,2,128]{0,2,1:T(8,128)} %fusion.20, bf16[512,2,128]{0,2,1:T(8,128)(2,1)} %bitcast.165, f32[2,512,512]{1,2,0:T(8,128)} %copy-done.3, f32[2,512]{1,0:T(2,128)S(1)} %max.11, pred[512,512]{0,1:T(8,128)(4,1)S(1)} %iota_compare_fusion, f32[512,2]{0,1:T(2,128)S(1)} %add_bitcast_fusion), kind=kOutput, calls=%fused_computation.39 | convolution fusion | flops 136708096 | bytes 3416064 | tf_op jit(solution)/shard_map/hqk,khd->qhd/dot_general | solution.py:155
  143.5 5.1 %all-to-all-start = ((bf16[8,512,256]{2,1,0:T(8,128)(2,1)}), bf16[8,512,256]{2,1,0:T(8,128)(2,1)}, u32[]{:S(2)}, u32[]{:S(2)}) async-start(bf16[8,512,256]{2,1,0:T(8,128)(2,1)} %bitcast.147), calls=%async_computation | async-start | bytes 4194304 | tf_op jit(solution)/shard_map/all_to_all | solution.py:177
  148.8 2.3 %convert_element_type.122 = bf16[128,2048]{1,0:T(8,128)(2,1)} reshape(bf16[32,8192]{1,0:T(8,128)(2,1)} %multiply_convert_fusion) | data formatting | bytes 1048576 | tf_op jit(solution)/shard_map/convert_element_type | solution.py:23
  151.1 2.8 %fusion.41 = f32[48,2,1,128]{3,2,1,0:T(1,128)S(1)} fusion(bf16[48,128,2,128]{1,3,2,0:T(8,128)(2,1)} %bitcast.144, bf16[48,2,128,1]{2,1,0,3:T(2,128)(2,1)S(1)} %fusion.46), kind=kOutput, calls=%fused_computation.84 | convolution fusion | flops 3145728 | bytes 3219456 | tf_op jit(solution)/shard_map/phd,pkhd->phk/dot_general | solution.py:207
  155.6 2.5 %fusion.10 = f32[48,2,1,128]{3,2,1,0:T(1,128)S(1)} fusion(f32[48,2,128,1]{2,0,1,3:T(8,128)S(1)} %get-tuple-element.44, bf16[48,128,256]{2,1,0:T(8,128)(2,1)S(1)} %copy-done), kind=kOutput, calls=%fused_computation.20 | convolution fusion | flops 18874368 | bytes 3244032 | tf_op jit(solution)/shard_map/phk,pkhd->phd/dot_general | solution.py:222
  158.6 16.4 %all-to-all-done = bf16[8,512,256]{2,1,0:T(8,128)(2,1)} async-done(((bf16[8,512,256]{2,1,0:T(8,128)(2,1)}), bf16[8,512,256]{2,1,0:T(8,128)(2,1)}, u32[]{:S(2)}, u32[]{:S(2)}) %all-to-all-start) | async-done | bytes 2097184 | tf_op jit(solution)/shard_map/all_to_all | solution.py:177
  175.7 6.9 %all-to-all-start.1 = ((f32[32,4,260]{2,1,0:T(4,128)}), f32[32,4,260]{2,1,0:T(4,128)S(1)}, u32[]{:S(2)}, u32[]{:S(2)}) async-start(f32[32,4,260]{2,1,0:T(4,128)} %reshape.410), calls=%async_computation.1 | async-start | bytes 393216 | tf_op jit(solution)/shard_map/all_to_all | solution.py:230
  182.6 2.3 %fusion.70 = bf16[128,256]{1,0:T(8,128)(2,1)} fusion(bf16[128,2048]{1,0:T(8,128)(2,1)} %convert_element_type.122, bf16[2048,256]{1,0:T(8,128)(2,1)} %bitcast.149), kind=kOutput, calls=%fused_computation.159 | convolution fusion | flops 134217728 | bytes 1638400 | tf_op jit(solution)/shard_map/dot_general | solution.py:102
  185.1 2.7 %convert_reduce_fusion.1 = f32[512,256]{1,0:T(8,128)} fusion(bf16[8,512,256]{2,1,0:T(8,128)(2,1)} %all-to-all-done), kind=kLoop, calls=%fused_computation.17 | loop fusion | flops 1966080 | bytes 2621440 | tf_op jit(solution)/shard_map/reduce_sum | solution.py:180
  187.9 4.2 %all-to-all-done.1 = f32[32,4,260]{2,1,0:T(4,128)S(1)} async-done(((f32[32,4,260]{2,1,0:T(4,128)}), f32[32,4,260]{2,1,0:T(4,128)S(1)}, u32[]{:S(2)}, u32[]{:S(2)}) %all-to-all-start.1) | async-done | bytes 133152 | tf_op jit(solution)/shard_map/all_to_all | solution.py:230
  194.4 2.2 %convolution_convert_fusion.1 = bf16[4,2048]{1,0:T(4,128)(2,1)} fusion(bf16[2048,256]{1,0:T(8,128)(2,1)} %bitcast.145, f32[1,4,2,128]{3,2,1,0:T(2,128)S(1)} %broadcast_bitcast_fusion, f32[1,4,2,128]{3,2,1,0:T(2,128)S(1)} %broadcast_bitcast_fusion.1, f32[4,256]{1,0:T(4,128)S(1)} %fusion.33, f32[1,4,2,128]{3,2,1,0:T(2,128)S(1)} %broadcast_bitcast_fusion.2, ...), kind=kOutput, calls=%fused_computation.24 | convolution fusion | flops 4208640 | bytes 1083396 | tf_op jit(solution)/shard_map/dot_general | solution.py:171
  196.7 6.1 %all-to-all-start.2 = ((bf16[8,4,256]{2,1,0:T(4,128)(2,1)}), bf16[8,4,256]{2,1,0:T(4,128)(2,1)S(1)}, u32[]{:S(2)}, u32[]{:S(2)}) async-start(bf16[8,4,256]{2,1,0:T(4,128)(2,1)} %bitcast.42), calls=%async_computation.2 | async-start | bytes 32768 | tf_op jit(solution)/shard_map/all_to_all | solution.py:177
  202.7 1.9 add_convert_fusion
  204.6 2.8 %all-to-all-done.2 = bf16[8,4,256]{2,1,0:T(4,128)(2,1)S(1)} async-done(((bf16[8,4,256]{2,1,0:T(4,128)(2,1)}), bf16[8,4,256]{2,1,0:T(4,128)(2,1)S(1)}, u32[]{:S(2)}, u32[]{:S(2)}) %all-to-all-start.2) | async-done | bytes 16416 | tf_op jit(solution)/shard_map/all_to_all | solution.py:177
  (129 shorter events, 40.8 us)
Async XLA Ops:
  7.2 148.4 %copy-start = (bf16[48,128,256]{2,1,0:T(8,128)(2,1)S(1)}, bf16[48,128,256]{2,1,0:T(8,128)(2,1)}, u32[]{:S(2)}) copy-start(bf16[48,128,256]{2,1,0:T(8,128)(2,1)} %param.27) | copy-start | bytes 9437188
  7.2 21.8 %copy-start.17 = (s32[128]{0:T(128)S(1)}, s32[128]{0:T(128)}, u32[]{:S(2)}) copy-start(s32[128]{0:T(128)} %param.31) | copy-start | bytes 1540
  7.2 86.7 %all-gather.4.cloned.1.call-start = ((), (), s32[]{:S(2)}) async-start(), calls=%async_computation.3 | async-start | bytes 5898240 | tf_op jit(solution)/shard_map/all_gather | solution.py:89
  40.9 3.2 %copy-start.1 = (bf16[512,2048]{1,0:T(8,128)(2,1)S(1)}, bf16[512,2048]{1,0:T(8,128)(2,1)}, u32[]{:S(2)}) copy-start(bf16[512,2048]{1,0:T(8,128)(2,1)} %param.17) | copy-start | bytes 6291460
  41.4 4.0 %copy-start.14 = (s32[48]{0:T(128)}, s32[48]{0:T(128)S(1)}, u32[]{:S(2)}) copy-start(s32[48]{0:T(128)S(1)} %get-tuple-element.25) | copy-start | bytes 580
  108.7 1.7 copy-start.5
  118.2 3.8 %copy-start.7 = (bf16[2048,256]{0,1:T(8,128)(2,1)S(1)}, bf16[2048,256]{0,1:T(8,128)(2,1)}, u32[]{:S(2)}) copy-start(bf16[2048,256]{0,1:T(8,128)(2,1)} %copy.86) | copy-start | bytes 3145732
  118.2 3.8 %copy-start.9 = (bf16[512,2048]{1,0:T(8,128)(2,1)S(1)}, bf16[512,2048]{1,0:T(8,128)(2,1)}, u32[]{:S(2)}) copy-start(bf16[512,2048]{1,0:T(8,128)(2,1)} %fusion.6) | copy-start | bytes 6291460
  122.0 1.2 copy-start.6
  123.2 1.2 copy-start.4
  124.0 2.0 copy-start.11
  124.0 2.0 copy-start.12
  125.9 1.2 copy-start.8
  127.1 1.7 copy-start.3
  130.0 2.5 %copy-start.10 = (bf16[1,2048,256]{1,2,0:T(8,128)(2,1)S(1)}, bf16[1,2048,256]{1,2,0:T(8,128)(2,1)}, u32[]{:S(2)}) copy-start(bf16[1,2048,256]{1,2,0:T(8,128)(2,1)} %copy.87) | copy-start | bytes 3145732
  137.1 3.3 %copy-start.2 = (bf16[1,4,512,256]{3,2,1,0:T(8,128)(2,1)S(1)}, bf16[1,4,512,256]{3,2,1,0:T(8,128)(2,1)}, u32[]{:S(2)}) copy-start(bf16[1,4,512,256]{3,2,1,0:T(8,128)(2,1)} %get-tuple-element.26) | copy-start | bytes 3145732
  142.6 6.1 %copy-start.16 = (pred[48]{0:T(512)(128)(4,1)S(1)}, pred[48]{0:T(512)(128)(4,1)}, u32[]{:S(2)}) copy-start(pred[48]{0:T(512)(128)(4,1)} %get-tuple-element.24) | copy-start | bytes 148
  143.5 31.5 %all-to-all-start = ((bf16[8,512,256]{2,1,0:T(8,128)(2,1)}), bf16[8,512,256]{2,1,0:T(8,128)(2,1)}, u32[]{:S(2)}, u32[]{:S(2)}) async-start(bf16[8,512,256]{2,1,0:T(8,128)(2,1)} %bitcast.147), calls=%async_computation | async-start | bytes 4194304 | tf_op jit(solution)/shard_map/all_to_all | solution.py:177
  148.7 5.3 %copy-start.13 = (pred[48,128]{1,0:T(8,128)(4,1)S(1)}, pred[48,128]{1,0:T(8,128)(4,1)}, u32[]{:S(2)}) copy-start(pred[48,128]{1,0:T(8,128)(4,1)} %iota_compare_fusion.2) | copy-start | bytes 18436
  148.7 6.6 %copy-start.15 = (s32[48]{0:T(128)S(1)}, s32[48]{0:T(128)}, u32[]{:S(2)}) copy-start(s32[48]{0:T(128)} %copy-done.14) | copy-start | bytes 580
  175.7 16.3 %all-to-all-start.1 = ((f32[32,4,260]{2,1,0:T(4,128)}), f32[32,4,260]{2,1,0:T(4,128)S(1)}, u32[]{:S(2)}, u32[]{:S(2)}) async-start(f32[32,4,260]{2,1,0:T(4,128)} %reshape.410), calls=%async_computation.1 | async-start | bytes 393216 | tf_op jit(solution)/shard_map/all_to_all | solution.py:230
  196.7 10.8 %all-to-all-start.2 = ((bf16[8,4,256]{2,1,0:T(4,128)(2,1)}), bf16[8,4,256]{2,1,0:T(4,128)(2,1)S(1)}, u32[]{:S(2)}, u32[]{:S(2)}) async-start(bf16[8,4,256]{2,1,0:T(4,128)(2,1)} %bitcast.42), calls=%async_computation.2 | async-start | bytes 32768 | tf_op jit(solution)/shard_map/all_to_all | solution.py:177
Sparse Core Ops, SparseCore 0:
  24.6 69.1 all-gather.3

commit v8 on v5

--- a/solution.py
+++ b/solution.py
@@ -80,21 +80,14 @@
     data_index = lax.axis_index(DP)
     model_index = lax.axis_index("fsdp")
 
-    decode_piece = decode_tokens.reshape(-1, local_width)
-    decode_piece = jnp.pad(decode_piece, ((0, weight_rows - decode_piece.shape[0]), (0, 0)))
-    bundle = jnp.stack(
-        [query_weight, key_weight, value_weight, jnp.transpose(out_weight), decode_piece]
-    )
+    bundle = jnp.stack([query_weight, key_weight, value_weight, jnp.transpose(out_weight)])
     across_y = lax.all_gather(bundle, "dy", axis=1, tiled=False)
     gathered = lax.all_gather(across_y, "dz", axis=2, tiled=False).reshape(
         bundle.shape[0], dp_size * weight_rows, local_width
     )
     projection_weights = [gathered[p] for p in range(3)]
     out_columns = gathered[3]
-    decode_size = decode_tokens.size
-    all_decode = (
-        gathered[4].reshape(dp_size, -1)[:, :decode_size].reshape(dp_size * decode_rows, -1)
-    )
+    all_decode = lax.all_gather(decode_tokens, DP, axis=0, tiled=True)
 
     def project(rows_in):
         normed = layer_norm(rows_in)

time: 206 us -> 206 us (level)
  blocking collectives: 13.3 us -> 62.2 us
  waiting for transfers between devices: 71.8 us -> 25.6 us
  starting transfers between devices: 18.1 us -> 28.9 us
  local copies, waits for them, and re-layouts: 39.7 us -> 30.5 us
  matrix products: 24.6 us -> 21.8 us
    all_gather x0 -> x1, blocking collectives: none -> 49.2 us  [per_device(): all_decode = lax.all_gather(decode_tokens, DP, axis=0, tiled=True)]
    all_gather x1, waiting for transfers between devices: 46.2 us -> 0.01 us  [per_device(): lax.all_gather(across_y, 'dz', axis=2, tiled=False)]
    all_to_all x2, starting transfers between devices: 11.2 us -> 22.8 us  [exchange(): return lax.all_to_all(shares, 'fsdp', 0, 0, tiled=False)]
    unnamed x45 -> x47, local copies, waits for them, and re-layouts: 4.22 us -> 1.06 us
    reshape x2 -> x0, local copies, waits for them, and re-layouts: 3.01 us -> none  [the longest x1 2.25 us: per_device(): gathered[4].reshape(dp_size, -1)[:, :decode_size]]
    dot_general x6, matrix products: 10.4 us -> 7.65 us  [project(): jnp.dot(normed, weight, preferred_element_type=jnp.float32)]
    slice x2 -> x1, local copies, waits for them, and re-layouts: 6.73 us -> 4.17 us  [per_device(): out_columns = gathered[3]]
    another operation x3 -> x1, local copies, waits for them, and re-layouts: 2.47 us -> 0.11 us  [the longest x1 2.35 us: per_device(): gathered[4].reshape(dp_size, -1)[:, :decode_size]]
  transfers between devices with their start and end apart: 4 -> 4, of which waited for: 4 -> 3; matrix products, arithmetic and copies ran while one was open for 18% -> 19% of each run, Pallas kernels for 0% -> 0%
where the time goes in v8:
time: 206 us; the launch traced here: 205 us
  blocking collectives  62.2 us (30%)
  local copies, waits for them, and re-layouts  30.5 us (15%)
  starting transfers between devices  28.9 us (14%)
  waiting for transfers between devices  25.6 us (12%)
  matrix products  21.8 us (11%)
  other arithmetic  20.6 us (10%)
  between operations  15.2 us (7%)
    all_gather x1, blocking collectives, per_device(): all_decode = lax.all_gather(decode_tokens, DP, axis=0, tiled=True)  49.2 us
    all_to_all x2, starting transfers between devices, exchange(): return lax.all_to_all(shares, 'fsdp', 0, 0, tiled=False)  22.8 us
    all_to_all x2, waiting for transfers between devices, exchange(): return lax.all_to_all(shares, 'fsdp', 0, 0, tiled=False)  21.5 us
    all_gather x1, blocking collectives, per_device(): across_y = lax.all_gather(bundle, 'dy', axis=1, tiled=False)  13 us
    dot_general x6, matrix products, project(): jnp.dot(normed, weight, preferred_element_type=jnp.float32)  7.65 us
    all_to_all x1, starting transfers between devices, per_device(): lax.all_to_all(partials.reshape(dp_size, decode_rows, -1), DP, 0, 0, tile...  6.07 us
    reshape x1, local copies, waits for them, and re-layouts, per_device(): page_keys = pool_keys.reshape(pool_local, PAGE, head_count, HEAD)  4.66 us
    squeeze x2, local copies, waits for them, and re-layouts, per_device(): projection_weights = [gathered[p] for p in range(3)]  4.56 us
  transfers between devices with their start and end apart: 4, of which 3 were waited for; matrix products, arithmetic and copies ran while one was open for 19% of the time, Pallas kernels for 0%

profile of v8, /device:TPU:1, one launch (start us, length us, event | category | flops | bytes accessed | tf_op | source)
XLA Modules:
  0.0 204.9 jit_solution(5124437509893021530)
XLA Ops:
  8.2 13.0 %all-gather = bf16[4,256,256]{2,1,0:T(8,128)(2,1)} all-gather(bf16[4,64,256]{2,1,0:T(8,128)(2,1)S(1)} %pad_maximum_fusion.4), channel_id=2, replica_groups=mesh['dy'=4,'dz'=8,'fsdp'=8] {'dy'}, dimensions={1}, use_global_device_ids=true | all-gather | bytes 655360 | tf_op jit(solution)/shard_map/all_gather | solution.py:84
  21.9 2.2 %reshape_squeeze.6 = bf16[2048,2,128]{2,1,0:T(2,128)(2,1)} reshape(bf16[1,2048,256]{2,1,0:T(8,128)(2,1)} %param.23) | data formatting | bytes 2097152 | tf_op jit(solution)/shard_map/reshape;squeeze | solution.py:115
  24.1 2.3 %copy.86 = bf16[1,2048,256]{1,2,0:T(8,128)(2,1)} copy(bf16[1,2048,256]{2,1,0:T(8,128)(2,1)} %param.24) | data formatting | bytes 2097152 | tf_op jit(solution)/shard_map/reshape;squeeze | solution.py:116
  26.4 49.2 %all-gather.2 = bf16[32,4,2048]{2,1,0:T(4,128)(2,1)} all-gather(bf16[1,4,2048]{2,1,0:T(4,128)(2,1)S(1)} %bitcast.152), channel_id=1, replica_groups=mesh['dy'=4,'dz'=8,'fsdp'=8] {'dy','dz'}, dimensions={0}, use_global_device_ids=true | all-gather | bytes 540672 | tf_op jit(solution)/shard_map/all_gather | solution.py:90
  75.6 2.0 reshape.432
  80.0 1.2 gather_fusion
  82.1 4.7 %copy.87 = bf16[48,128,256]{1,2,0:T(8,128)(2,1)} copy(bf16[48,128,256]{2,1,0:T(8,128)(2,1)} %param.26) | data formatting | bytes 6291456 | tf_op jit(solution)/shard_map/reshape | solution.py:195
  88.0 1.9 convert_reduce_fusion
  92.3 1.2 multiply_cosine_fusion
  93.5 1.9 fusion.6
  95.4 4.2 %fusion.84 = (bf16[1,4,512,256]{3,2,1,0:T(8,128)(2,1)}, bf16[1,4,512,256]{3,2,1,0:T(8,128)(2,1)}, bf16[1,4,512,256]{3,2,1,0:T(8,128)(2,1)}, bf16[1,4,512,256]{3,2,1,0:T(8,128)(2,1)}) fusion(bf16[4,4,512,256]{3,2,1,0:T(8,128)(2,1)} %all-gather.5.cloned.1.call-done), kind=kLoop, calls=%fused_computation.164 | loop fusion | bytes 8388608 | tf_op jit(solution)/shard_map/slice | solution.py:89
  99.6 2.3 %copy.85 = bf16[2048,256]{0,1:T(8,128)(2,1)} copy(bf16[2048,256]{1,0:T(8,128)(2,1)} %bitcast.134) | data formatting | bytes 2097152 | tf_op jit(solution)/shard_map/squeeze | solution.py:88
  101.9 2.3 %copy.84 = bf16[2048,256]{0,1:T(8,128)(2,1)} copy(bf16[2048,256]{1,0:T(8,128)(2,1)} %bitcast.133) | data formatting | bytes 2097152 | tf_op jit(solution)/shard_map/squeeze | solution.py:88
  104.2 2.7 %fusion.13 = f32[512,2,128]{0,2,1:T(8,128)S(1)} fusion(bf16[2,128,2048]{2,1,0:T(8,128)(2,1)} %bitcast.137, bf16[512,2048]{1,0:T(8,128)(2,1)} %fusion.6), kind=kOutput, calls=%fused_computation.26 | convolution fusion | flops 536870912 | bytes 3670016 | tf_op jit(solution)/shard_map/dot_general | solution.py:95
  108.2 1.7 fusion
  111.1 2.1 %fusion.1 = f32[2,512]{1,0:T(2,128)S(1)} fusion(f32[2,512,2048]{2,1,0:T(8,128)S(1)} %get-tuple-element.45, f32[2,512]{1,0:T(2,128)S(1)} %max.11, pred[2048]{0:T(1024)(128)(4,1)S(1)} %iota_compare_fusion.4), kind=kLoop, calls=%fused_computation.9 | loop fusion | flops 8387584 | bytes 8398848 | tf_op jit(solution)/shard_map/reduce_sum | solution.py:134
  113.2 2.1 %fusion.22 = f32[512,2,128]{0,2,1:T(8,128)S(1)} fusion(bf16[2048,2,128]{0,2,1:T(8,128)(2,1)S(1)} %bitcast.136, f32[2,512,2048]{2,1,0:T(8,128)S(1)} %get-tuple-element.45, f32[2,512]{1,0:T(2,128)S(1)} %max.11, pred[2048]{0:T(1024)(128)(4,1)S(1)} %iota_compare_fusion.4), kind=kOutput, calls=%fused_computation.39 | convolution fusion | flops 545259520 | bytes 9967616 | tf_op jit(solution)/shard_map/hqk,khd->qhd/dot_general | solution.py:135
  118.0 1.4 copy.125
  122.0 16.8 %all-to-all-start = ((bf16[8,512,256]{2,1,0:T(8,128)(2,1)}), bf16[8,512,256]{2,1,0:T(8,128)(2,1)}, u32[]{:S(2)}, u32[]{:S(2)}) async-start(bf16[8,512,256]{2,1,0:T(8,128)(2,1)} %bitcast.131), calls=%async_computation | async-start | bytes 4194304 | tf_op jit(solution)/shard_map/all_to_all | solution.py:163
  138.9 2.8 %fusion.53 = f32[48,2,1,128]{3,2,1,0:T(1,128)S(1)} fusion(bf16[48,128,2,128]{1,3,2,0:T(8,128)(2,1)} %bitcast.128, bf16[48,2,128,1]{2,1,0,3:T(2,128)(2,1)S(1)} %fusion.58), kind=kOutput, calls=%fused_computation.95 | convolution fusion | flops 3145728 | bytes 3219456 | tf_op jit(solution)/shard_map/phd,pkhd->phk/dot_general | solution.py:197
  143.4 2.5 %fusion.10 = f32[48,2,1,128]{3,2,1,0:T(1,128)S(1)} fusion(f32[48,2,128,1]{2,0,1,3:T(8,128)S(1)} %get-tuple-element.35, bf16[48,128,256]{2,1,0:T(8,128)(2,1)S(1)} %copy-done), kind=kOutput, calls=%fused_computation.20 | convolution fusion | flops 18874368 | bytes 3244032 | tf_op jit(solution)/shard_map/phk,pkhd->phd/dot_general | solution.py:212
  146.5 18.6 %all-to-all-done = bf16[8,512,256]{2,1,0:T(8,128)(2,1)} async-done(((bf16[8,512,256]{2,1,0:T(8,128)(2,1)}), bf16[8,512,256]{2,1,0:T(8,128)(2,1)}, u32[]{:S(2)}, u32[]{:S(2)}) %all-to-all-start) | async-done | bytes 2097184 | tf_op jit(solution)/shard_map/all_to_all | solution.py:163
  165.8 6.1 %all-to-all-start.1 = ((f32[32,4,260]{2,1,0:T(4,128)}), f32[32,4,260]{2,1,0:T(4,128)S(1)}, u32[]{:S(2)}, u32[]{:S(2)}) async-start(f32[32,4,260]{2,1,0:T(4,128)} %reshape.363), calls=%async_computation.1 | async-start | bytes 393216 | tf_op jit(solution)/shard_map/all_to_all | solution.py:220
  171.9 2.4 %fusion.79 = bf16[128,256]{1,0:T(8,128)(2,1)} fusion(bf16[2048,256]{1,0:T(8,128)(2,1)} %bitcast.141, bf16[128,2048]{1,0:T(8,128)(2,1)} %reshape.432, f32[128]{0:T(128)} %copy-done.21, f32[128]{0:T(128)} %copy-done.19), kind=kOutput, calls=%fused_computation.163 | convolution fusion | flops 135266304 | bytes 1639424 | tf_op jit(solution)/shard_map/dot_general | solution.py:95
  174.5 2.7 %convert_reduce_fusion.1 = f32[512,256]{1,0:T(8,128)} fusion(bf16[8,512,256]{2,1,0:T(8,128)(2,1)} %all-to-all-done), kind=kLoop, calls=%fused_computation.17 | loop fusion | flops 1966080 | bytes 2621440 | tf_op jit(solution)/shard_map/reduce_sum | solution.py:166
  177.2 4.1 %all-to-all-done.1 = f32[32,4,260]{2,1,0:T(4,128)S(1)} async-done(((f32[32,4,260]{2,1,0:T(4,128)}), f32[32,4,260]{2,1,0:T(4,128)S(1)}, u32[]{:S(2)}, u32[]{:S(2)}) %all-to-all-start.1) | async-done | bytes 133152 | tf_op jit(solution)/shard_map/all_to_all | solution.py:220
  182.3 1.0 mul.331
  183.8 2.2 %convolution_convert_fusion.1 = bf16[4,2048]{1,0:T(4,128)(2,1)} fusion(bf16[2048,256]{1,0:T(8,128)(2,1)} %bitcast.129, f32[1,4,2,128]{3,2,1,0:T(2,128)S(1)} %broadcast_bitcast_fusion, f32[1,4,2,128]{3,2,1,0:T(2,128)S(1)} %broadcast_bitcast_fusion.1, f32[4,256]{1,0:T(4,128)S(1)} %fusion.45, f32[1,4,2,128]{3,2,1,0:T(2,128)S(1)} %broadcast_bitcast_fusion.2, ...), kind=kOutput, calls=%fused_computation.24 | convolution fusion | flops 4208640 | bytes 1083396 | tf_op jit(solution)/shard_map/dot_general | solution.py:157
  186.0 6.1 %all-to-all-start.2 = ((bf16[8,4,256]{2,1,0:T(4,128)(2,1)}), bf16[8,4,256]{2,1,0:T(4,128)(2,1)S(1)}, u32[]{:S(2)}, u32[]{:S(2)}) async-start(bf16[8,4,256]{2,1,0:T(4,128)(2,1)} %bitcast.38), calls=%async_computation.2 | async-start | bytes 32768 | tf_op jit(solution)/shard_map/all_to_all | solution.py:163
  192.0 1.9 add_convert_fusion
  193.9 2.8 %all-to-all-done.2 = bf16[8,4,256]{2,1,0:T(4,128)(2,1)S(1)} async-done(((bf16[8,4,256]{2,1,0:T(4,128)(2,1)}), bf16[8,4,256]{2,1,0:T(4,128)(2,1)S(1)}, u32[]{:S(2)}, u32[]{:S(2)}) %all-to-all-start.2) | async-done | bytes 16416 | tf_op jit(solution)/shard_map/all_to_all | solution.py:163
  196.7 1.3 add_convert_fusion.5
  (120 shorter events, 20.0 us)
Async XLA Ops:
  7.2 136.3 %copy-start = (bf16[48,128,256]{2,1,0:T(8,128)(2,1)S(1)}, bf16[48,128,256]{2,1,0:T(8,128)(2,1)}, u32[]{:S(2)}) copy-start(bf16[48,128,256]{2,1,0:T(8,128)(2,1)} %param.27) | copy-start | bytes 9437188
  7.2 19.2 %copy-start.14 = (bf16[4,2048]{1,0:T(4,128)(2,1)S(1)}, bf16[4,2048]{1,0:T(4,128)(2,1)}, u32[]{:S(2)}) copy-start(bf16[4,2048]{1,0:T(4,128)(2,1)} %param.18) | copy-start | bytes 49156
  7.2 88.2 %all-gather.5.cloned.1.call-start = ((), (), s32[]{:S(2)}) async-start(), calls=%async_computation.3 | async-start | bytes 4718592 | tf_op jit(solution)/shard_map/all_gather | solution.py:85
  21.2 56.4 %copy-start.17 = (s32[128]{0:T(128)S(1)}, s32[128]{0:T(128)}, u32[]{:S(2)}) copy-start(s32[128]{0:T(128)} %param.29) | copy-start | bytes 1540
  21.2 56.8 %copy-start.15 = (s32[1536]{0:T(1024)S(1)}, s32[1536]{0:T(1024)}, u32[]{:S(2)}) copy-start(s32[1536]{0:T(1024)} %param.28) | copy-start | bytes 18436
  21.2 57.0 %copy-start.18 = (s32[128]{0:T(128)S(1)}, s32[128]{0:T(128)}, u32[]{:S(2)}) copy-start(s32[128]{0:T(128)} %param.30) | copy-start | bytes 1540
  21.9 58.1 %copy-start.20 = (s32[128]{0:T(128)S(1)}, s32[128]{0:T(128)}, u32[]{:S(2)}) copy-start(s32[128]{0:T(128)} %param.31) | copy-start | bytes 1540
  86.8 3.2 %copy-start.1 = (bf16[512,2048]{1,0:T(8,128)(2,1)S(1)}, bf16[512,2048]{1,0:T(8,128)(2,1)}, u32[]{:S(2)}) copy-start(bf16[512,2048]{1,0:T(8,128)(2,1)} %param.17) | copy-start | bytes 6291460
  104.2 2.8 %copy-start.5 = (bf16[512,2048]{1,0:T(8,128)(2,1)S(1)}, bf16[512,2048]{1,0:T(8,128)(2,1)}, u32[]{:S(2)}) copy-start(bf16[512,2048]{1,0:T(8,128)(2,1)} %fusion.6) | copy-start | bytes 6291460
  104.2 2.8 %copy-start.8 = (bf16[2048,256]{0,1:T(8,128)(2,1)S(1)}, bf16[2048,256]{0,1:T(8,128)(2,1)}, u32[]{:S(2)}) copy-start(bf16[2048,256]{0,1:T(8,128)(2,1)} %copy.84) | copy-start | bytes 3145732
  106.9 0.9 copy-start.10
  107.0 1.2 copy-start.4
  111.1 2.1 %copy-start.6 = (bf16[1,2048,256]{1,2,0:T(8,128)(2,1)S(1)}, bf16[1,2048,256]{1,2,0:T(8,128)(2,1)}, u32[]{:S(2)}) copy-start(bf16[1,2048,256]{1,2,0:T(8,128)(2,1)} %copy.86) | copy-start | bytes 3145732
  113.2 2.1 %copy-start.9 = (bf16[1,4,512,256]{3,2,1,0:T(8,128)(2,1)S(1)}, bf16[1,4,512,256]{3,2,1,0:T(8,128)(2,1)}, u32[]{:S(2)}) copy-start(bf16[1,4,512,256]{3,2,1,0:T(8,128)(2,1)} %get-tuple-element.19) | copy-start | bytes 3145732
  116.0 1.2 copy-start.2
  117.3 2.2 %copy-start.3 = (bf16[128,2048]{1,0:T(8,128)(2,1)S(1)}, bf16[128,2048]{1,0:T(8,128)(2,1)}, u32[]{:S(2)}) copy-start(bf16[128,2048]{1,0:T(8,128)(2,1)} %reshape.432) | copy-start | bytes 1572868
  118.0 2.4 %copy-start.7 = (bf16[2048,256]{0,1:T(8,128)(2,1)S(1)}, bf16[2048,256]{0,1:T(8,128)(2,1)}, u32[]{:S(2)}) copy-start(bf16[2048,256]{0,1:T(8,128)(2,1)} %copy.85) | copy-start | bytes 3145732
  119.5 1.5 copy-start.11
  119.5 1.6 copy-start.12
  119.6 1.5 copy-start.19
  119.9 1.2 copy-start.21
  120.5 18.3 %copy-start.16 = (pred[48]{0:T(512)(128)(4,1)S(1)}, pred[48]{0:T(512)(128)(4,1)}, u32[]{:S(2)}) copy-start(pred[48]{0:T(512)(128)(4,1)} %get-tuple-element.16) | copy-start | bytes 148
  122.0 19.8 %copy-start.13 = (pred[48,128]{1,0:T(8,128)(4,1)S(1)}, pred[48,128]{1,0:T(8,128)(4,1)}, u32[]{:S(2)}) copy-start(pred[48,128]{1,0:T(8,128)(4,1)} %iota_compare_fusion.2) | copy-start | bytes 18436
  122.0 43.1 %all-to-all-start = ((bf16[8,512,256]{2,1,0:T(8,128)(2,1)}), bf16[8,512,256]{2,1,0:T(8,128)(2,1)}, u32[]{:S(2)}, u32[]{:S(2)}) async-start(bf16[8,512,256]{2,1,0:T(8,128)(2,1)} %bitcast.131), calls=%async_computation | async-start | bytes 4194304 | tf_op jit(solution)/shard_map/all_to_all | solution.py:163
  165.8 15.5 %all-to-all-start.1 = ((f32[32,4,260]{2,1,0:T(4,128)}), f32[32,4,260]{2,1,0:T(4,128)S(1)}, u32[]{:S(2)}, u32[]{:S(2)}) async-start(f32[32,4,260]{2,1,0:T(4,128)} %reshape.363), calls=%async_computation.1 | async-start | bytes 393216 | tf_op jit(solution)/shard_map/all_to_all | solution.py:220
  186.0 10.7 %all-to-all-start.2 = ((bf16[8,4,256]{2,1,0:T(4,128)(2,1)}), bf16[8,4,256]{2,1,0:T(4,128)(2,1)S(1)}, u32[]{:S(2)}, u32[]{:S(2)}) async-start(bf16[8,4,256]{2,1,0:T(4,128)(2,1)} %bitcast.38), calls=%async_computation.2 | async-start | bytes 32768 | tf_op jit(solution)/shard_map/all_to_all | solution.py:163
Sparse Core Ops, SparseCore 0:
  21.3 61.9 all-gather.4

commit v9 on v5

--- a/solution.py
+++ b/solution.py
@@ -121,41 +121,51 @@
     group_values = group_values.reshape(group_rows, head_count, HEAD)
     stored_keys = prior_keys[0].reshape(prior_slots, head_count, HEAD)
     stored_values = prior_values[0].reshape(prior_slots, head_count, HEAD)
-    prior_scores = (
-        jnp.einsum("qhd,khd->hqk", group_queries, stored_keys, preferred_element_type=jnp.float32)
-        * score_scale
-    )
     prior_live = jnp.arange(prior_slots, dtype=jnp.int32) < prior_length[0]
-    prior_scores = jnp.where(prior_live[None, None, :], prior_scores, NEG_FILL)
-    group_scores = (
-        jnp.einsum("qhd,khd->hqk", group_queries, group_keys, preferred_element_type=jnp.float32)
-        * score_scale
-    )
-    causal = jnp.arange(group_rows)[None, :] <= jnp.arange(group_rows)[:, None]
-    group_scores = jnp.where(causal[None], group_scores, NEG_FILL)
-    row_top = jnp.maximum(
-        jnp.max(prior_scores, axis=2, keepdims=True), jnp.max(group_scores, axis=2, keepdims=True)
-    )
-    prior_weights = jnp.exp(prior_scores - row_top)
-    group_weights = jnp.exp(group_scores - row_top)
-    weight_total = jnp.sum(prior_weights, axis=2) + jnp.sum(group_weights, axis=2)
-    combined = jnp.einsum(
-        "hqk,khd->qhd",
-        prior_weights.astype(jnp.bfloat16),
-        stored_values,
-        preferred_element_type=jnp.float32,
-    )
-    combined = combined + jnp.einsum(
-        "hqk,khd->qhd",
-        group_weights.astype(jnp.bfloat16),
-        group_values,
-        preferred_element_type=jnp.float32,
-    )
-    prefill_attended = (
-        (combined / jnp.transpose(weight_total)[:, :, None])
-        .reshape(group_rows, local_width)
-        .astype(jnp.bfloat16)
-    )
+
+    def prefill_rows(start, count, row_queries):
+        row_queries = row_queries[start : start + count]
+        prior_scores = (
+            jnp.einsum(
+                "qhd,khd->hqk", row_queries, stored_keys, preferred_element_type=jnp.float32
+            )
+            * score_scale
+        )
+        prior_scores = jnp.where(prior_live[None, None, :], prior_scores, NEG_FILL)
+        group_scores = (
+            jnp.einsum(
+                "qhd,khd->hqk", row_queries, group_keys, preferred_element_type=jnp.float32
+            )
+            * score_scale
+        )
+        causal = (
+            jnp.arange(group_rows)[None, :] <= (start + jnp.arange(count))[:, None]
+        )
+        group_scores = jnp.where(causal[None], group_scores, NEG_FILL)
+        row_top = jnp.maximum(
+            jnp.max(prior_scores, axis=2, keepdims=True),
+            jnp.max(group_scores, axis=2, keepdims=True),
+        )
+        prior_weights = jnp.exp(prior_scores - row_top)
+        group_weights = jnp.exp(group_scores - row_top)
+        weight_total = jnp.sum(prior_weights, axis=2) + jnp.sum(group_weights, axis=2)
+        combined = jnp.einsum(
+            "hqk,khd->qhd",
+            prior_weights.astype(jnp.bfloat16),
+            stored_values,
+            preferred_element_type=jnp.float32,
+        )
+        combined = combined + jnp.einsum(
+            "hqk,khd->qhd",
+            group_weights.astype(jnp.bfloat16),
+            group_values,
+            preferred_element_type=jnp.float32,
+        )
+        return (
+            (combined / jnp.transpose(weight_total)[:, :, None])
+            .reshape(count, local_width)
+            .astype(jnp.bfloat16)
+        )
 
     model_size = out_columns.shape[0] // local_width
     column_start = model_index * local_width
@@ -174,10 +184,15 @@
         residual = lax.dynamic_slice_in_dim(own_tokens, column_start, local_width, 1)
         return (residual.astype(jnp.float32) + branch).astype(jnp.bfloat16)
 
-    prefill_shares, all_decode = lax.optimization_barrier(
-        (send_shares(prefill_attended), all_decode)
-    )
-    prefill_received = exchange(prefill_shares)
+    half = group_rows // 2
+    first_shares = send_shares(prefill_rows(0, half, group_queries))
+    first_received = exchange(first_shares)
+    first_shares, later_queries = lax.optimization_barrier((first_shares, group_queries))
+    second_shares = send_shares(prefill_rows(half, group_rows - half, later_queries))
+    second_shares, first_received, all_decode = lax.optimization_barrier(
+        (second_shares, first_received, all_decode)
+    )
+    second_received = exchange(second_shares)
     decode_q, decode_k, decode_v = project(all_decode)
     slot_queries = rotary(decode_q, decode_positions, HEAD).astype(jnp.bfloat16)
     slot_keys = rotary(decode_k, decode_positions, HEAD).astype(jnp.bfloat16)
@@ -223,7 +238,7 @@
         member_weights.T, page_mix.reshape(pool_local, local_width), precision=lax.Precision.HIGHEST
     )
     partials = jnp.concatenate([slot_top, slot_total, slot_mix], axis=1)
-    partials, prefill_received = lax.optimization_barrier((partials, prefill_received))
+    partials, second_received = lax.optimization_barrier((partials, second_received))
     received = lax.all_to_all(
         partials.reshape(dp_size, decode_rows, -1), DP, 0, 0, tiled=False
     )
@@ -254,7 +269,13 @@
     )
     decode_attended = rescale(final_mix, 1.0 / final_total, HEAD).astype(jnp.bfloat16)
     return (
-        mixed(prefill_received, prefill_tokens),
+        jnp.concatenate(
+            [
+                mixed(first_received, prefill_tokens[:half]),
+                mixed(second_received, prefill_tokens[half:]),
+            ],
+            axis=0,
+        ),
         mixed(exchange(send_shares(decode_attended)), decode_tokens),
     )
 

time: 206 us -> 213 us (1.034)
  waiting for transfers between devices: 71.8 us -> 65.5 us
  starting transfers between devices: 18.1 us -> 23.3 us
  other arithmetic: 21.9 us -> 25 us
  matrix products: 24.6 us -> 26.8 us
    all_to_all x2 -> x3, waiting for transfers between devices: 21.5 us -> 14.2 us  [exchange(): return lax.all_to_all(shares, 'fsdp', 0, 0, tiled=False)]
    all_to_all x2 -> x3, starting transfers between devices: 11.2 us -> 16.4 us  [exchange(): return lax.all_to_all(shares, 'fsdp', 0, 0, tiled=False)]
    all_to_all x1, waiting for transfers between devices: 4.09 us -> 6.43 us  [per_device(): lax.all_to_all(partials.reshape(dp_size, decode_rows, -1), DP, 0, 0, tile...]
    dot_general x4 -> x8, matrix products: 5.18 us -> 7.25 us  [the longest x2 3.2 us: prefill_rows(): jnp.einsum('qhd,khd->hqk', row_queries, stored_keys, preferred_element_ty...]
  transfers between devices with their start and end apart: 4 -> 5, of which waited for: 4 -> 5; matrix products, arithmetic and copies ran while one was open for 18% -> 22% of each run, Pallas kernels for 0% -> 0%
where the time goes in v9:
time: 213 us; the launch traced here: 211 us
  waiting for transfers between devices  65.5 us (31%)
  local copies, waits for them, and re-layouts  41.8 us (20%)
  matrix products  26.8 us (13%)
  other arithmetic  25 us (12%)
  starting transfers between devices  23.3 us (11%)
  between operations  15.3 us (7%)
  blocking collectives  13.3 us (6%)
    all_gather x1, waiting for transfers between devices, per_device(): lax.all_gather(across_y, 'dz', axis=2, tiled=False)  44.9 us
    all_to_all x3, starting transfers between devices, exchange(): return lax.all_to_all(shares, 'fsdp', 0, 0, tiled=False)  16.4 us
    all_to_all x3, waiting for transfers between devices, exchange(): return lax.all_to_all(shares, 'fsdp', 0, 0, tiled=False)  14.2 us
    all_gather x1, blocking collectives, per_device(): across_y = lax.all_gather(bundle, 'dy', axis=1, tiled=False)  13.3 us
    dot_general x6, matrix products, project(): jnp.dot(normed, weight, preferred_element_type=jnp.float32)  10.4 us
    all_to_all x1, starting transfers between devices, per_device(): lax.all_to_all(partials.reshape(dp_size, decode_rows, -1), DP, 0, 0, tile...  6.88 us
    slice x2, local copies, waits for them, and re-layouts, per_device(): gathered[4].reshape(dp_size, -1)[:, :decode_size]  6.77 us
    all_to_all x1, waiting for transfers between devices, per_device(): lax.all_to_all(partials.reshape(dp_size, decode_rows, -1), DP, 0, 0, tile...  6.43 us
  transfers between devices with their start and end apart: 5, of which 5 were waited for; matrix products, arithmetic and copies ran while one was open for 22% of the time, Pallas kernels for 0%

profile of v9, /device:TPU:1, one launch (start us, length us, event | category | flops | bytes accessed | tf_op | source)
XLA Modules:
  0.0 211.2 jit_solution(14976448088581696014)
XLA Ops:
  11.2 13.3 %all-gather = bf16[5,256,256]{2,1,0:T(8,128)(2,1)} all-gather(bf16[5,64,256]{2,1,0:T(8,128)(2,1)S(1)} %bitcast_dynamic-update-slice_fusion.1), channel_id=2, replica_groups=mesh['dy'=4,'dz'=8,'fsdp'=8] {'dy'}, dimensions={1}, use_global_device_ids=true | all-gather | bytes 819200 | tf_op jit(solution)/shard_map/all_gather | solution.py:88
  25.2 2.2 %reshape_squeeze.9 = bf16[2048,2,128]{2,1,0:T(2,128)(2,1)} reshape(bf16[1,2048,256]{2,1,0:T(8,128)(2,1)} %param.23) | data formatting | bytes 2097152 | tf_op jit(solution)/shard_map/reshape;squeeze | solution.py:122
  27.4 2.3 %copy.108 = bf16[1,2048,256]{1,2,0:T(8,128)(2,1)} copy(bf16[1,2048,256]{2,1,0:T(8,128)(2,1)} %param.24) | data formatting | bytes 2097152 | tf_op jit(solution)/shard_map/reshape;squeeze | solution.py:123
  34.2 4.7 %copy.106 = bf16[48,128,256]{1,2,0:T(8,128)(2,1)} copy(bf16[48,128,256]{2,1,0:T(8,128)(2,1)} %param.26) | data formatting | bytes 6291456 | tf_op jit(solution)/shard_map/reshape | solution.py:217
  39.7 2.0 convert_reduce_fusion
  41.7 2.3 %fusion.2 = f32[512]{0:T(512)S(1)} fusion(bf16[512,2048]{1,0:T(8,128)(2,1)} %param.17, f32[512]{0:T(512)S(1)} %broadcast_multiply_fusion), kind=kLoop, calls=%fused_computation.10 | loop fusion | flops 4193792 | bytes 2101248 | tf_op jit(solution)/shard_map/reduce_sum | solution.py:22
  47.1 1.9 fusion.3
  49.1 44.9 %all-gather.4.cloned.1.call-done = bf16[5,4,512,256]{3,2,1,0:T(8,128)(2,1)} async-done(((bf16[5,4,64,256]{3,2,1,0:T(8,128)(2,1)}), bf16[5,4,512,256]{3,2,1,0:T(8,128)(2,1)}) %all-gather.4.cloned.1.call-update) | async-done | bytes 5242896 | tf_op jit(solution)/shard_map/all_gather | solution.py:89
  93.9 4.9 %fusion.100 = (bf16[1,4,512,256]{3,2,1,0:T(8,128)(2,1)}, bf16[1,4,512,256]{3,2,1,0:T(8,128)(2,1)}, bf16[1,4,512,256]{3,2,1,0:T(8,128)(2,1)}, bf16[1,4,512,256]{3,2,1,0:T(8,128)(2,1)}, bf16[1,4,512,256]{3,2,1,0:T(8,128)(2,1)}) fusion(bf16[5,4,512,256]{3,2,1,0:T(8,128)(2,1)} %all-gather.4.cloned.1.call-done), kind=kLoop, calls=%fused_computation.194 | loop fusion | bytes 10485760 | tf_op jit(solution)/shard_map/slice | solution.py:96
  98.8 2.3 %copy.104 = bf16[2048,256]{0,1:T(8,128)(2,1)} copy(bf16[2048,256]{1,0:T(8,128)(2,1)} %bitcast.164) | data formatting | bytes 2097152 | tf_op jit(solution)/shard_map/squeeze | solution.py:92
  101.1 2.3 %copy.105 = bf16[2048,256]{0,1:T(8,128)(2,1)} copy(bf16[2048,256]{1,0:T(8,128)(2,1)} %bitcast.163) | data formatting | bytes 2097152 | tf_op jit(solution)/shard_map/squeeze | solution.py:92
  103.4 2.7 %fusion.15 = f32[512,2,128]{0,2,1:T(8,128)S(1)} fusion(bf16[2,128,2048]{2,1,0:T(8,128)(2,1)} %bitcast.174, bf16[512,2048]{1,0:T(8,128)(2,1)} %fusion.3), kind=kOutput, calls=%fused_computation.30 | convolution fusion | flops 536870912 | bytes 3670016 | tf_op jit(solution)/shard_map/dot_general | solution.py:102
  114.2 5.3 %all-to-all-start = ((bf16[8,256,256]{2,1,0:T(8,128)(2,1)}), bf16[8,256,256]{2,1,0:T(8,128)(2,1)}, u32[]{:S(2)}, u32[]{:S(2)}) async-start(bf16[8,256,256]{2,1,0:T(8,128)(2,1)} %bitcast.166), calls=%async_computation | async-start | bytes 2097152 | tf_op jit(solution)/shard_map/all_to_all | solution.py:180
  119.5 2.2 %fusion.5 = (f32[2,256]{1,0:T(2,128)S(1)}, f32[2,256,2048]{2,1,0:T(8,128)S(1)}) fusion(pred[2048]{0:T(1024)(128)(4,1)S(1)} %iota_compare_fusion.5, bf16[2048,2,128]{2,1,0:T(2,128)(2,1)} %reshape_squeeze.9, bf16[512,2,128]{0,2,1:T(8,128)(2,1)S(1)} %maximum_convert_fusion), kind=kOutput, calls=%fused_computation.17 | convolution fusion | flops 271580672 | bytes 5378048 | tf_op jit(solution)/shard_map/qhd,khd->hqk/dot_general | solution.py:129
  126.7 2.3 %reshape_squeeze.11 = bf16[32,16384]{1,0:T(8,128)(2,1)} reshape(bf16[1,4,512,256]{3,2,1,0:T(8,128)(2,1)} %get-tuple-element.22) | data formatting | bytes 2097152 | tf_op jit(solution)/shard_map/reshape;squeeze | solution.py:96
  129.0 1.9 slice.118
  130.9 2.2 %reshape.407 = bf16[128,2048]{1,0:T(8,128)(2,1)} reshape(bf16[32,8192]{1,0:T(8,128)(2,1)} %slice.118) | data formatting | bytes 1048576 | tf_op jit(solution)/shard_map/reshape | solution.py:96
  137.1 1.9 fusion.53
  139.0 1.9 fusion.51
  141.9 2.8 %fusion.69 = f32[48,2,1,128]{3,2,1,0:T(1,128)S(1)} fusion(bf16[48,128,2,128]{1,3,2,0:T(8,128)(2,1)} %bitcast.162, bf16[48,2,128,1]{2,1,0,3:T(2,128)(2,1)S(1)} %fusion.74), kind=kOutput, calls=%fused_computation.118 | convolution fusion | flops 3145728 | bytes 3219456 | tf_op jit(solution)/shard_map/phd,pkhd->phk/dot_general | solution.py:219
  146.0 2.5 %fusion.10 = f32[48,2,1,128]{3,2,1,0:T(1,128)S(1)} fusion(f32[48,2,128,1]{2,0,1,3:T(8,128)S(1)} %get-tuple-element.40, bf16[48,128,256]{2,1,0:T(8,128)(2,1)S(1)} %copy-done), kind=kOutput, calls=%fused_computation.22 | convolution fusion | flops 18874368 | bytes 3244032 | tf_op jit(solution)/shard_map/phk,pkhd->phd/dot_general | solution.py:234
  148.9 5.1 %all-to-all-start.1 = ((bf16[8,256,256]{2,1,0:T(8,128)(2,1)}), bf16[8,256,256]{2,1,0:T(8,128)(2,1)}, u32[]{:S(2)}, u32[]{:S(2)}) async-start(bf16[8,256,256]{2,1,0:T(8,128)(2,1)} %bitcast.165), calls=%async_computation.1 | async-start | bytes 2097152 | tf_op jit(solution)/shard_map/all_to_all | solution.py:180
  157.0 2.4 %fusion.95 = bf16[128,256]{1,0:T(8,128)(2,1)} fusion(bf16[2048,256]{1,0:T(8,128)(2,1)} %bitcast.170, bf16[128,2048]{1,0:T(8,128)(2,1)} %reshape.407, f32[128]{0:T(128)} %copy-done.22, f32[128]{0:T(128)S(1)} %broadcast_multiply_fusion.1), kind=kOutput, calls=%fused_computation.193 | convolution fusion | flops 135266304 | bytes 1639424 | tf_op jit(solution)/shard_map/dot_general | solution.py:102
  159.4 9.7 %all-to-all-done.1 = bf16[8,256,256]{2,1,0:T(8,128)(2,1)} async-done(((bf16[8,256,256]{2,1,0:T(8,128)(2,1)}), bf16[8,256,256]{2,1,0:T(8,128)(2,1)}, u32[]{:S(2)}, u32[]{:S(2)}) %all-to-all-start.1) | async-done | bytes 1048608 | tf_op jit(solution)/shard_map/all_to_all | solution.py:180
  169.8 6.9 %all-to-all-start.2 = ((f32[32,4,260]{2,1,0:T(4,128)}), f32[32,4,260]{2,1,0:T(4,128)S(1)}, u32[]{:S(2)}, u32[]{:S(2)}) async-start(f32[32,4,260]{2,1,0:T(4,128)} %reshape.413), calls=%async_computation.2 | async-start | bytes 393216 | tf_op jit(solution)/shard_map/all_to_all | solution.py:242
  178.1 1.6 add_convert_fusion
  179.7 6.4 %all-to-all-done.2 = f32[32,4,260]{2,1,0:T(4,128)S(1)} async-done(((f32[32,4,260]{2,1,0:T(4,128)}), f32[32,4,260]{2,1,0:T(4,128)S(1)}, u32[]{:S(2)}, u32[]{:S(2)}) %all-to-all-start.2) | async-done | bytes 133152 | tf_op jit(solution)/shard_map/all_to_all | solution.py:242
  187.1 1.7 mul.331
  190.1 2.2 %convolution_convert_fusion.2 = bf16[4,2048]{1,0:T(4,128)(2,1)} fusion(bf16[2048,256]{1,0:T(8,128)(2,1)} %bitcast.159, f32[1,4,2,128]{3,2,1,0:T(2,128)S(1)} %broadcast_bitcast_fusion, f32[1,4,2,128]{3,2,1,0:T(2,128)S(1)} %broadcast_bitcast_fusion.1, f32[4,256]{1,0:T(4,128)S(1)} %fusion.57, f32[1,4,2,128]{3,2,1,0:T(2,128)S(1)} %broadcast_bitcast_fusion.2, ...), kind=kOutput, calls=%fused_computation.27 | convolution fusion | flops 4208640 | bytes 1083396 | tf_op jit(solution)/shard_map/dot_general | solution.py:174
  192.3 6.1 %all-to-all-start.3 = ((bf16[8,4,256]{2,1,0:T(4,128)(2,1)}), bf16[8,4,256]{2,1,0:T(4,128)(2,1)S(1)}, u32[]{:S(2)}, u32[]{:S(2)}) async-start(bf16[8,4,256]{2,1,0:T(4,128)(2,1)} %bitcast.43), calls=%async_computation.3 | async-start | bytes 32768 | tf_op jit(solution)/shard_map/all_to_all | solution.py:180
  198.4 1.6 pad_maximum_fusion.1
  200.0 3.0 %all-to-all-done.3 = bf16[8,4,256]{2,1,0:T(4,128)(2,1)S(1)} async-done(((bf16[8,4,256]{2,1,0:T(4,128)(2,1)}), bf16[8,4,256]{2,1,0:T(4,128)(2,1)S(1)}, u32[]{:S(2)}, u32[]{:S(2)}) %all-to-all-start.3) | async-done | bytes 16416 | tf_op jit(solution)/shard_map/all_to_all | solution.py:180
  (148 shorter events, 40.4 us)
Async XLA Ops:
  7.2 138.8 %copy-start = (bf16[48,128,256]{2,1,0:T(8,128)(2,1)S(1)}, bf16[48,128,256]{2,1,0:T(8,128)(2,1)}, u32[]{:S(2)}) copy-start(bf16[48,128,256]{2,1,0:T(8,128)(2,1)} %param.27) | copy-start | bytes 9437188
  7.2 22.5 %copy-start.17 = (s32[128]{0:T(128)S(1)}, s32[128]{0:T(128)}, u32[]{:S(2)}) copy-start(s32[128]{0:T(128)} %param.29) | copy-start | bytes 1540
  7.2 22.9 %copy-start.16 = (s32[1536]{0:T(1024)S(1)}, s32[1536]{0:T(1024)}, u32[]{:S(2)}) copy-start(s32[1536]{0:T(1024)} %param.28) | copy-start | bytes 18436
  7.2 23.1 %copy-start.18 = (s32[128]{0:T(128)S(1)}, s32[128]{0:T(128)}, u32[]{:S(2)}) copy-start(s32[128]{0:T(128)} %param.30) | copy-start | bytes 1540
  7.2 24.8 %copy-start.19 = (s32[128]{0:T(128)S(1)}, s32[128]{0:T(128)}, u32[]{:S(2)}) copy-start(s32[128]{0:T(128)} %param.31) | copy-start | bytes 1540
  7.2 86.7 %all-gather.4.cloned.1.call-start = ((), (), s32[]{:S(2)}) async-start(), calls=%async_computation.4 | async-start | bytes 5898240 | tf_op jit(solution)/shard_map/all_gather | solution.py:89
  38.9 6.8 %copy-start.1 = (bf16[512,2048]{1,0:T(8,128)(2,1)S(1)}, bf16[512,2048]{1,0:T(8,128)(2,1)}, u32[]{:S(2)}) copy-start(bf16[512,2048]{1,0:T(8,128)(2,1)} %param.17) | copy-start | bytes 6291460
  103.4 2.8 %copy-start.5 = (bf16[512,2048]{1,0:T(8,128)(2,1)S(1)}, bf16[512,2048]{1,0:T(8,128)(2,1)}, u32[]{:S(2)}) copy-start(bf16[512,2048]{1,0:T(8,128)(2,1)} %fusion.3) | copy-start | bytes 6291460
  103.4 2.8 %copy-start.9 = (bf16[2048,256]{0,1:T(8,128)(2,1)S(1)}, bf16[2048,256]{0,1:T(8,128)(2,1)}, u32[]{:S(2)}) copy-start(bf16[2048,256]{0,1:T(8,128)(2,1)} %copy.105) | copy-start | bytes 3145732
  106.2 1.2 copy-start.4
  107.0 1.5 copy-start.11
  107.2 2.1 copy-start.12
  107.2 2.1 copy-start.14
  108.4 1.8 copy-start.7
  110.2 1.2 copy-start.6
  111.3 1.4 copy-start.2
  112.2 2.1 copy-start.20
  114.2 20.3 %all-to-all-start = ((bf16[8,256,256]{2,1,0:T(8,128)(2,1)}), bf16[8,256,256]{2,1,0:T(8,128)(2,1)}, u32[]{:S(2)}, u32[]{:S(2)}) async-start(bf16[8,256,256]{2,1,0:T(8,128)(2,1)} %bitcast.166), calls=%async_computation | async-start | bytes 2097152 | tf_op jit(solution)/shard_map/all_to_all | solution.py:180
  119.5 2.2 %copy-start.10 = (pred[256,512]{1,0:T(8,128)(4,1)S(1)}, pred[256,512]{1,0:T(8,128)(4,1)}, u32[]{:S(2)}) copy-start(pred[256,512]{1,0:T(8,128)(4,1)} %iota_compare_fusion) | copy-start | bytes 393220
  119.5 2.2 %copy-start.13 = (bf16[512,2,64]{0,2,1:T(8,128)(2,1)S(1)}, bf16[512,2,64]{0,2,1:T(8,128)(2,1)}, u32[]{:S(2)}) copy-start(bf16[512,2,64]{0,2,1:T(8,128)(2,1)} %copy-done.12) | copy-start | bytes 393220
  119.5 2.3 %copy-start.15 = (bf16[512,2,64]{0,2,1:T(8,128)(2,1)S(1)}, bf16[512,2,64]{0,2,1:T(8,128)(2,1)}, u32[]{:S(2)}) copy-start(bf16[512,2,64]{0,2,1:T(8,128)(2,1)} %copy-done.14) | copy-start | bytes 393220
  121.8 1.8 copy-start.8
  123.5 1.1 copy-start.21
  123.6 1.6 copy-start.3
  137.1 4.8 %copy-start.22 = (f32[128]{0:T(128)}, f32[128]{0:T(128)S(1)}, u32[]{:S(2)}) copy-start(f32[128]{0:T(128)S(1)} %add_rsqrt_fusion.1) | copy-start | bytes 1540
  148.9 20.2 %all-to-all-start.1 = ((bf16[8,256,256]{2,1,0:T(8,128)(2,1)}), bf16[8,256,256]{2,1,0:T(8,128)(2,1)}, u32[]{:S(2)}, u32[]{:S(2)}) async-start(bf16[8,256,256]{2,1,0:T(8,128)(2,1)} %bitcast.165), calls=%async_computation.1 | async-start | bytes 2097152 | tf_op jit(solution)/shard_map/all_to_all | solution.py:180
  169.8 16.3 %all-to-all-start.2 = ((f32[32,4,260]{2,1,0:T(4,128)}), f32[32,4,260]{2,1,0:T(4,128)S(1)}, u32[]{:S(2)}, u32[]{:S(2)}) async-start(f32[32,4,260]{2,1,0:T(4,128)} %reshape.413), calls=%async_computation.2 | async-start | bytes 393216 | tf_op jit(solution)/shard_map/all_to_all | solution.py:242
  192.3 10.7 %all-to-all-start.3 = ((bf16[8,4,256]{2,1,0:T(4,128)(2,1)}), bf16[8,4,256]{2,1,0:T(4,128)(2,1)S(1)}, u32[]{:S(2)}, u32[]{:S(2)}) async-start(bf16[8,4,256]{2,1,0:T(4,128)(2,1)} %bitcast.43), calls=%async_computation.3 | async-start | bytes 32768 | tf_op jit(solution)/shard_map/all_to_all | solution.py:180
Sparse Core Ops, SparseCore 0:
  24.7 69.2 all-gather.3

commit v10 on v5

--- a/solution.py
+++ b/solution.py
@@ -80,7 +80,7 @@
     data_index = lax.axis_index(DP)
     model_index = lax.axis_index("fsdp")
 
-    decode_piece = decode_tokens.reshape(-1, local_width)
+    decode_piece = layer_norm(decode_tokens).reshape(-1, local_width)
     decode_piece = jnp.pad(decode_piece, ((0, weight_rows - decode_piece.shape[0]), (0, 0)))
     bundle = jnp.stack(
         [query_weight, key_weight, value_weight, jnp.transpose(out_weight), decode_piece]
@@ -92,16 +92,18 @@
     projection_weights = [gathered[p] for p in range(3)]
     out_columns = gathered[3]
     decode_size = decode_tokens.size
-    all_decode = (
+    decode_normed = (
         gathered[4].reshape(dp_size, -1)[:, :decode_size].reshape(dp_size * decode_rows, -1)
     )
 
-    def project(rows_in):
-        normed = layer_norm(rows_in)
+    def project_normed(normed):
         return tuple(
             jnp.dot(normed, weight, preferred_element_type=jnp.float32)
             for weight in projection_weights
         )
+
+    def project(rows_in):
+        return project_normed(layer_norm(rows_in))
 
     cache_length = (page_counts - 1) * PAGE + last_fill
     first_page = jnp.cumsum(page_counts) - page_counts
@@ -174,11 +176,11 @@
         residual = lax.dynamic_slice_in_dim(own_tokens, column_start, local_width, 1)
         return (residual.astype(jnp.float32) + branch).astype(jnp.bfloat16)
 
-    prefill_shares, all_decode = lax.optimization_barrier(
-        (send_shares(prefill_attended), all_decode)
+    prefill_shares, decode_normed = lax.optimization_barrier(
+        (send_shares(prefill_attended), decode_normed)
     )
     prefill_received = exchange(prefill_shares)
-    decode_q, decode_k, decode_v = project(all_decode)
+    decode_q, decode_k, decode_v = project_normed(decode_normed)
     slot_queries = rotary(decode_q, decode_positions, HEAD).astype(jnp.bfloat16)
     slot_keys = rotary(decode_k, decode_positions, HEAD).astype(jnp.bfloat16)
     slot_values = decode_v.astype(jnp.bfloat16)

time: 206 us -> 205 us (level)
    unnamed x45 -> x41, local copies, waits for them, and re-layouts: 4.22 us -> 4.15 us
where the time goes in v10:
time: 205 us; the launch traced here: 204 us
  waiting for transfers between devices  71.9 us (35%)
  local copies, waits for them, and re-layouts  38.9 us (19%)
  matrix products  24.4 us (12%)
  other arithmetic  22.1 us (11%)
  starting transfers between devices  18.1 us (9%)
  between operations  15.1 us (7%)
  blocking collectives  13.3 us (6%)
    all_gather x1, waiting for transfers between devices, per_device(): lax.all_gather(across_y, 'dz', axis=2, tiled=False)  46.2 us
    all_to_all x2, waiting for transfers between devices, exchange(): return lax.all_to_all(shares, 'fsdp', 0, 0, tiled=False)  21.5 us
    all_gather x1, blocking collectives, per_device(): across_y = lax.all_gather(bundle, 'dy', axis=1, tiled=False)  13.3 us
    all_to_all x2, starting transfers between devices, exchange(): return lax.all_to_all(shares, 'fsdp', 0, 0, tiled=False)  11.2 us
    dot_general x6, matrix products, project_normed(): jnp.dot(normed, weight, preferred_element_type=jnp.float32)  10.2 us
    all_to_all x1, starting transfers between devices, per_device(): lax.all_to_all(partials.reshape(dp_size, decode_rows, -1), DP, 0, 0, tile...  6.87 us
    slice x2, local copies, waits for them, and re-layouts, per_device(): gathered[4].reshape(dp_size, -1)[:, :decode_size]  6.74 us
    reshape x1, local copies, waits for them, and re-layouts, per_device(): page_keys = pool_keys.reshape(pool_local, PAGE, head_count, HEAD)  4.67 us
  transfers between devices with their start and end apart: 4, of which 4 were waited for; matrix products, arithmetic and copies ran while one was open for 18% of the time, Pallas kernels for 0%

profile of v10, /device:TPU:1, one launch (start us, length us, event | category | flops | bytes accessed | tf_op | source)
XLA Modules:
  0.0 203.8 jit_solution(5401409382018397703)
XLA Ops:
  13.1 13.3 %all-gather = bf16[5,256,256]{2,1,0:T(8,128)(2,1)} all-gather(bf16[5,64,256]{2,1,0:T(8,128)(2,1)S(1)} %bitcast_dynamic-update-slice_fusion.1), channel_id=2, replica_groups=mesh['dy'=4,'dz'=8,'fsdp'=8] {'dy'}, dimensions={1}, use_global_device_ids=true | all-gather | bytes 819200 | tf_op jit(solution)/shard_map/all_gather | solution.py:88
  27.1 2.1 %reshape_squeeze.9 = bf16[2048,2,128]{2,1,0:T(2,128)(2,1)} reshape(bf16[1,2048,256]{2,1,0:T(8,128)(2,1)} %param.23) | data formatting | bytes 2097152 | tf_op jit(solution)/shard_map/reshape;squeeze | solution.py:124
  29.2 2.3 %copy.86 = bf16[1,2048,256]{1,2,0:T(8,128)(2,1)} copy(bf16[1,2048,256]{2,1,0:T(8,128)(2,1)} %param.24) | data formatting | bytes 2097152 | tf_op jit(solution)/shard_map/reshape;squeeze | solution.py:125
  36.1 4.7 %copy.87 = bf16[48,128,256]{1,2,0:T(8,128)(2,1)} copy(bf16[48,128,256]{2,1,0:T(8,128)(2,1)} %param.26) | data formatting | bytes 6291456 | tf_op jit(solution)/shard_map/reshape | solution.py:204
  42.0 2.1 %convert_reduce_fusion = f32[512]{0:T(512)S(1)} fusion(bf16[512,2048]{1,0:T(8,128)(2,1)} %param.17), kind=kLoop, calls=%fused_computation.12 | loop fusion | flops 2096640 | bytes 2099200 | tf_op jit(solution)/shard_map/reduce_sum | solution.py:20
  47.6 1.9 fusion.6
  49.5 46.2 %all-gather.4.cloned.1.call-done = bf16[5,4,512,256]{3,2,1,0:T(8,128)(2,1)} async-done(((bf16[5,4,64,256]{3,2,1,0:T(8,128)(2,1)}), bf16[5,4,512,256]{3,2,1,0:T(8,128)(2,1)}) %all-gather.4.cloned.1.call-update) | async-done | bytes 5242896 | tf_op jit(solution)/shard_map/all_gather | solution.py:89
  95.8 4.8 %fusion.80 = (bf16[1,4,512,256]{3,2,1,0:T(8,128)(2,1)}, bf16[1,4,512,256]{3,2,1,0:T(8,128)(2,1)}, bf16[1,4,512,256]{3,2,1,0:T(8,128)(2,1)}, bf16[1,4,512,256]{3,2,1,0:T(8,128)(2,1)}, bf16[1,4,512,256]{3,2,1,0:T(8,128)(2,1)}) fusion(bf16[5,4,512,256]{3,2,1,0:T(8,128)(2,1)} %all-gather.4.cloned.1.call-done), kind=kLoop, calls=%fused_computation.167 | loop fusion | bytes 10485760 | tf_op jit(solution)/shard_map/slice | solution.py:96
  100.6 2.3 %copy.85 = bf16[2048,256]{0,1:T(8,128)(2,1)} copy(bf16[2048,256]{1,0:T(8,128)(2,1)} %bitcast.144) | data formatting | bytes 2097152 | tf_op jit(solution)/shard_map/squeeze | solution.py:92
  102.9 2.3 %copy.84 = bf16[2048,256]{0,1:T(8,128)(2,1)} copy(bf16[2048,256]{1,0:T(8,128)(2,1)} %bitcast.143) | data formatting | bytes 2097152 | tf_op jit(solution)/shard_map/squeeze | solution.py:92
  105.2 2.8 %fusion.13 = f32[512,2,128]{0,2,1:T(8,128)S(1)} fusion(bf16[2,128,2048]{2,1,0:T(8,128)(2,1)} %bitcast.145, bf16[512,2048]{1,0:T(8,128)(2,1)} %fusion.6), kind=kOutput, calls=%fused_computation.26 | convolution fusion | flops 536870912 | bytes 3670016 | tf_op jit(solution)/shard_map/dot_general | solution.py:101
  109.3 1.7 fusion
  112.2 2.1 %fusion.1 = f32[2,512]{1,0:T(2,128)S(1)} fusion(f32[2,512,2048]{2,1,0:T(8,128)S(1)} %get-tuple-element.46, f32[2,512]{1,0:T(2,128)S(1)} %max.11, pred[2048]{0:T(1024)(128)(4,1)S(1)} %iota_compare_fusion.4), kind=kLoop, calls=%fused_computation.9 | loop fusion | flops 8387584 | bytes 8398848 | tf_op jit(solution)/shard_map/reduce_sum | solution.py:143
  114.3 2.1 %fusion.20 = f32[512,2,128]{0,2,1:T(8,128)S(1)} fusion(bf16[2048,2,128]{0,2,1:T(8,128)(2,1)S(1)} %bitcast.150, f32[2,512,2048]{2,1,0:T(8,128)S(1)} %get-tuple-element.46, f32[2,512]{1,0:T(2,128)S(1)} %max.11, pred[2048]{0:T(1024)(128)(4,1)S(1)} %iota_compare_fusion.4), kind=kOutput, calls=%fused_computation.35 | convolution fusion | flops 545259520 | bytes 9967616 | tf_op jit(solution)/shard_map/hqk,khd->qhd/dot_general | solution.py:144
  119.1 1.5 copy.125
  120.6 2.4 %reshape_squeeze.11 = bf16[32,16384]{1,0:T(8,128)(2,1)} reshape(bf16[1,4,512,256]{3,2,1,0:T(8,128)(2,1)} %get-tuple-element.18) | data formatting | bytes 2097152 | tf_op jit(solution)/shard_map/reshape;squeeze | solution.py:96
  122.9 1.9 slice.99
  124.9 2.2 %reshape.369 = bf16[128,2048]{1,0:T(8,128)(2,1)} reshape(bf16[32,8192]{1,0:T(8,128)(2,1)} %slice.99) | data formatting | bytes 1048576 | tf_op jit(solution)/shard_map/reshape | solution.py:96
  127.1 1.8 fusion.35
  128.9 1.8 fusion.33
  131.8 5.1 %all-to-all-start = ((bf16[8,512,256]{2,1,0:T(8,128)(2,1)}), bf16[8,512,256]{2,1,0:T(8,128)(2,1)}, u32[]{:S(2)}, u32[]{:S(2)}) async-start(bf16[8,512,256]{2,1,0:T(8,128)(2,1)} %bitcast.139), calls=%async_computation | async-start | bytes 4194304 | tf_op jit(solution)/shard_map/all_to_all | solution.py:172
  137.0 2.8 %fusion.49 = f32[48,2,1,128]{3,2,1,0:T(1,128)S(1)} fusion(bf16[48,128,2,128]{1,3,2,0:T(8,128)(2,1)} %bitcast.136, bf16[48,2,128,1]{2,1,0,3:T(2,128)(2,1)S(1)} %fusion.58), kind=kOutput, calls=%fused_computation.88 | convolution fusion | flops 3145728 | bytes 3219456 | tf_op jit(solution)/shard_map/phd,pkhd->phk/dot_general | solution.py:206
  141.5 2.5 %fusion.10 = f32[48,2,1,128]{3,2,1,0:T(1,128)S(1)} fusion(f32[48,2,128,1]{2,0,1,3:T(8,128)S(1)} %get-tuple-element.36, bf16[48,128,256]{2,1,0:T(8,128)(2,1)S(1)} %copy-done), kind=kOutput, calls=%fused_computation.20 | convolution fusion | flops 18874368 | bytes 3244032 | tf_op jit(solution)/shard_map/phk,pkhd->phd/dot_general | solution.py:221
  144.6 18.7 %all-to-all-done = bf16[8,512,256]{2,1,0:T(8,128)(2,1)} async-done(((bf16[8,512,256]{2,1,0:T(8,128)(2,1)}), bf16[8,512,256]{2,1,0:T(8,128)(2,1)}, u32[]{:S(2)}, u32[]{:S(2)}) %all-to-all-start) | async-done | bytes 2097184 | tf_op jit(solution)/shard_map/all_to_all | solution.py:172
  164.0 6.9 %all-to-all-start.1 = ((f32[32,4,260]{2,1,0:T(4,128)}), f32[32,4,260]{2,1,0:T(4,128)S(1)}, u32[]{:S(2)}, u32[]{:S(2)}) async-start(f32[32,4,260]{2,1,0:T(4,128)} %reshape.373), calls=%async_computation.1 | async-start | bytes 393216 | tf_op jit(solution)/shard_map/all_to_all | solution.py:229
  170.8 2.3 %fusion.82 = bf16[128,256]{1,0:T(8,128)(2,1)} fusion(bf16[128,2048]{1,0:T(8,128)(2,1)} %reshape.369, bf16[2048,256]{1,0:T(8,128)(2,1)} %bitcast.141), kind=kOutput, calls=%fused_computation.169 | convolution fusion | flops 134217728 | bytes 1638400 | tf_op jit(solution)/shard_map/dot_general | solution.py:101
  173.4 2.7 %convert_reduce_fusion.1 = f32[512,256]{1,0:T(8,128)} fusion(bf16[8,512,256]{2,1,0:T(8,128)(2,1)} %all-to-all-done), kind=kLoop, calls=%fused_computation.17 | loop fusion | flops 1966080 | bytes 2621440 | tf_op jit(solution)/shard_map/reduce_sum | solution.py:175
  176.1 4.1 %all-to-all-done.1 = f32[32,4,260]{2,1,0:T(4,128)S(1)} async-done(((f32[32,4,260]{2,1,0:T(4,128)}), f32[32,4,260]{2,1,0:T(4,128)S(1)}, u32[]{:S(2)}, u32[]{:S(2)}) %all-to-all-start.1) | async-done | bytes 133152 | tf_op jit(solution)/shard_map/all_to_all | solution.py:229
  182.7 2.2 %convolution_convert_fusion.1 = bf16[4,2048]{1,0:T(4,128)(2,1)} fusion(bf16[2048,256]{1,0:T(8,128)(2,1)} %bitcast.137, f32[1,4,2,128]{3,2,1,0:T(2,128)S(1)} %broadcast_bitcast_fusion, f32[1,4,2,128]{3,2,1,0:T(2,128)S(1)} %broadcast_bitcast_fusion.1, f32[4,256]{1,0:T(4,128)S(1)} %fusion.41, f32[1,4,2,128]{3,2,1,0:T(2,128)S(1)} %broadcast_bitcast_fusion.2, ...), kind=kOutput, calls=%fused_computation.24 | convolution fusion | flops 4208640 | bytes 1083396 | tf_op jit(solution)/shard_map/dot_general | solution.py:166
  184.9 6.1 %all-to-all-start.2 = ((bf16[8,4,256]{2,1,0:T(4,128)(2,1)}), bf16[8,4,256]{2,1,0:T(4,128)(2,1)S(1)}, u32[]{:S(2)}, u32[]{:S(2)}) async-start(bf16[8,4,256]{2,1,0:T(4,128)(2,1)} %bitcast.38), calls=%async_computation.2 | async-start | bytes 32768 | tf_op jit(solution)/shard_map/all_to_all | solution.py:172
  191.0 1.9 add_convert_fusion
  192.9 2.8 %all-to-all-done.2 = bf16[8,4,256]{2,1,0:T(4,128)(2,1)S(1)} async-done(((bf16[8,4,256]{2,1,0:T(4,128)(2,1)}), bf16[8,4,256]{2,1,0:T(4,128)(2,1)S(1)}, u32[]{:S(2)}, u32[]{:S(2)}) %all-to-all-start.2) | async-done | bytes 16416 | tf_op jit(solution)/shard_map/all_to_all | solution.py:172
  (117 shorter events, 28.1 us)
Async XLA Ops:
  7.2 134.4 %copy-start = (bf16[48,128,256]{2,1,0:T(8,128)(2,1)S(1)}, bf16[48,128,256]{2,1,0:T(8,128)(2,1)}, u32[]{:S(2)}) copy-start(bf16[48,128,256]{2,1,0:T(8,128)(2,1)} %param.27) | copy-start | bytes 9437188
  7.2 24.3 %copy-start.14 = (s32[128]{0:T(128)S(1)}, s32[128]{0:T(128)}, u32[]{:S(2)}) copy-start(s32[128]{0:T(128)} %param.29) | copy-start | bytes 1540
  7.2 88.6 %all-gather.4.cloned.1.call-start = ((), (), s32[]{:S(2)}) async-start(), calls=%async_computation.3 | async-start | bytes 5898240 | tf_op jit(solution)/shard_map/all_gather | solution.py:89
  10.0 21.9 %copy-start.12 = (s32[1536]{0:T(1024)S(1)}, s32[1536]{0:T(1024)}, u32[]{:S(2)}) copy-start(s32[1536]{0:T(1024)} %param.28) | copy-start | bytes 18436
  10.0 22.1 %copy-start.15 = (s32[128]{0:T(128)S(1)}, s32[128]{0:T(128)}, u32[]{:S(2)}) copy-start(s32[128]{0:T(128)} %param.30) | copy-start | bytes 1540
  26.4 7.5 %copy-start.16 = (s32[128]{0:T(128)S(1)}, s32[128]{0:T(128)}, u32[]{:S(2)}) copy-start(s32[128]{0:T(128)} %param.31) | copy-start | bytes 1540
  40.7 3.4 %copy-start.1 = (bf16[512,2048]{1,0:T(8,128)(2,1)S(1)}, bf16[512,2048]{1,0:T(8,128)(2,1)}, u32[]{:S(2)}) copy-start(bf16[512,2048]{1,0:T(8,128)(2,1)} %param.17) | copy-start | bytes 6291460
  105.2 2.8 %copy-start.4 = (bf16[2048,256]{0,1:T(8,128)(2,1)S(1)}, bf16[2048,256]{0,1:T(8,128)(2,1)}, u32[]{:S(2)}) copy-start(bf16[2048,256]{0,1:T(8,128)(2,1)} %copy.84) | copy-start | bytes 3145732
  105.2 2.9 %copy-start.6 = (bf16[512,2048]{1,0:T(8,128)(2,1)S(1)}, bf16[512,2048]{1,0:T(8,128)(2,1)}, u32[]{:S(2)}) copy-start(bf16[512,2048]{1,0:T(8,128)(2,1)} %fusion.6) | copy-start | bytes 6291460
  107.9 0.9 copy-start.8
  108.0 1.2 copy-start.5
  112.2 2.1 %copy-start.7 = (bf16[1,2048,256]{1,2,0:T(8,128)(2,1)S(1)}, bf16[1,2048,256]{1,2,0:T(8,128)(2,1)}, u32[]{:S(2)}) copy-start(bf16[1,2048,256]{1,2,0:T(8,128)(2,1)} %copy.86) | copy-start | bytes 3145732
  114.3 2.1 %copy-start.3 = (bf16[1,4,512,256]{3,2,1,0:T(8,128)(2,1)S(1)}, bf16[1,4,512,256]{3,2,1,0:T(8,128)(2,1)}, u32[]{:S(2)}) copy-start(bf16[1,4,512,256]{3,2,1,0:T(8,128)(2,1)} %get-tuple-element.20) | copy-start | bytes 3145732
  117.1 1.2 copy-start.2
  122.9 7.8 %copy-start.9 = (f32[128,64]{0,1:T(8,128)S(1)}, f32[128,64]{0,1:T(8,128)}, u32[]{:S(2)}) copy-start(f32[128,64]{0,1:T(8,128)} %get-tuple-element.39) | copy-start | bytes 98308
  122.9 7.9 %copy-start.10 = (f32[128,64]{0,1:T(8,128)S(1)}, f32[128,64]{0,1:T(8,128)}, u32[]{:S(2)}) copy-start(f32[128,64]{0,1:T(8,128)} %get-tuple-element.40) | copy-start | bytes 98308
  128.9 8.0 %copy-start.13 = (pred[48]{0:T(512)(128)(4,1)S(1)}, pred[48]{0:T(512)(128)(4,1)}, u32[]{:S(2)}) copy-start(pred[48]{0:T(512)(128)(4,1)} %get-tuple-element.16) | copy-start | bytes 148
  131.8 8.2 %copy-start.11 = (pred[48,128]{1,0:T(8,128)(4,1)S(1)}, pred[48,128]{1,0:T(8,128)(4,1)}, u32[]{:S(2)}) copy-start(pred[48,128]{1,0:T(8,128)(4,1)} %iota_compare_fusion.2) | copy-start | bytes 18436
  131.8 31.4 %all-to-all-start = ((bf16[8,512,256]{2,1,0:T(8,128)(2,1)}), bf16[8,512,256]{2,1,0:T(8,128)(2,1)}, u32[]{:S(2)}, u32[]{:S(2)}) async-start(bf16[8,512,256]{2,1,0:T(8,128)(2,1)} %bitcast.139), calls=%async_computation | async-start | bytes 4194304 | tf_op jit(solution)/shard_map/all_to_all | solution.py:172
  164.0 16.3 %all-to-all-start.1 = ((f32[32,4,260]{2,1,0:T(4,128)}), f32[32,4,260]{2,1,0:T(4,128)S(1)}, u32[]{:S(2)}, u32[]{:S(2)}) async-start(f32[32,4,260]{2,1,0:T(4,128)} %reshape.373), calls=%async_computation.1 | async-start | bytes 393216 | tf_op jit(solution)/shard_map/all_to_all | solution.py:229
  184.9 10.8 %all-to-all-start.2 = ((bf16[8,4,256]{2,1,0:T(4,128)(2,1)}), bf16[8,4,256]{2,1,0:T(4,128)(2,1)S(1)}, u32[]{:S(2)}, u32[]{:S(2)}) async-start(bf16[8,4,256]{2,1,0:T(4,128)(2,1)} %bitcast.38), calls=%async_computation.2 | async-start | bytes 32768 | tf_op jit(solution)/shard_map/all_to_all | solution.py:172
Sparse Core Ops, SparseCore 0:
  26.5 69.2 all-gather.3
